TPU v7x, 512 devices: a whole 4x8x8 slice. The times are simulated.
512 devices in a mesh: gx: 8 (over z_lo, x), gy: 16 (over y, core), gz: 4 (over z_hi).
Axes of the slice: x: 4, y: 8, z: 8 (z_hi: 4, z_lo: 2; z = z_hi * 2 + z_lo), core: 2. Of those that a mesh axis runs over, the one named last changes fastest.
Arguments:
- positions: float32 [3, 262144], P(None, ('gx', 'gy', 'gz')), may hold values from 0 to 1
- velocities: float32 [3, 262144], P(None, ('gx', 'gy', 'gz')), may hold values from -5 to 5
- neighbour_index: int32 [24, 262144], P(None, ('gx', 'gy', 'gz')), may hold values from 0 to 3967, as said below
- neighbour_count: int32 [262144], P(('gx', 'gy', 'gz')), may hold values from 0 to 24, as said below
- ghost_list: int32 [65536], P(('gx', 'gy', 'gz')), may hold values from 0 to 511, as said below
- brick_count: int32 [512], P(('gx', 'gy', 'gz')), may hold values from 128 to 512, as said below
- atom_cell: int32 [262144], P(('gx', 'gy', 'gz')), may hold values from 0 to 127
- radial_weight: float32 [16, 8], replicated, may hold values from -2 to 2
- linear_weight: float32 [16], replicated, may hold values from -4 to 4
- pair_coupling: float32 [4, 16, 16], replicated, may hold values from -0.375 to 0.375
- electron_temp: float32 [16, 64, 64], P('gz', 'gy', 'gx'), may hold values from 1 to 2
- conductivity: float32 [16, 64, 64], P('gz', 'gy', 'gx'), may hold values from 0.3 to 1
- heating: float32 [16, 64, 64], P('gz', 'gy', 'gx'), may hold values from 0.05 to 1
Outputs:
- forces: float32 [3, 262144], P(None, ('gx', 'gy', 'gz'))
- new_velocity: float32 [3, 262144], P(None, ('gx', 'gy', 'gz'))
- new_electron_temp: float32 [16, 64, 64], P('gz', 'gy', 'gx')
- totals: float32 [10], replicated
Inputs may be any that keep to these rules, and one draw needn't show every extreme that they name: `brick_count`: bricks with b % 4 == 3 are full. `ghost_list`: entries of brick b name live atoms of brick b. `neighbour_count`: zero for atoms that are not live, at least 12 for live ones. `neighbour_index`: A used entry below 512 names a live atom of the same brick; otherwise it is 512 + s * 128 + g with slot s != 13, and never a slot whose depth offset crosses the film's surface (o2 = -1 in bricks with bz = 0, o2 = 1 in bricks with bz = 3).
All inputs are finite; a program needn't handle non-finite values.
Results may differ from a plain program's by a relative error of at most 0.0003.
Values sent between devices are 32-bit elements; how exact they have to be, the bound alone decides.
No kernel may reach another device: no remote copies, remote signals or barrier semaphores. Data moves between devices by JAX's collectives and lax.ppermute only.
A program may use at most 64 MiB of HBM per device.

v0:
```python
import functools

import jax
import jax.numpy as jnp
from jax import lax
from jax.experimental import pallas as pl
from jax.experimental.pallas import tpu as pltpu
from jax.sharding import Mesh
from jax.sharding import PartitionSpec as P

SUBSTEPS = 4
GX_GY_GZ = ("gx_0", "gx_1", "gy_0", "gy_1", "gz")
GX = ("gx_0", "gx_1")
GY = ("gy_0", "gy_1")


HEAT_STEP = 0.15
COUPLE = 0.5
RELAX = 0.2
KICK = 0.05
SPREAD = 2.0
ROOT_THREE = 1.7320508


def padded(cells, sides, width):
    for axis, dim in sides:
        count = lax.axis_size(axis)
        head = lax.slice_in_dim(cells, 0, width, axis=dim)
        tail = lax.slice_in_dim(cells, cells.shape[dim] - width, cells.shape[dim], axis=dim)
        cells = jnp.concatenate(
            [
                lax.ppermute(tail, axis, [(i, (i + 1) % count) for i in range(count)]),
                cells,
                lax.ppermute(head, axis, [((i + 1) % count, i) for i in range(count)]),
            ],
            axis=dim,
        )
    return cells


def by_axis(shard, axes):
    return functools.reduce(lax.psum, axes, shard)


def group_sum(values, axes):
    count = lax.axis_size(axes)
    here = lax.axis_index(axes)
    received = [values] + [
        lax.ppermute(values, axes, [(j, (j - shift) % count) for j in range(count)])
        for shift in range(1, count)
    ]
    ordered = jnp.roll(jnp.stack(received), here, axis=0)
    return jnp.sum(ordered, axis=0)


def row_gather(table_rows, flat_index, chunk=1024):
    rows, width = table_rows.shape
    total = flat_index.shape[0]

    def kernel(index_ref, table_ref, out_ref, stage_ref):
        base = pl.program_id(0) * chunk

        def copy_rows(group, carry):
            first = pl.multiple_of(group * 8, 8)
            picked = [
                table_ref[pl.ds(index_ref[base + first + r], 1), :] for r in range(8)
            ]
            stage_ref[pl.ds(first, 8), :] = jnp.concatenate(picked, axis=0)
            return carry

        lax.fori_loop(0, chunk // 8, copy_rows, 0, unroll=4)
        for part in range(chunk // 128):
            out_ref[:, part * 128 : (part + 1) * 128] = stage_ref[
                part * 128 : (part + 1) * 128, :
            ].T

    return pl.pallas_call(
        kernel,
        out_shape=jax.ShapeDtypeStruct((width, total), table_rows.dtype),
        grid_spec=pltpu.PrefetchScalarGridSpec(
            num_scalar_prefetch=1,
            grid=(total // chunk,),
            in_specs=[pl.BlockSpec((rows, width), lambda i, index: (0, 0))],
            out_specs=pl.BlockSpec((width, chunk), lambda i, index: (0, i)),
            scratch_shapes=[pltpu.VMEM((chunk, width), table_rows.dtype)],
        ),
        cost_estimate=pl.CostEstimate(
            flops=0, transcendentals=0, bytes_accessed=4 * (rows * width + 2 * width * total)
        ),
    )(flat_index, table_rows)


def column_gather(table, index):
    rows, width = table.shape
    lanes = 128
    blocks = -(-width // lanes)
    padded_table = jnp.pad(table, ((0, 0), (0, blocks * lanes - width)))
    flat = index.reshape(-1)
    high = flat // lanes
    low = flat % lanes
    picks = (jnp.arange(lanes)[:, None] == low[None, :]).astype(jnp.float32)
    spread = jnp.dot(
        padded_table.reshape(rows * blocks, lanes), picks, precision=lax.Precision.HIGHEST
    ).reshape(rows, blocks, flat.shape[0])
    chosen = jnp.arange(blocks)[:, None] == high[None, :]
    gathered = jnp.sum(jnp.where(chosen[None], spread, 0.0), axis=1)
    return gathered.reshape((rows,) + index.shape)


def harmonics(vector):
    coord_x, coord_y, coord_z = (vector[0], vector[1], vector[2])
    radius_sq = coord_x * coord_x + coord_y * coord_y + coord_z * coord_z
    terms = [
        jnp.ones_like(coord_x),
        coord_x,
        coord_y,
        coord_z,
        ROOT_THREE * coord_x * coord_y,
        ROOT_THREE * coord_y * coord_z,
        0.5 * (3.0 * coord_z * coord_z - radius_sq),
        ROOT_THREE * coord_x * coord_z,
        0.5 * ROOT_THREE * (coord_x * coord_x - coord_y * coord_y),
        0.79 * coord_y * (3.0 * coord_x * coord_x - coord_y * coord_y),
        3.87 * coord_x * coord_y * coord_z,
        0.61 * coord_y * (4.0 * coord_z * coord_z - coord_x * coord_x - coord_y * coord_y),
        0.5
        * coord_z
        * (2.0 * coord_z * coord_z - 3.0 * coord_x * coord_x - 3.0 * coord_y * coord_y),
        0.61 * coord_x * (4.0 * coord_z * coord_z - coord_x * coord_x - coord_y * coord_y),
        1.94 * coord_z * (coord_x * coord_x - coord_y * coord_y),
        0.79 * coord_x * (coord_x * coord_x - 3.0 * coord_y * coord_y),
    ]
    return jnp.stack(terms)


def radial(vector, orders):
    radius_sq = jnp.sum(vector * vector, axis=0)
    decay = jnp.exp(-radius_sq / SPREAD)
    argument = 2.0 * decay - 1.0
    polys = [jnp.ones_like(argument), argument]
    for order_id in range(2, orders):
        polys.append(2.0 * argument * polys[-1] - polys[-2])
    return decay * jnp.stack(polys[:orders])


def pair_energy(vector, weights):
    basis = radial(vector, weights.shape[0])
    mixed = jnp.sum(weights * basis[:, None], axis=0)
    return jnp.sum(mixed * harmonics(vector), axis=0)


def atom_basis(separation, pair_mask, radial_weight):
    basis = radial(separation, radial_weight.shape[1])
    shaped = jnp.sum(radial_weight[:, :, None, None] * basis[None], axis=1) * pair_mask
    return jnp.sum(shaped[:, None] * harmonics(separation)[None], axis=2)


def adjoints(basis_sum, linear_weight, pair_coupling):
    per_harmonic = jnp.concatenate(
        [
            jnp.repeat(pair_coupling[degree_id : degree_id + 1], copies, axis=0)
            for degree_id, copies in enumerate((1, 3, 5, 7))
        ],
        axis=0,
    )
    by_harmonic = jnp.transpose(basis_sum, (1, 0, 2))
    forward = jnp.sum(
        jnp.transpose(per_harmonic, (1, 0, 2))[:, :, :, None] * by_harmonic[None], axis=2
    )
    backward = jnp.sum(
        jnp.transpose(per_harmonic, (2, 0, 1))[:, :, :, None] * by_harmonic[None], axis=2
    )
    energy = jnp.dot(linear_weight, basis_sum[:, 0, :], precision=lax.Precision.HIGHEST) + jnp.sum(
        basis_sum * forward, axis=(0, 1)
    )
    isotropic = (jnp.arange(basis_sum.shape[1]) == 0).astype(jnp.float32)
    adjoint = forward + backward + linear_weight[:, None, None] * isotropic[None, :, None]
    return (energy, adjoint)


def pair_forces(separation, pair_mask, own_weights, other_weights):
    own_grad = jax.grad(lambda vector: jnp.sum(pair_energy(vector, own_weights)))(separation)
    other_grad = jax.grad(lambda vector: jnp.sum(pair_energy(vector, other_weights)))(-separation)
    pieces = (own_grad - other_grad) * pair_mask
    return (
        jnp.sum(pieces, axis=1),
        jnp.einsum("aki,bki->ab", separation, pieces, precision=lax.Precision.HIGHEST),
    )


def substep(temp_ext, kappa_ext, heat_here, lattice_here, occupancy_here, lower_open, upper_open):
    centre = temp_ext[1:-1, 1:-1, 1:-1]
    centre_kappa = kappa_ext[1:-1, 1:-1, 1:-1]

    def face(beside_temp, beside_kappa):
        return 0.5 * (centre_kappa + beside_kappa) * (beside_temp - centre)

    divergence = (
        face(temp_ext[1:-1, 1:-1, 2:], kappa_ext[1:-1, 1:-1, 2:])
        + face(temp_ext[1:-1, 1:-1, :-2], kappa_ext[1:-1, 1:-1, :-2])
        + face(temp_ext[1:-1, 2:, 1:-1], kappa_ext[1:-1, 2:, 1:-1])
        + face(temp_ext[1:-1, :-2, 1:-1], kappa_ext[1:-1, :-2, 1:-1])
        + face(temp_ext[2:, 1:-1, 1:-1], kappa_ext[2:, 1:-1, 1:-1]) * upper_open
        + face(temp_ext[:-2, 1:-1, 1:-1], kappa_ext[:-2, 1:-1, 1:-1]) * lower_open
    )
    return centre + HEAT_STEP / centre * (
        divergence + heat_here - COUPLE * occupancy_here * (centre - lattice_here)
    )


def local(
    positions,
    velocities,
    neighbour_index,
    neighbour_count,
    ghost_list,
    brick_count,
    atom_cell,
    radial_weight,
    linear_weight,
    pair_coupling,
    electron_temp,
    conductivity,
    heating,
):
    atom_slots = positions.shape[1]
    ghosts = ghost_list.shape[0]
    neigh_depth = neighbour_index.shape[0]
    orders = radial_weight.shape[1]
    live_count = brick_count[0]
    alive_mask = (jnp.arange(atom_slots) < live_count).astype(jnp.float32)
    slot_ids = jnp.arange(27)
    offsets = jnp.stack(
        [slot_ids // 9 - 1, slot_ids // 3 % 3 - 1, slot_ids % 3 - 1], axis=1
    ).astype(jnp.float32)
    ghost_sent = jnp.take(positions, ghost_list, axis=1).reshape(1, 1, 1, 3, ghosts)
    framed = padded(ghost_sent, (("gz", 2), (GX, 0), (GY, 1)), 1)
    shifted = framed.reshape(27, 3, ghosts) + offsets[:, :, None]
    pos_table = jnp.concatenate(
        [positions, jnp.transpose(shifted, (1, 0, 2)).reshape(3, 27 * ghosts)], axis=1
    )
    separation = column_gather(pos_table, neighbour_index) - positions[:, None, :]
    pair_mask = (jnp.arange(neigh_depth)[:, None] < neighbour_count[None, :]).astype(jnp.float32)
    basis_sum = atom_basis(separation, pair_mask, radial_weight)
    energy, adjoint = adjoints(basis_sum, linear_weight, pair_coupling)
    reduced = jnp.sum(radial_weight.T[:, :, None, None] * adjoint[None], axis=1)
    own_table = reduced.reshape(orders * 16, atom_slots)
    picked = jnp.take(own_table, ghost_list, axis=1).reshape(1, 1, 1, orders * 16, ghosts)
    framed_adjoint = padded(picked, (("gz", 2), (GX, 0), (GY, 1)), 1)
    remote = framed_adjoint.reshape(27, orders * 16, ghosts)
    table_rows = jnp.concatenate(
        [own_table.T, jnp.transpose(remote, (0, 2, 1)).reshape(27 * ghosts, orders * 16)], axis=0
    )
    other_weights = row_gather(table_rows, neighbour_index.reshape(-1)).reshape(
        orders, 16, neigh_depth, atom_slots
    )
    forces, virial = pair_forces(
        separation, pair_mask, own_table.reshape(orders, 16, 1, atom_slots), other_weights
    )
    kicked = velocities + KICK * forces
    grid_shape = electron_temp.shape
    cell_total = grid_shape[0] * grid_shape[1] * grid_shape[2]
    cell_picks = (jnp.arange(cell_total)[:, None] == atom_cell[None, :]).astype(jnp.float32)
    per_cell = jnp.dot(
        cell_picks,
        jnp.stack([alive_mask * jnp.sum(kicked * kicked, axis=0), alive_mask], axis=1),
        precision=lax.Precision.HIGHEST,
    )
    kinetic = per_cell[:, 0]
    filled = per_cell[:, 1]
    lattice = (kinetic / (3.0 * jnp.maximum(filled, 1.0))).reshape(grid_shape)
    occupancy = jnp.minimum(filled, 1.0).reshape(grid_shape)
    depth_index = lax.axis_index("gz")
    depth_total = grid_shape[0] * lax.axis_size("gz")
    stacked = jnp.stack([electron_temp, conductivity, heating, lattice, occupancy])
    margins = padded(stacked, (("gz", 1), (GX, 3), (GY, 2)), SUBSTEPS)
    electron = margins[0]
    cond_ext = margins[1]
    heat_ext = margins[2]
    lattice_ext = margins[3]
    occupancy_ext = margins[4]
    for substep_id in range(SUBSTEPS):
        margin = SUBSTEPS - substep_id - 1
        heat_ext = heat_ext[1:-1, 1:-1, 1:-1]
        lattice_ext = lattice_ext[1:-1, 1:-1, 1:-1]
        occupancy_ext = occupancy_ext[1:-1, 1:-1, 1:-1]
        global_z = depth_index * grid_shape[0] - margin + jnp.arange(heat_ext.shape[0])
        lower_open = (global_z != 0).astype(jnp.float32)[:, None, None]
        upper_open = (global_z != depth_total - 1).astype(jnp.float32)[:, None, None]
        lower_open, upper_open = (lower_open, upper_open)
        electron = substep(
            electron,
            cond_ext * electron,
            heat_ext,
            lattice_ext,
            occupancy_ext,
            lower_open,
            upper_open,
        )
        cond_ext = cond_ext[1:-1, 1:-1, 1:-1]
    exchange_rate = RELAX * (electron - lattice) / (electron + lattice)
    scaling = jnp.dot(
        exchange_rate.reshape(1, -1), cell_picks, precision=lax.Precision.HIGHEST
    ).reshape(-1)
    new_velocity = kicked * (1.0 + scaling) * alive_mask
    packed = jnp.concatenate(
        [
            jnp.reshape(jnp.sum(energy * alive_mask), (1,)),
            virial.reshape(9),
            jnp.reshape(live_count.astype(jnp.float32), (1,)),
        ]
    )
    summed = by_axis(packed, GX_GY_GZ)
    totals = summed[:10] / summed[10]
    return (forces, new_velocity, electron, totals)


def solution(mesh):
    torus = Mesh(
        mesh.devices.reshape(2, 4, 8, 2, mesh.shape["gz"]), ("gx_0", "gx_1", "gy_0", "gy_1", "gz")
    )
    placed = (
        P(None, GX_GY_GZ),
        P(None, GX_GY_GZ),
        P(None, GX_GY_GZ),
        P(GX_GY_GZ),
        P(GX_GY_GZ),
        P(GX_GY_GZ),
        P(GX_GY_GZ),
        P(),
        P(),
        P(),
        P("gz", GY, GX),
        P("gz", GY, GX),
        P("gz", GY, GX),
    )
    return jax.shard_map(
        local,
        mesh=torus,
        in_specs=placed,
        out_specs=(P(None, GX_GY_GZ), P(None, GX_GY_GZ), P("gz", GY, GX), P()),
        check_vma=False,
    )
```

profile of v0, /device:TPU:1, one launch (start us, length us, event | category | flops | bytes accessed | tf_op | source)
XLA Modules:
  0.0 194.4 jit_solution(10494831263220108505)
XLA Ops:
  2.0 0.8 copy.102
  3.6 6.6 %collective-permute-start = (f32[1,1,1,3,128]{3,4,2,1,0:T(8,128)S(1)}, f32[1,1,1,3,128]{3,4,2,1,0:T(8,128)S(1)}, u32[]{:S(2)}, u32[]{:S(2)}) collective-permute-start(f32[1,1,1,3,128]{3,4,2,1,0:T(8,128)S(1)} %bitcast_select_fusion.1), channel_id=1, source_target_pairs={{0,1},{1,2},{2,3},{3,0},{4,5},{5,6},{6,7},{7,4},{8,9},{9,10},{10,1... | collective-permute-start | bytes 4616 | tf_op jit(solution)/shard_map/ppermute | solution.py:32
  10.2 6.8 %collective-permute-start.1 = (f32[1,1,1,3,128]{3,4,2,1,0:T(8,128)S(1)}, f32[1,1,1,3,128]{3,4,2,1,0:T(8,128)S(1)}, u32[]{:S(2)}, u32[]{:S(2)}) collective-permute-start(f32[1,1,1,3,128]{3,4,2,1,0:T(8,128)S(1)} %bitcast_select_fusion.1), channel_id=1, source_target_pairs={{1,0},{2,1},{3,2},{0,3},{5,4},{6,5},{7,6},{4,7},{9,8},{10,9},{11,1... | collective-permute-start | bytes 4616 | tf_op jit(solution)/shard_map/ppermute | solution.py:34
  17.6 0.8 copy.117
  19.4 0.7 fusion.268
  21.6 0.7 broadcast_multiply_fusion.4
  22.3 0.7 constant_dynamic-update-slice_fusion.39
  23.0 0.7 constant_dynamic-update-slice_fusion.38
  24.0 3.1 %collective-permute-start.2 = (f32[1,1,3,3,128]{4,1,3,2,0:T(1,128)S(1)}, f32[1,1,3,3,128]{4,1,3,2,0:T(1,128)S(1)}, u32[]{:S(2)}, u32[]{:S(2)}) collective-permute-start(f32[1,1,3,3,128]{4,1,3,2,0:T(1,128)S(1)} %pad_maximum_fusion.11), channel_id=1, source_target_pairs={{0,64},{64,128},{128,192},{192,256},{256,320},{320,384},{384,448},... | collective-permute-start | bytes 13832 | tf_op jit(solution)/shard_map/ppermute | solution.py:32
  27.2 4.3 %collective-permute-start.3 = (f32[1,1,3,3,128]{4,1,3,2,0:T(1,128)S(1)}, f32[1,1,3,3,128]{4,1,3,2,0:T(1,128)S(1)}, u32[]{:S(2)}, u32[]{:S(2)}) collective-permute-start(f32[1,1,3,3,128]{4,1,3,2,0:T(1,128)S(1)} %pad_maximum_fusion.11), channel_id=1, source_target_pairs={{64,0},{128,64},{192,128},{256,192},{320,256},{384,320},{448,384},... | collective-permute-start | bytes 13832 | tf_op jit(solution)/shard_map/ppermute | solution.py:34
  31.5 0.7 collective-permute-done.3
  32.2 3.3 %collective-permute-start.4 = (f32[3,1,3,3,128]{4,1,3,2,0:T(1,128)S(1)}, f32[3,1,3,3,128]{4,1,3,2,0:T(1,128)S(1)}, u32[]{:S(2)}, u32[]{:S(2)}) collective-permute-start(f32[3,1,3,3,128]{4,1,3,2,0:T(1,128)S(1)} %pad_maximum_fusion.10), channel_id=1, source_target_pairs={{0,4},{4,8},{8,12},{12,16},{16,20},{20,24},{24,28},{28,32},{32,36}... | collective-permute-start | bytes 41480 | tf_op jit(solution)/shard_map/ppermute | solution.py:32
  35.6 0.8 copy.101
  36.5 2.2 %collective-permute-done.5 = f32[3,1,3,3,128]{4,1,3,2,0:T(1,128)S(1)} collective-permute-done((f32[3,1,3,3,128]{4,1,3,2,0:T(1,128)S(1)}, f32[3,1,3,3,128]{4,1,3,2,0:T(1,128)S(1)}, u32[]{:S(2)}, u32[]{:S(2)}) %collective-permute-start.5) | collective-permute-done | bytes 13856 | tf_op jit(solution)/shard_map/ppermute | solution.py:34
  38.8 0.7 pad_maximum_fusion.8
  39.6 3.3 %fusion.5 = f32[3,12288]{1,0:T(4,128)S(1)} fusion(f32[3,31,128]{2,1,0:T(8,128)S(1)} %dot_general.17, s32[12288]{0:T(1024)S(1)} %get-tuple-element.45, pred[31,12288]{1,0:T(8,128)(4,1)S(1)} %iota_compare_fusion.1), kind=kOutput, calls=%fused_computation.19 | convolution fusion | flops 1759137792 | bytes 625152 | tf_op jit(solution)/shard_map/dot_general | solution.py:102
  43.0 0.7 constant_dynamic-update-slice_fusion.34
  44.3 0.8 multiply_reduce_fusion.5
  45.2 2.7 %multiply_reduce_fusion = f32[16,16,512]{2,1,0:T(8,128)S(1)} fusion(f32[16,24,512]{2,1,0:T(8,128)S(1)} %constant_dynamic-update-slice_fusion.8, f32[16,24,512]{2,1,0:T(8,128)S(1)} %broadcast_multiply_fusion), kind=kLoop, calls=%fused_computation.3 | loop fusion | flops 6160384 | bytes 2097152 | tf_op jit(solution)/shard_map/reduce_sum | solution.py:155
  48.2 3.1 %multiply_reduce_fusion.1 = (f32[16,16,512]{2,1,0:T(8,128)S(1)}, f32[16,16,512]{2,1,0:T(8,128)S(1)}) fusion(f32[16,16,16]{2,1,0:T(8,128)S(1)} %copy.111, f32[16,16,512]{2,1,0:T(8,128)S(1)} %copy.110, f32[16,16,16]{2,1,0:T(8,128)S(1)} %get-tuple-element.35), kind=kLoop, calls=%fused_computation.4 | loop fusion | flops 8126464 | bytes 1605632 | tf_op jit(solution)/shard_map/reduce_sum | solution.py:170
  52.8 2.7 %collective-permute-start.6 = (f32[1,1,1,128,128]{3,4,2,1,0:T(8,128)S(1)}, f32[1,1,1,128,128]{3,4,2,1,0:T(8,128)S(1)}, u32[]{:S(2)}, u32[]{:S(2)}) collective-permute-start(f32[1,1,1,128,128]{3,4,2,1,0:T(8,128)S(1)} %bitcast_select_fusion), channel_id=1, source_target_pairs={{0,1},{1,2},{2,3},{3,0},{4,5},{5,6},{6,7},{7,4},{8,9},{9,10},{10,1... | collective-permute-start | bytes 196616 | tf_op jit(solution)/shard_map/ppermute | solution.py:32
  55.5 4.7 %collective-permute-start.7 = (f32[1,1,1,128,128]{3,4,2,1,0:T(8,128)S(1)}, f32[1,1,1,128,128]{3,4,2,1,0:T(8,128)S(1)}, u32[]{:S(2)}, u32[]{:S(2)}) collective-permute-start(f32[1,1,1,128,128]{3,4,2,1,0:T(8,128)S(1)} %bitcast_select_fusion), channel_id=1, source_target_pairs={{1,0},{2,1},{3,2},{0,3},{5,4},{6,5},{7,6},{4,7},{9,8},{10,9},{11,1... | collective-permute-start | bytes 196616 | tf_op jit(solution)/shard_map/ppermute | solution.py:34
  65.9 2.7 %collective-permute-start.8 = (f32[1,1,3,128,128]{3,4,2,1,0:T(8,128)S(1)}, f32[1,1,3,128,128]{3,4,2,1,0:T(8,128)S(1)}, u32[]{:S(2)}, u32[]{:S(2)}) collective-permute-start(f32[1,1,3,128,128]{3,4,2,1,0:T(8,128)S(1)} %pad_maximum_fusion.4), channel_id=1, source_target_pairs={{0,64},{64,128},{128,192},{192,256},{256,320},{320,384},{384,448},... | collective-permute-start | bytes 589832 | tf_op jit(solution)/shard_map/ppermute | solution.py:32
  68.6 5.5 %collective-permute-start.9 = (f32[1,1,3,128,128]{3,4,2,1,0:T(8,128)S(1)}, f32[1,1,3,128,128]{3,4,2,1,0:T(8,128)S(1)}, u32[]{:S(2)}, u32[]{:S(2)}) collective-permute-start(f32[1,1,3,128,128]{3,4,2,1,0:T(8,128)S(1)} %pad_maximum_fusion.4), channel_id=1, source_target_pairs={{64,0},{128,64},{192,128},{256,192},{320,256},{384,320},{448,384},... | collective-permute-start | bytes 589832 | tf_op jit(solution)/shard_map/ppermute | solution.py:34
  74.7 1.5 collective-permute-done.8
  76.2 0.9 collective-permute-done.9
  77.2 2.7 %collective-permute-start.10 = (f32[3,1,3,128,128]{3,4,2,1,0:T(8,128)S(1)}, f32[3,1,3,128,128]{3,4,2,1,0:T(8,128)S(1)}, u32[]{:S(2)}, u32[]{:S(2)}) collective-permute-start(f32[3,1,3,128,128]{3,4,2,1,0:T(8,128)S(1)} %pad_maximum_fusion.2), channel_id=1, source_target_pairs={{0,4},{4,8},{8,12},{12,16},{16,20},{20,24},{24,28},{28,32},{32,36}... | collective-permute-start | bytes 1769480 | tf_op jit(solution)/shard_map/ppermute | solution.py:32
  81.9 4.8 %collective-permute-done.10 = f32[3,1,3,128,128]{3,4,2,1,0:T(8,128)S(1)} collective-permute-done((f32[3,1,3,128,128]{3,4,2,1,0:T(8,128)S(1)}, f32[3,1,3,128,128]{3,4,2,1,0:T(8,128)S(1)}, u32[]{:S(2)}, u32[]{:S(2)}) %collective-permute-start.10) | collective-permute-done | bytes 589856 | tf_op jit(solution)/shard_map/ppermute | solution.py:32
  86.7 2.5 %collective-permute-done.11 = f32[3,1,3,128,128]{3,4,2,1,0:T(8,128)S(1)} collective-permute-done((f32[3,1,3,128,128]{3,4,2,1,0:T(8,128)S(1)}, f32[3,1,3,128,128]{3,4,2,1,0:T(8,128)S(1)}, u32[]{:S(2)}, u32[]{:S(2)}) %collective-permute-start.11) | collective-permute-done | bytes 589856 | tf_op jit(solution)/shard_map/ppermute | solution.py:34
  89.3 1.5 pad_maximum_fusion.table_ref
  90.8 18.7 %shard_map.156 = f32[128,12288]{1,0:T(8,128)} custom-call(s32[12288]{0:T(1024)} %bitcast.277, f32[3968,128]{1,0:T(8,128)} %pad_maximum_fusion.table_ref), custom_call_target="tpu_custom_call" | custom-call | bytes 14614528 | tf_op jit(solution)/shard_map/pallas_call | solution.py:77
  109.5 7.7 %copy.119 = f32[16,8,24,512]{3,2,1,0:T(8,128)S(1)} copy(f32[16,8,24,512]{3,1,2,0:T(8,128)} %bitcast.270) | data formatting | bytes 12582912
  117.3 2.3 %fusion.1 = (f32[8,24,512]{2,1,0:T(8,128)S(1)}, f32[16,24,512]{2,1,0:T(8,128)S(1)}, f32[16,24,512]{2,1,0:T(8,128)S(1)}, f32[8,24,512]{2,1,0:T(8,128)S(1)}) fusion(f32[16,24,512]{2,1,0:T(8,128)S(1)} %copy-done, f32[8,24,512]{2,1,0:T(8,128)S(1)} %broadcast_multiply_fusion.3, f32[8,16,512]{2,1,0:T(8,128)S(1)} %multiply_reduce_fusion.6, ...), kind=kLoop, calls=%fused_computation.9 | loop fusion | flops 11993088 | bytes 10878976 | tf_op jit(solution)/shard_map/transpose(jvp())/reduce_sum | solution.py:148
  120.8 1.0 convolution_bitcast_fusion
  121.9 0.7 pad_maximum_fusion.12
  122.6 3.8 %psum.35 = f32[11]{0:T(128)S(1)} all-reduce(f32[11]{0:T(128)S(1)} %pad_maximum_fusion.12), channel_id=1, replica_groups=mesh['gx_0'=2,'gx_1'=4,'gy_0'=8,'gy_1'=2,'gz'=4] {'gx_0'}, use_global_device_ids=true, to_apply=%region_17.18 | all-reduce | flops 11 | bytes 88 | tf_op jit(solution)/shard_map/psum | solution.py:42
  128.1 4.2 %collective-permute-start.12 = (f32[5,4,4,8]{3,2,1,0:T(4,128)S(1)}, f32[5,4,4,8]{3,2,1,0:T(4,128)S(1)}, u32[]{:S(2)}, u32[]{:S(2)}) collective-permute-start(f32[5,4,4,8]{3,2,1,0:T(4,128)S(1)} %constant_dynamic-update-slice_fusion.36), channel_id=1, source_target_pairs={{0,1},{1,2},{2,3},{3,0},{4,5},{5,6},{6,7},{7,4},{8,9},{9,10},{10,1... | collective-permute-start | bytes 7688 | tf_op jit(solution)/shard_map/ppermute | solution.py:32
  132.3 3.2 %collective-permute-start.13 = (f32[5,4,4,8]{3,2,1,0:T(4,128)S(1)}, f32[5,4,4,8]{3,2,1,0:T(4,128)S(1)}, u32[]{:S(2)}, u32[]{:S(2)}) collective-permute-start(f32[5,4,4,8]{3,2,1,0:T(4,128)S(1)} %constant_dynamic-update-slice_fusion.36), channel_id=1, source_target_pairs={{1,0},{2,1},{3,2},{0,3},{5,4},{6,5},{7,6},{4,7},{9,8},{10,9},{11,1... | collective-permute-start | bytes 7688 | tf_op jit(solution)/shard_map/ppermute | solution.py:34
  135.5 10.3 %psum.36 = f32[11]{0:T(128)S(1)} all-reduce(f32[11]{0:T(128)S(1)} %psum.35), channel_id=1, replica_groups=mesh['gx_0'=2,'gx_1'=4,'gy_0'=8,'gy_1'=2,'gz'=4] {'gx_1'}, use_global_device_ids=true, to_apply=%region_18.19 | all-reduce | flops 11 | bytes 88 | tf_op jit(solution)/shard_map/psum | solution.py:42
  145.8 14.4 %psum.37 = f32[11]{0:T(128)S(1)} all-reduce(f32[11]{0:T(128)S(1)} %psum.36), channel_id=1, replica_groups=mesh['gx_0'=2,'gx_1'=4,'gy_0'=8,'gy_1'=2,'gz'=4] {'gy_0'}, use_global_device_ids=true, to_apply=%region_19.20 | all-reduce | flops 11 | bytes 88 | tf_op jit(solution)/shard_map/psum | solution.py:42
  160.2 7.6 %psum.38 = f32[11]{0:T(128)S(1)} all-reduce(f32[11]{0:T(128)S(1)} %psum.37), channel_id=1, replica_groups=mesh['gx_0'=2,'gx_1'=4,'gy_0'=8,'gy_1'=2,'gz'=4] {'gy_1'}, use_global_device_ids=true, to_apply=%region_20.21 | all-reduce | flops 11 | bytes 88 | tf_op jit(solution)/shard_map/psum | solution.py:42
  167.9 1.9 collective-permute-start.14
  169.9 5.5 %collective-permute-start.15 = (f32[5,12,4,4]{3,2,1,0:T(4,128)S(1)}, f32[5,12,4,4]{3,2,1,0:T(4,128)S(1)}, u32[]{:S(2)}, u32[]{:S(2)}) collective-permute-start(f32[5,12,4,4]{3,2,1,0:T(4,128)S(1)} %get-tuple-element.41), channel_id=1, source_target_pairs={{64,0},{128,64},{192,128},{256,192},{320,256},{384,320},{448,384},... | collective-permute-start | bytes 11528 | tf_op jit(solution)/shard_map/ppermute | solution.py:34
  175.3 7.7 %psum.39 = f32[11]{0:T(128)S(1)} all-reduce(f32[11]{0:T(128)S(1)} %psum.38), channel_id=1, replica_groups=mesh['gx_0'=2,'gx_1'=4,'gy_0'=8,'gy_1'=2,'gz'=4] {'gz'}, use_global_device_ids=true, to_apply=%region_21.22 | all-reduce | flops 11 | bytes 88 | tf_op jit(solution)/shard_map/psum | solution.py:42
  183.8 3.1 %collective-permute-start.16 = (f32[5,12,4,16]{3,2,1,0:T(4,128)S(1)}, f32[5,12,4,16]{3,2,1,0:T(4,128)S(1)}, u32[]{:S(2)}, u32[]{:S(2)}) collective-permute-start(f32[5,12,4,16]{3,2,1,0:T(4,128)S(1)} %pad_maximum_fusion.7), channel_id=1, source_target_pairs={{0,4},{4,8},{8,12},{12,16},{16,20},{20,24},{24,28},{28,32},{32,36}... | collective-permute-start | bytes 46088 | tf_op jit(solution)/shard_map/ppermute | solution.py:32
  186.9 1.2 slice_divide_fusion
  188.8 2.7 %collective-permute-done.17 = f32[5,12,4,16]{3,2,1,0:T(4,128)S(1)} collective-permute-done((f32[5,12,4,16]{3,2,1,0:T(4,128)S(1)}, f32[5,12,4,16]{3,2,1,0:T(4,128)S(1)}, u32[]{:S(2)}, u32[]{:S(2)}) %collective-permute-start.17) | collective-permute-done | bytes 15392 | tf_op jit(solution)/shard_map/ppermute | solution.py:34
  192.7 0.7 add_divide_fusion
  (149 shorter events, 22.7 us)
Async XLA Ops:
  0.6 42.3 %copy-start.2 = (f32[3,512]{1,0:T(4,128)S(1)}, f32[3,512]{1,0:T(4,128)}, u32[]{:S(2)}) copy-start(f32[3,512]{1,0:T(4,128)} %param.13) | copy-start | bytes 18436
  3.6 20.3 %collective-permute-start = (f32[1,1,1,3,128]{3,4,2,1,0:T(8,128)S(1)}, f32[1,1,1,3,128]{3,4,2,1,0:T(8,128)S(1)}, u32[]{:S(2)}, u32[]{:S(2)}) collective-permute-start(f32[1,1,1,3,128]{3,4,2,1,0:T(8,128)S(1)} %bitcast_select_fusion.1), channel_id=1, source_target_pairs={{0,1},{1,2},{2,3},{3,0},{4,5},{5,6},{6,7},{7,4},{8,9},{9,10},{10,1... | collective-permute-start | bytes 4616 | tf_op jit(solution)/shard_map/ppermute | solution.py:32
  10.2 13.7 %collective-permute-start.1 = (f32[1,1,1,3,128]{3,4,2,1,0:T(8,128)S(1)}, f32[1,1,1,3,128]{3,4,2,1,0:T(8,128)S(1)}, u32[]{:S(2)}, u32[]{:S(2)}) collective-permute-start(f32[1,1,1,3,128]{3,4,2,1,0:T(8,128)S(1)} %bitcast_select_fusion.1), channel_id=1, source_target_pairs={{1,0},{2,1},{3,2},{0,3},{5,4},{6,5},{7,6},{4,7},{9,8},{10,9},{11,1... | collective-permute-start | bytes 4616 | tf_op jit(solution)/shard_map/ppermute | solution.py:34
  18.5 25.3 %copy-start.1 = (s32[3,4,8,128]{3,1,2,0:T(4,128)}, s32[3,4,8,128]{3,1,2,0:T(4,128)S(1)}, u32[]{:S(2)}) copy-start(s32[3,4,8,128]{3,1,2,0:T(4,128)S(1)} %copy.117) | copy-start | bytes 147460
  24.0 7.4 %collective-permute-start.2 = (f32[1,1,3,3,128]{4,1,3,2,0:T(1,128)S(1)}, f32[1,1,3,3,128]{4,1,3,2,0:T(1,128)S(1)}, u32[]{:S(2)}, u32[]{:S(2)}) collective-permute-start(f32[1,1,3,3,128]{4,1,3,2,0:T(1,128)S(1)} %pad_maximum_fusion.11), channel_id=1, source_target_pairs={{0,64},{64,128},{128,192},{192,256},{256,320},{320,384},{384,448},... | collective-permute-start | bytes 13832 | tf_op jit(solution)/shard_map/ppermute | solution.py:32
  27.2 5.0 %collective-permute-start.3 = (f32[1,1,3,3,128]{4,1,3,2,0:T(1,128)S(1)}, f32[1,1,3,3,128]{4,1,3,2,0:T(1,128)S(1)}, u32[]{:S(2)}, u32[]{:S(2)}) collective-permute-start(f32[1,1,3,3,128]{4,1,3,2,0:T(1,128)S(1)} %pad_maximum_fusion.11), channel_id=1, source_target_pairs={{64,0},{128,64},{192,128},{256,192},{320,256},{384,320},{448,384},... | collective-permute-start | bytes 13832 | tf_op jit(solution)/shard_map/ppermute | solution.py:34
  32.2 4.3 %collective-permute-start.4 = (f32[3,1,3,3,128]{4,1,3,2,0:T(1,128)S(1)}, f32[3,1,3,3,128]{4,1,3,2,0:T(1,128)S(1)}, u32[]{:S(2)}, u32[]{:S(2)}) collective-permute-start(f32[3,1,3,3,128]{4,1,3,2,0:T(1,128)S(1)} %pad_maximum_fusion.10), channel_id=1, source_target_pairs={{0,4},{4,8},{8,12},{12,16},{16,20},{20,24},{24,28},{28,32},{32,36}... | collective-permute-start | bytes 41480 | tf_op jit(solution)/shard_map/ppermute | solution.py:32
  35.5 3.2 %collective-permute-start.5 = (f32[3,1,3,3,128]{4,1,3,2,0:T(1,128)S(1)}, f32[3,1,3,3,128]{4,1,3,2,0:T(1,128)S(1)}, u32[]{:S(2)}, u32[]{:S(2)}) collective-permute-start(f32[3,1,3,3,128]{4,1,3,2,0:T(1,128)S(1)} %pad_maximum_fusion.10), channel_id=1, source_target_pairs={{4,0},{8,4},{12,8},{16,12},{20,16},{24,20},{28,24},{32,28},{36,32}... | collective-permute-start | bytes 41480 | tf_op jit(solution)/shard_map/ppermute | solution.py:34
  44.3 7.1 %copy-start.5 = (f32[16,8]{0,1:T(8,128)S(1)}, f32[16,8]{0,1:T(8,128)}, u32[]{:S(2)}) copy-start(f32[16,8]{0,1:T(8,128)} %param.20) | copy-start | bytes 1540
  48.2 31.7 %copy-start.6 = (f32[16]{0:T(128)S(1)}, f32[16]{0:T(128)}, u32[]{:S(2)}) copy-start(f32[16]{0:T(128)} %param.21) | copy-start | bytes 196
  52.8 13.1 %collective-permute-start.6 = (f32[1,1,1,128,128]{3,4,2,1,0:T(8,128)S(1)}, f32[1,1,1,128,128]{3,4,2,1,0:T(8,128)S(1)}, u32[]{:S(2)}, u32[]{:S(2)}) collective-permute-start(f32[1,1,1,128,128]{3,4,2,1,0:T(8,128)S(1)} %bitcast_select_fusion), channel_id=1, source_target_pairs={{0,1},{1,2},{2,3},{3,0},{4,5},{5,6},{6,7},{7,4},{8,9},{9,10},{10,1... | collective-permute-start | bytes 196616 | tf_op jit(solution)/shard_map/ppermute | solution.py:32
  55.5 10.4 %collective-permute-start.7 = (f32[1,1,1,128,128]{3,4,2,1,0:T(8,128)S(1)}, f32[1,1,1,128,128]{3,4,2,1,0:T(8,128)S(1)}, u32[]{:S(2)}, u32[]{:S(2)}) collective-permute-start(f32[1,1,1,128,128]{3,4,2,1,0:T(8,128)S(1)} %bitcast_select_fusion), channel_id=1, source_target_pairs={{1,0},{2,1},{3,2},{0,3},{5,4},{6,5},{7,6},{4,7},{9,8},{10,9},{11,1... | collective-permute-start | bytes 196616 | tf_op jit(solution)/shard_map/ppermute | solution.py:34
  65.9 10.3 %collective-permute-start.8 = (f32[1,1,3,128,128]{3,4,2,1,0:T(8,128)S(1)}, f32[1,1,3,128,128]{3,4,2,1,0:T(8,128)S(1)}, u32[]{:S(2)}, u32[]{:S(2)}) collective-permute-start(f32[1,1,3,128,128]{3,4,2,1,0:T(8,128)S(1)} %pad_maximum_fusion.4), channel_id=1, source_target_pairs={{0,64},{64,128},{128,192},{192,256},{256,320},{320,384},{384,448},... | collective-permute-start | bytes 589832 | tf_op jit(solution)/shard_map/ppermute | solution.py:32
  68.6 8.5 %collective-permute-start.9 = (f32[1,1,3,128,128]{3,4,2,1,0:T(8,128)S(1)}, f32[1,1,3,128,128]{3,4,2,1,0:T(8,128)S(1)}, u32[]{:S(2)}, u32[]{:S(2)}) collective-permute-start(f32[1,1,3,128,128]{3,4,2,1,0:T(8,128)S(1)} %pad_maximum_fusion.4), channel_id=1, source_target_pairs={{64,0},{128,64},{192,128},{256,192},{320,256},{384,320},{448,384},... | collective-permute-start | bytes 589832 | tf_op jit(solution)/shard_map/ppermute | solution.py:34
  77.2 9.5 %collective-permute-start.10 = (f32[3,1,3,128,128]{3,4,2,1,0:T(8,128)S(1)}, f32[3,1,3,128,128]{3,4,2,1,0:T(8,128)S(1)}, u32[]{:S(2)}, u32[]{:S(2)}) collective-permute-start(f32[3,1,3,128,128]{3,4,2,1,0:T(8,128)S(1)} %pad_maximum_fusion.2), channel_id=1, source_target_pairs={{0,4},{4,8},{8,12},{12,16},{16,20},{20,24},{24,28},{28,32},{32,36}... | collective-permute-start | bytes 1769480 | tf_op jit(solution)/shard_map/ppermute | solution.py:32
  79.9 9.3 %collective-permute-start.11 = (f32[3,1,3,128,128]{3,4,2,1,0:T(8,128)S(1)}, f32[3,1,3,128,128]{3,4,2,1,0:T(8,128)S(1)}, u32[]{:S(2)}, u32[]{:S(2)}) collective-permute-start(f32[3,1,3,128,128]{3,4,2,1,0:T(8,128)S(1)} %pad_maximum_fusion.2), channel_id=1, source_target_pairs={{4,0},{8,4},{12,8},{16,12},{20,16},{24,20},{28,24},{32,28},{36,32}... | collective-permute-start | bytes 1769480 | tf_op jit(solution)/shard_map/ppermute | solution.py:34
  109.5 7.7 %copy-start = (f32[16,24,512]{2,1,0:T(8,128)S(1)}, f32[16,24,512]{2,1,0:T(8,128)}, u32[]{:S(2)}) copy-start(f32[16,24,512]{2,1,0:T(8,128)} %constant_dynamic-update-slice_fusion.22) | copy-start | bytes 2359300
  119.6 6.8 %copy-start.4 = (f32[3,512]{1,0:T(4,128)S(1)}, f32[3,512]{1,0:T(4,128)}, u32[]{:S(2)}) copy-start(f32[3,512]{1,0:T(4,128)} %param.14) | copy-start | bytes 18436
  119.6 6.9 %copy-start.7 = (s32[512]{0:T(512)S(1)}, s32[512]{0:T(512)}, u32[]{:S(2)}) copy-start(s32[512]{0:T(512)} %param.19) | copy-start | bytes 6148
  120.8 73.6 %copy-start.3 = (f32[3,512]{1,0:T(4,128)}, f32[3,512]{1,0:T(4,128)S(1)}, u32[]{:S(2)}) copy-start(f32[3,512]{1,0:T(4,128)S(1)} %get-tuple-element.22) | copy-start | bytes 18436
  128.1 39.7 %collective-permute-start.12 = (f32[5,4,4,8]{3,2,1,0:T(4,128)S(1)}, f32[5,4,4,8]{3,2,1,0:T(4,128)S(1)}, u32[]{:S(2)}, u32[]{:S(2)}) collective-permute-start(f32[5,4,4,8]{3,2,1,0:T(4,128)S(1)} %constant_dynamic-update-slice_fusion.36), channel_id=1, source_target_pairs={{0,1},{1,2},{2,3},{3,0},{4,5},{5,6},{6,7},{7,4},{8,9},{9,10},{10,1... | collective-permute-start | bytes 7688 | tf_op jit(solution)/shard_map/ppermute | solution.py:32
  132.3 35.5 %collective-permute-start.13 = (f32[5,4,4,8]{3,2,1,0:T(4,128)S(1)}, f32[5,4,4,8]{3,2,1,0:T(4,128)S(1)}, u32[]{:S(2)}, u32[]{:S(2)}) collective-permute-start(f32[5,4,4,8]{3,2,1,0:T(4,128)S(1)} %constant_dynamic-update-slice_fusion.36), channel_id=1, source_target_pairs={{1,0},{2,1},{3,2},{0,3},{5,4},{6,5},{7,6},{4,7},{9,8},{10,9},{11,1... | collective-permute-start | bytes 7688 | tf_op jit(solution)/shard_map/ppermute | solution.py:34
  167.9 15.7 %collective-permute-start.14 = (f32[5,12,4,4]{3,2,1,0:T(4,128)S(1)}, f32[5,12,4,4]{3,2,1,0:T(4,128)S(1)}, u32[]{:S(2)}, u32[]{:S(2)}) collective-permute-start(f32[5,12,4,4]{3,2,1,0:T(4,128)S(1)} %get-tuple-element.40), channel_id=1, source_target_pairs={{0,64},{64,128},{128,192},{192,256},{256,320},{320,384},{384,448},... | collective-permute-start | bytes 11528 | tf_op jit(solution)/shard_map/ppermute | solution.py:32
  169.9 13.8 %collective-permute-start.15 = (f32[5,12,4,4]{3,2,1,0:T(4,128)S(1)}, f32[5,12,4,4]{3,2,1,0:T(4,128)S(1)}, u32[]{:S(2)}, u32[]{:S(2)}) collective-permute-start(f32[5,12,4,4]{3,2,1,0:T(4,128)S(1)} %get-tuple-element.41), channel_id=1, source_target_pairs={{64,0},{128,64},{192,128},{256,192},{320,256},{384,320},{448,384},... | collective-permute-start | bytes 11528 | tf_op jit(solution)/shard_map/ppermute | solution.py:34
  183.8 4.9 %collective-permute-start.16 = (f32[5,12,4,16]{3,2,1,0:T(4,128)S(1)}, f32[5,12,4,16]{3,2,1,0:T(4,128)S(1)}, u32[]{:S(2)}, u32[]{:S(2)}) collective-permute-start(f32[5,12,4,16]{3,2,1,0:T(4,128)S(1)} %pad_maximum_fusion.7), channel_id=1, source_target_pairs={{0,4},{4,8},{8,12},{12,16},{16,20},{20,24},{24,28},{28,32},{32,36}... | collective-permute-start | bytes 46088 | tf_op jit(solution)/shard_map/ppermute | solution.py:32
  186.9 4.6 %collective-permute-start.17 = (f32[5,12,4,16]{3,2,1,0:T(4,128)S(1)}, f32[5,12,4,16]{3,2,1,0:T(4,128)S(1)}, u32[]{:S(2)}, u32[]{:S(2)}) collective-permute-start(f32[5,12,4,16]{3,2,1,0:T(4,128)S(1)} %pad_maximum_fusion.7), channel_id=1, source_target_pairs={{4,0},{8,4},{12,8},{16,12},{20,16},{24,20},{28,24},{32,28},{36,32}... | collective-permute-start | bytes 46088 | tf_op jit(solution)/shard_map/ppermute | solution.py:34
where the time goes:
time: 196 us; the launch traced here: 194 us
  starting transfers between devices  60.1 us (31%)
  blocking collectives  43.7 us (22%)
  other arithmetic  31.2 us (16%)
  Pallas kernels  18.7 us (10%)
  local copies, waits for them, and re-layouts  17.7 us (9%)
  waiting for transfers between devices  16 us (8%)
  matrix products  4.84 us (2%)
  between operations  2.06 us (1%)
    psum x5, blocking collectives, by_axis(): return functools.reduce(lax.psum, axes, shard)  43.7 us
    ppermute x9, starting transfers between devices, padded(): lax.ppermute(tail, axis, [(i, (i + 1) % count) for i in range(count)])  30.3 us
    ppermute x9, starting transfers between devices, padded(): lax.ppermute(head, axis, [((i + 1) % count, i) for i in range(count)])  29.8 us
    pallas_call x1, Pallas kernels, row_gather(): pl.pallas_call(kernel, out_shape=jax.ShapeDtypeStruct((width, total), tab...  18.7 us
    unnamed x26, local copies, waits for them, and re-layouts  12.9 us
    ppermute x9, waiting for transfers between devices, padded(): lax.ppermute(head, axis, [((i + 1) % count, i) for i in range(count)])  9.01 us
    unnamed x29, other arithmetic  7.98 us
    ppermute x9, waiting for transfers between devices, padded(): lax.ppermute(tail, axis, [(i, (i + 1) % count) for i in range(count)])  6.98 us
  transfers between devices with their start and end apart: 18, of which 8 were waited for; matrix products, arithmetic and copies ran while one was open for 9% of the time, Pallas kernels for 0%

commit v1 on v0

--- a/solution.py
+++ b/solution.py
@@ -144,8 +144,8 @@
 
 
 def pair_energy(vector, weights):
-    basis = radial(vector, weights.shape[0])
-    mixed = jnp.sum(weights * basis[:, None], axis=0)
+    basis = radial(vector, weights.shape[1])
+    mixed = jnp.sum(weights * basis[None], axis=1)
     return jnp.sum(mixed * harmonics(vector), axis=0)
 
 
@@ -244,7 +244,7 @@
     basis_sum = atom_basis(separation, pair_mask, radial_weight)
     energy, adjoint = adjoints(basis_sum, linear_weight, pair_coupling)
     reduced = jnp.sum(radial_weight.T[:, :, None, None] * adjoint[None], axis=1)
-    own_table = reduced.reshape(orders * 16, atom_slots)
+    own_table = jnp.transpose(reduced, (1, 0, 2)).reshape(16 * orders, atom_slots)
     picked = jnp.take(own_table, ghost_list, axis=1).reshape(1, 1, 1, orders * 16, ghosts)
     framed_adjoint = padded(picked, (("gz", 2), (GX, 0), (GY, 1)), 1)
     remote = framed_adjoint.reshape(27, orders * 16, ghosts)
@@ -252,10 +252,10 @@
         [own_table.T, jnp.transpose(remote, (0, 2, 1)).reshape(27 * ghosts, orders * 16)], axis=0
     )
     other_weights = row_gather(table_rows, neighbour_index.reshape(-1)).reshape(
-        orders, 16, neigh_depth, atom_slots
+        16, orders, neigh_depth, atom_slots
     )
     forces, virial = pair_forces(
-        separation, pair_mask, own_table.reshape(orders, 16, 1, atom_slots), other_weights
+        separation, pair_mask, own_table.reshape(16, orders, 1, atom_slots), other_weights
     )
     kicked = velocities + KICK * forces
     grid_shape = electron_temp.shape

time: 196 us -> 196 us (level)
  local copies, waits for them, and re-layouts: 17.7 us -> 10.4 us
  other arithmetic: 31.2 us -> 38.1 us
    ppermute x9, starting transfers between devices: 29.8 us -> 44.1 us  [padded(): lax.ppermute(head, axis, [((i + 1) % count, i) for i in range(count)])]
    ppermute x9, starting transfers between devices: 30.3 us -> 17.5 us  [padded(): lax.ppermute(tail, axis, [(i, (i + 1) % count) for i in range(count)])]
    unnamed x26 -> x25, local copies, waits for them, and re-layouts: 12.9 us -> 5.19 us
    reduce_sum x1, other arithmetic: 2.3 us -> 7.34 us  [pair_energy(): mixed = jnp.sum(weights * basis[None], axis=1)]
  transfers between devices with their start and end apart: 18 -> 18, of which waited for: 8 -> 6; matrix products, arithmetic and copies ran while one was open for 9% -> 9% of each run, Pallas kernels for 0% -> 0%
where the time goes in v1:
time: 196 us; the launch traced here: 195 us
  starting transfers between devices  61.6 us (31%)
  blocking collectives  43.4 us (22%)
  other arithmetic  38.1 us (19%)
  Pallas kernels  18.9 us (10%)
  waiting for transfers between devices  16.1 us (8%)
  local copies, waits for them, and re-layouts  10.4 us (5%)
  matrix products  4.83 us (2%)
  between operations  2.07 us (1%)
    ppermute x9, starting transfers between devices, padded(): lax.ppermute(head, axis, [((i + 1) % count, i) for i in range(count)])  44.1 us
    psum x5, blocking collectives, by_axis(): return functools.reduce(lax.psum, axes, shard)  43.4 us
    pallas_call x1, Pallas kernels, row_gather(): pl.pallas_call(kernel, out_shape=jax.ShapeDtypeStruct((width, total), tab...  18.9 us
    ppermute x9, starting transfers between devices, padded(): lax.ppermute(tail, axis, [(i, (i + 1) % count) for i in range(count)])  17.5 us
    ppermute x9, waiting for transfers between devices, padded(): lax.ppermute(tail, axis, [(i, (i + 1) % count) for i in range(count)])  8.75 us
    unnamed x29, other arithmetic  7.98 us
    ppermute x9, waiting for transfers between devices, padded(): lax.ppermute(head, axis, [((i + 1) % count, i) for i in range(count)])  7.37 us
    reduce_sum x1, other arithmetic, pair_energy(): mixed = jnp.sum(weights * basis[None], axis=1)  7.34 us
  transfers between devices with their start and end apart: 18, of which 6 were waited for; matrix products, arithmetic and copies ran while one was open for 9% of the time, Pallas kernels for 0%

profile of v1, /device:TPU:1, one launch (start us, length us, event | category | flops | bytes accessed | tf_op | source)
XLA Modules:
  0.0 195.3 jit_solution(7588377031849226364)
XLA Ops:
  2.0 0.8 copy.128
  3.5 11.5 %collective-permute-start.1 = (f32[1,1,1,3,128]{3,4,2,1,0:T(8,128)S(1)}, f32[1,1,1,3,128]{3,4,2,1,0:T(8,128)S(1)}, u32[]{:S(2)}, u32[]{:S(2)}) collective-permute-start(f32[1,1,1,3,128]{3,4,2,1,0:T(8,128)S(1)} %bitcast_select_fusion.1), channel_id=1, source_target_pairs={{1,0},{2,1},{3,2},{0,3},{5,4},{6,5},{7,6},{4,7},{9,8},{10,9},{11,1... | collective-permute-start | bytes 4616 | tf_op jit(solution)/shard_map/ppermute | solution.py:34
  15.0 1.9 collective-permute-start
  18.3 0.8 fusion.267
  19.1 0.7 constant_dynamic-update-slice_fusion.40
  19.8 0.7 fusion.167
  20.5 0.8 copy.150
  21.6 0.7 broadcast_multiply_fusion.2
  22.3 0.7 constant_dynamic-update-slice_fusion.39
  23.0 0.7 constant_dynamic-update-slice_fusion.38
  24.1 5.3 %collective-permute-start.3 = (f32[1,1,3,3,128]{4,1,3,2,0:T(1,128)S(1)}, f32[1,1,3,3,128]{4,1,3,2,0:T(1,128)S(1)}, u32[]{:S(2)}, u32[]{:S(2)}) collective-permute-start(f32[1,1,3,3,128]{4,1,3,2,0:T(1,128)S(1)} %pad_maximum_fusion.11), channel_id=1, source_target_pairs={{64,0},{128,64},{192,128},{256,192},{320,256},{384,320},{448,384},... | collective-permute-start | bytes 13832 | tf_op jit(solution)/shard_map/ppermute | solution.py:34
  29.4 1.9 collective-permute-start.2
  31.3 4.5 %collective-permute-done.2 = f32[1,1,3,3,128]{4,1,3,2,0:T(1,128)S(1)} collective-permute-done((f32[1,1,3,3,128]{4,1,3,2,0:T(1,128)S(1)}, f32[1,1,3,3,128]{4,1,3,2,0:T(1,128)S(1)}, u32[]{:S(2)}, u32[]{:S(2)}) %collective-permute-start.2) | collective-permute-done | bytes 4640 | tf_op jit(solution)/shard_map/ppermute | solution.py:32
  35.9 2.4 %collective-permute-start.5 = (f32[3,1,3,3,128]{4,1,3,2,0:T(1,128)S(1)}, f32[3,1,3,3,128]{4,1,3,2,0:T(1,128)S(1)}, u32[]{:S(2)}, u32[]{:S(2)}) collective-permute-start(f32[3,1,3,3,128]{4,1,3,2,0:T(1,128)S(1)} %pad_maximum_fusion.10), channel_id=1, source_target_pairs={{4,0},{8,4},{12,8},{16,12},{20,16},{24,20},{28,24},{32,28},{36,32}... | collective-permute-start | bytes 41480 | tf_op jit(solution)/shard_map/ppermute | solution.py:34
  38.3 1.2 collective-permute-start.4
  39.5 0.8 copy.127
  41.0 0.7 pad_maximum_fusion.8
  41.8 3.3 %fusion.3 = f32[3,12288]{1,0:T(4,128)S(1)} fusion(f32[3,31,128]{2,1,0:T(8,128)S(1)} %dot_general.17, s32[12288]{0:T(1024)S(1)} %get-tuple-element.47, pred[31,12288]{1,0:T(8,128)(4,1)S(1)} %iota_compare_fusion.1), kind=kOutput, calls=%fused_computation.17 | convolution fusion | flops 1759137792 | bytes 625152 | tf_op jit(solution)/shard_map/dot_general | solution.py:102
  45.1 0.7 constant_dynamic-update-slice_fusion.34
  46.7 2.2 %multiply_reduce_fusion.7 = f32[16,24,512]{2,1,0:T(8,128)S(1)} fusion(f32[8,24,512]{2,0,1:T(8,128)S(1)} %copy.136, f32[16,8]{1,0:T(8,128)S(1)} %copy.127), kind=kLoop, calls=%fused_computation.10 | loop fusion | flops 2949120 | bytes 1180160 | tf_op jit(solution)/shard_map/reduce_sum | solution.py:154
  49.0 2.7 %multiply_reduce_fusion = f32[16,16,512]{2,1,0:T(8,128)S(1)} fusion(f32[16,24,512]{2,1,0:T(8,128)S(1)} %constant_dynamic-update-slice_fusion.8, f32[16,24,512]{2,1,0:T(8,128)S(1)} %broadcast_multiply_fusion), kind=kLoop, calls=%fused_computation.3 | loop fusion | flops 6160384 | bytes 2097152 | tf_op jit(solution)/shard_map/reduce_sum | solution.py:155
  52.0 3.1 %multiply_reduce_fusion.1 = (f32[16,16,512]{2,1,0:T(8,128)S(1)}, f32[16,16,512]{2,1,0:T(8,128)S(1)}) fusion(f32[16,16,16]{2,1,0:T(8,128)S(1)} %copy.138, f32[16,16,512]{2,1,0:T(8,128)S(1)} %copy.137, f32[16,16,16]{2,1,0:T(8,128)S(1)} %get-tuple-element.37), kind=kLoop, calls=%fused_computation.4 | loop fusion | flops 8126464 | bytes 1605632 | tf_op jit(solution)/shard_map/reduce_sum | solution.py:170
  56.8 5.8 %collective-permute-start.7 = (f32[1,1,1,128,128]{3,4,2,1,0:T(8,128)S(1)}, f32[1,1,1,128,128]{3,4,2,1,0:T(8,128)S(1)}, u32[]{:S(2)}, u32[]{:S(2)}) collective-permute-start(f32[1,1,1,128,128]{3,4,2,1,0:T(8,128)S(1)} %bitcast_select_fusion), channel_id=1, source_target_pairs={{1,0},{2,1},{3,2},{0,3},{5,4},{6,5},{7,6},{4,7},{9,8},{10,9},{11,1... | collective-permute-start | bytes 196616 | tf_op jit(solution)/shard_map/ppermute | solution.py:34
  62.5 1.9 collective-permute-start.6
  70.2 2.1 %collective-permute-start.9 = (f32[1,1,3,128,128]{3,4,2,1,0:T(8,128)S(1)}, f32[1,1,3,128,128]{3,4,2,1,0:T(8,128)S(1)}, u32[]{:S(2)}, u32[]{:S(2)}) collective-permute-start(f32[1,1,3,128,128]{3,4,2,1,0:T(8,128)S(1)} %pad_maximum_fusion.4), channel_id=1, source_target_pairs={{64,0},{128,64},{192,128},{256,192},{320,256},{384,320},{448,384},... | collective-permute-start | bytes 589832 | tf_op jit(solution)/shard_map/ppermute | solution.py:34
  72.3 3.4 %collective-permute-start.8 = (f32[1,1,3,128,128]{3,4,2,1,0:T(8,128)S(1)}, f32[1,1,3,128,128]{3,4,2,1,0:T(8,128)S(1)}, u32[]{:S(2)}, u32[]{:S(2)}) collective-permute-start(f32[1,1,3,128,128]{3,4,2,1,0:T(8,128)S(1)} %pad_maximum_fusion.4), channel_id=1, source_target_pairs={{0,64},{64,128},{128,192},{192,256},{256,320},{320,384},{384,448},... | collective-permute-start | bytes 589832 | tf_op jit(solution)/shard_map/ppermute | solution.py:32
  76.6 4.2 %collective-permute-done.8 = f32[1,1,3,128,128]{3,4,2,1,0:T(8,128)S(1)} collective-permute-done((f32[1,1,3,128,128]{3,4,2,1,0:T(8,128)S(1)}, f32[1,1,3,128,128]{3,4,2,1,0:T(8,128)S(1)}, u32[]{:S(2)}, u32[]{:S(2)}) %collective-permute-start.8) | collective-permute-done | bytes 196640 | tf_op jit(solution)/shard_map/ppermute | solution.py:32
  80.9 5.5 %collective-permute-start.11 = (f32[3,1,3,128,128]{3,4,2,1,0:T(8,128)S(1)}, f32[3,1,3,128,128]{3,4,2,1,0:T(8,128)S(1)}, u32[]{:S(2)}, u32[]{:S(2)}) collective-permute-start(f32[3,1,3,128,128]{3,4,2,1,0:T(8,128)S(1)} %pad_maximum_fusion.2), channel_id=1, source_target_pairs={{4,0},{8,4},{12,8},{16,12},{20,16},{24,20},{28,24},{32,28},{36,32}... | collective-permute-start | bytes 1769480 | tf_op jit(solution)/shard_map/ppermute | solution.py:34
  88.3 5.1 %collective-permute-done.11 = f32[3,1,3,128,128]{3,4,2,1,0:T(8,128)S(1)} collective-permute-done((f32[3,1,3,128,128]{3,4,2,1,0:T(8,128)S(1)}, f32[3,1,3,128,128]{3,4,2,1,0:T(8,128)S(1)}, u32[]{:S(2)}, u32[]{:S(2)}) %collective-permute-start.11) | collective-permute-done | bytes 589856 | tf_op jit(solution)/shard_map/ppermute | solution.py:34
  93.6 1.5 pad_maximum_fusion.table_ref
  95.1 18.9 %shard_map.156 = f32[128,12288]{1,0:T(8,128)} custom-call(s32[12288]{0:T(1024)} %bitcast.270, f32[3968,128]{1,0:T(8,128)} %pad_maximum_fusion.table_ref), custom_call_target="tpu_custom_call" | custom-call | bytes 14614528 | tf_op jit(solution)/shard_map/pallas_call | solution.py:77
  113.9 7.3 %multiply_reduce_fusion.3 = (f32[8,24,512]{2,0,1:T(8,128)S(1)}, f32[16,24,512]{2,1,0:T(8,128)S(1)}, f32[16,24,512]{2,1,0:T(8,128)S(1)}, f32[8,24,512]{2,0,1:T(8,128)S(1)}) fusion(f32[16,8,24,512]{3,1,2,0:T(8,128)} %bitcast.263, f32[16,24,512]{2,1,0:T(8,128)S(1)} %copy-done, f32[8,24,512]{2,0,1:T(8,128)S(1)} %copy.136, f32[16,8,512]{2,1,0:T(8,128)S(1)} %copy.168, ...), kind=kLoop, calls=%fused_computation.6 | loop fusion | flops 11993088 | bytes 10878976 | tf_op jit(solution)/shard_map/transpose(jvp())/reduce_sum | solution.py:148
  122.9 1.0 convolution_bitcast_fusion
  124.0 0.7 pad_maximum_fusion.12
  124.7 3.8 %psum.35 = f32[11]{0:T(128)S(1)} all-reduce(f32[11]{0:T(128)S(1)} %pad_maximum_fusion.12), channel_id=1, replica_groups=mesh['gx_0'=2,'gx_1'=4,'gy_0'=8,'gy_1'=2,'gz'=4] {'gx_0'}, use_global_device_ids=true, to_apply=%region_17.18 | all-reduce | flops 11 | bytes 88 | tf_op jit(solution)/shard_map/psum | solution.py:42
  130.2 4.9 %collective-permute-start.13 = (f32[5,4,4,8]{3,2,1,0:T(4,128)S(1)}, f32[5,4,4,8]{3,2,1,0:T(4,128)S(1)}, u32[]{:S(2)}, u32[]{:S(2)}) collective-permute-start(f32[5,4,4,8]{3,2,1,0:T(4,128)S(1)} %constant_dynamic-update-slice_fusion.36), channel_id=1, source_target_pairs={{1,0},{2,1},{3,2},{0,3},{5,4},{6,5},{7,6},{4,7},{9,8},{10,9},{11,1... | collective-permute-start | bytes 7688 | tf_op jit(solution)/shard_map/ppermute | solution.py:34
  135.1 1.9 collective-permute-start.12
  137.0 6.0 %psum.36 = f32[11]{0:T(128)S(1)} all-reduce(f32[11]{0:T(128)S(1)} %psum.35), channel_id=1, replica_groups=mesh['gx_0'=2,'gx_1'=4,'gy_0'=8,'gy_1'=2,'gz'=4] {'gx_1'}, use_global_device_ids=true, to_apply=%region_18.19 | all-reduce | flops 11 | bytes 88 | tf_op jit(solution)/shard_map/psum | solution.py:42
  143.0 14.2 %psum.37 = f32[11]{0:T(128)S(1)} all-reduce(f32[11]{0:T(128)S(1)} %psum.36), channel_id=1, replica_groups=mesh['gx_0'=2,'gx_1'=4,'gy_0'=8,'gy_1'=2,'gz'=4] {'gy_0'}, use_global_device_ids=true, to_apply=%region_19.20 | all-reduce | flops 11 | bytes 88 | tf_op jit(solution)/shard_map/psum | solution.py:42
  157.2 8.6 %psum.38 = f32[11]{0:T(128)S(1)} all-reduce(f32[11]{0:T(128)S(1)} %psum.37), channel_id=1, replica_groups=mesh['gx_0'=2,'gx_1'=4,'gy_0'=8,'gy_1'=2,'gz'=4] {'gy_1'}, use_global_device_ids=true, to_apply=%region_20.21 | all-reduce | flops 11 | bytes 88 | tf_op jit(solution)/shard_map/psum | solution.py:42
  166.0 3.7 %collective-permute-start.14 = (f32[5,12,4,4]{3,2,1,0:T(4,128)S(1)}, f32[5,12,4,4]{3,2,1,0:T(4,128)S(1)}, u32[]{:S(2)}, u32[]{:S(2)}) collective-permute-start(f32[5,12,4,4]{3,2,1,0:T(4,128)S(1)} %get-tuple-element.42), channel_id=1, source_target_pairs={{0,64},{64,128},{128,192},{192,256},{256,320},{320,384},{384,448},... | collective-permute-start | bytes 11528 | tf_op jit(solution)/shard_map/ppermute | solution.py:32
  169.7 3.7 %collective-permute-start.15 = (f32[5,12,4,4]{3,2,1,0:T(4,128)S(1)}, f32[5,12,4,4]{3,2,1,0:T(4,128)S(1)}, u32[]{:S(2)}, u32[]{:S(2)}) collective-permute-start(f32[5,12,4,4]{3,2,1,0:T(4,128)S(1)} %get-tuple-element.43), channel_id=1, source_target_pairs={{64,0},{128,64},{192,128},{256,192},{320,256},{384,320},{448,384},... | collective-permute-start | bytes 11528 | tf_op jit(solution)/shard_map/ppermute | solution.py:34
  173.4 10.8 %psum.39 = f32[11]{0:T(128)S(1)} all-reduce(f32[11]{0:T(128)S(1)} %psum.38), channel_id=1, replica_groups=mesh['gx_0'=2,'gx_1'=4,'gy_0'=8,'gy_1'=2,'gz'=4] {'gz'}, use_global_device_ids=true, to_apply=%region_21.22 | all-reduce | flops 11 | bytes 88 | tf_op jit(solution)/shard_map/psum | solution.py:42
  185.0 2.9 %collective-permute-start.17 = (f32[5,12,4,16]{3,2,1,0:T(4,128)S(1)}, f32[5,12,4,16]{3,2,1,0:T(4,128)S(1)}, u32[]{:S(2)}, u32[]{:S(2)}) collective-permute-start(f32[5,12,4,16]{3,2,1,0:T(4,128)S(1)} %pad_maximum_fusion.7), channel_id=1, source_target_pairs={{4,0},{8,4},{12,8},{16,12},{20,16},{24,20},{28,24},{32,28},{36,32}... | collective-permute-start | bytes 46088 | tf_op jit(solution)/shard_map/ppermute | solution.py:34
  187.9 1.6 collective-permute-start.16
  189.5 1.2 slice_divide_fusion
  190.8 1.6 collective-permute-done.17
  193.6 0.7 add_divide_fusion
  (150 shorter events, 22.1 us)
Async XLA Ops:
  3.5 20.3 %collective-permute-start.1 = (f32[1,1,1,3,128]{3,4,2,1,0:T(8,128)S(1)}, f32[1,1,1,3,128]{3,4,2,1,0:T(8,128)S(1)}, u32[]{:S(2)}, u32[]{:S(2)}) collective-permute-start(f32[1,1,1,3,128]{3,4,2,1,0:T(8,128)S(1)} %bitcast_select_fusion.1), channel_id=1, source_target_pairs={{1,0},{2,1},{3,2},{0,3},{5,4},{6,5},{7,6},{4,7},{9,8},{10,9},{11,1... | collective-permute-start | bytes 4616 | tf_op jit(solution)/shard_map/ppermute | solution.py:34
  15.0 8.9 %collective-permute-start = (f32[1,1,1,3,128]{3,4,2,1,0:T(8,128)S(1)}, f32[1,1,1,3,128]{3,4,2,1,0:T(8,128)S(1)}, u32[]{:S(2)}, u32[]{:S(2)}) collective-permute-start(f32[1,1,1,3,128]{3,4,2,1,0:T(8,128)S(1)} %bitcast_select_fusion.1), channel_id=1, source_target_pairs={{0,1},{1,2},{2,3},{3,0},{4,5},{5,6},{6,7},{7,4},{8,9},{9,10},{10,1... | collective-permute-start | bytes 4616 | tf_op jit(solution)/shard_map/ppermute | solution.py:32
  17.0 28.1 %copy-start.2 = (f32[3,512]{1,0:T(4,128)S(1)}, f32[3,512]{1,0:T(4,128)}, u32[]{:S(2)}) copy-start(f32[3,512]{1,0:T(4,128)} %param.13) | copy-start | bytes 18436
  21.3 23.9 %copy-start.1 = (s32[3,4,8,128]{3,1,2,0:T(4,128)}, s32[3,4,8,128]{3,1,2,0:T(4,128)S(1)}, u32[]{:S(2)}) copy-start(s32[3,4,8,128]{3,1,2,0:T(4,128)S(1)} %copy.150) | copy-start | bytes 147460
  24.1 7.2 %collective-permute-start.3 = (f32[1,1,3,3,128]{4,1,3,2,0:T(1,128)S(1)}, f32[1,1,3,3,128]{4,1,3,2,0:T(1,128)S(1)}, u32[]{:S(2)}, u32[]{:S(2)}) collective-permute-start(f32[1,1,3,3,128]{4,1,3,2,0:T(1,128)S(1)} %pad_maximum_fusion.11), channel_id=1, source_target_pairs={{64,0},{128,64},{192,128},{256,192},{320,256},{384,320},{448,384},... | collective-permute-start | bytes 13832 | tf_op jit(solution)/shard_map/ppermute | solution.py:34
  29.4 6.5 %collective-permute-start.2 = (f32[1,1,3,3,128]{4,1,3,2,0:T(1,128)S(1)}, f32[1,1,3,3,128]{4,1,3,2,0:T(1,128)S(1)}, u32[]{:S(2)}, u32[]{:S(2)}) collective-permute-start(f32[1,1,3,3,128]{4,1,3,2,0:T(1,128)S(1)} %pad_maximum_fusion.11), channel_id=1, source_target_pairs={{0,64},{64,128},{128,192},{192,256},{256,320},{320,384},{384,448},... | collective-permute-start | bytes 13832 | tf_op jit(solution)/shard_map/ppermute | solution.py:32
  35.9 5.0 %collective-permute-start.5 = (f32[3,1,3,3,128]{4,1,3,2,0:T(1,128)S(1)}, f32[3,1,3,3,128]{4,1,3,2,0:T(1,128)S(1)}, u32[]{:S(2)}, u32[]{:S(2)}) collective-permute-start(f32[3,1,3,3,128]{4,1,3,2,0:T(1,128)S(1)} %pad_maximum_fusion.10), channel_id=1, source_target_pairs={{4,0},{8,4},{12,8},{16,12},{20,16},{24,20},{28,24},{32,28},{36,32}... | collective-permute-start | bytes 41480 | tf_op jit(solution)/shard_map/ppermute | solution.py:34
  38.3 2.6 %collective-permute-start.4 = (f32[3,1,3,3,128]{4,1,3,2,0:T(1,128)S(1)}, f32[3,1,3,3,128]{4,1,3,2,0:T(1,128)S(1)}, u32[]{:S(2)}, u32[]{:S(2)}) collective-permute-start(f32[3,1,3,3,128]{4,1,3,2,0:T(1,128)S(1)} %pad_maximum_fusion.10), channel_id=1, source_target_pairs={{0,4},{4,8},{8,12},{12,16},{16,20},{20,24},{24,28},{28,32},{32,36}... | collective-permute-start | bytes 41480 | tf_op jit(solution)/shard_map/ppermute | solution.py:32
  48.9 6.3 %copy-start.5 = (f32[16,8]{0,1:T(8,128)S(1)}, f32[16,8]{0,1:T(8,128)}, u32[]{:S(2)}) copy-start(f32[16,8]{0,1:T(8,128)} %param.20) | copy-start | bytes 1540
  55.1 31.2 %copy-start.6 = (f32[16]{0:T(128)S(1)}, f32[16]{0:T(128)}, u32[]{:S(2)}) copy-start(f32[16]{0:T(128)} %param.21) | copy-start | bytes 196
  56.8 13.4 %collective-permute-start.7 = (f32[1,1,1,128,128]{3,4,2,1,0:T(8,128)S(1)}, f32[1,1,1,128,128]{3,4,2,1,0:T(8,128)S(1)}, u32[]{:S(2)}, u32[]{:S(2)}) collective-permute-start(f32[1,1,1,128,128]{3,4,2,1,0:T(8,128)S(1)} %bitcast_select_fusion), channel_id=1, source_target_pairs={{1,0},{2,1},{3,2},{0,3},{5,4},{6,5},{7,6},{4,7},{9,8},{10,9},{11,1... | collective-permute-start | bytes 196616 | tf_op jit(solution)/shard_map/ppermute | solution.py:34
  62.5 7.6 %collective-permute-start.6 = (f32[1,1,1,128,128]{3,4,2,1,0:T(8,128)S(1)}, f32[1,1,1,128,128]{3,4,2,1,0:T(8,128)S(1)}, u32[]{:S(2)}, u32[]{:S(2)}) collective-permute-start(f32[1,1,1,128,128]{3,4,2,1,0:T(8,128)S(1)} %bitcast_select_fusion), channel_id=1, source_target_pairs={{0,1},{1,2},{2,3},{3,0},{4,5},{5,6},{6,7},{7,4},{8,9},{9,10},{10,1... | collective-permute-start | bytes 196616 | tf_op jit(solution)/shard_map/ppermute | solution.py:32
  70.2 6.4 %collective-permute-start.9 = (f32[1,1,3,128,128]{3,4,2,1,0:T(8,128)S(1)}, f32[1,1,3,128,128]{3,4,2,1,0:T(8,128)S(1)}, u32[]{:S(2)}, u32[]{:S(2)}) collective-permute-start(f32[1,1,3,128,128]{3,4,2,1,0:T(8,128)S(1)} %pad_maximum_fusion.4), channel_id=1, source_target_pairs={{64,0},{128,64},{192,128},{256,192},{320,256},{384,320},{448,384},... | collective-permute-start | bytes 589832 | tf_op jit(solution)/shard_map/ppermute | solution.py:34
  72.3 8.5 %collective-permute-start.8 = (f32[1,1,3,128,128]{3,4,2,1,0:T(8,128)S(1)}, f32[1,1,3,128,128]{3,4,2,1,0:T(8,128)S(1)}, u32[]{:S(2)}, u32[]{:S(2)}) collective-permute-start(f32[1,1,3,128,128]{3,4,2,1,0:T(8,128)S(1)} %pad_maximum_fusion.4), channel_id=1, source_target_pairs={{0,64},{64,128},{128,192},{192,256},{256,320},{320,384},{384,448},... | collective-permute-start | bytes 589832 | tf_op jit(solution)/shard_map/ppermute | solution.py:32
  80.9 12.6 %collective-permute-start.11 = (f32[3,1,3,128,128]{3,4,2,1,0:T(8,128)S(1)}, f32[3,1,3,128,128]{3,4,2,1,0:T(8,128)S(1)}, u32[]{:S(2)}, u32[]{:S(2)}) collective-permute-start(f32[3,1,3,128,128]{3,4,2,1,0:T(8,128)S(1)} %pad_maximum_fusion.2), channel_id=1, source_target_pairs={{4,0},{8,4},{12,8},{16,12},{20,16},{24,20},{28,24},{32,28},{36,32}... | collective-permute-start | bytes 1769480 | tf_op jit(solution)/shard_map/ppermute | solution.py:34
  86.3 7.1 %collective-permute-start.10 = (f32[3,1,3,128,128]{3,4,2,1,0:T(8,128)S(1)}, f32[3,1,3,128,128]{3,4,2,1,0:T(8,128)S(1)}, u32[]{:S(2)}, u32[]{:S(2)}) collective-permute-start(f32[3,1,3,128,128]{3,4,2,1,0:T(8,128)S(1)} %pad_maximum_fusion.2), channel_id=1, source_target_pairs={{0,4},{4,8},{8,12},{12,16},{16,20},{20,24},{24,28},{28,32},{32,36}... | collective-permute-start | bytes 1769480 | tf_op jit(solution)/shard_map/ppermute | solution.py:32
  95.1 18.9 %copy-start = (f32[16,24,512]{2,1,0:T(8,128)S(1)}, f32[16,24,512]{2,1,0:T(8,128)}, u32[]{:S(2)}) copy-start(f32[16,24,512]{2,1,0:T(8,128)} %constant_dynamic-update-slice_fusion.22) | copy-start | bytes 2359300
  121.3 7.2 %copy-start.4 = (f32[3,512]{1,0:T(4,128)S(1)}, f32[3,512]{1,0:T(4,128)}, u32[]{:S(2)}) copy-start(f32[3,512]{1,0:T(4,128)} %param.14) | copy-start | bytes 18436
  121.3 7.2 %copy-start.7 = (s32[512]{0:T(512)S(1)}, s32[512]{0:T(512)}, u32[]{:S(2)}) copy-start(s32[512]{0:T(512)} %param.19) | copy-start | bytes 6148
  122.8 72.5 %copy-start.3 = (f32[3,512]{1,0:T(4,128)}, f32[3,512]{1,0:T(4,128)S(1)}, u32[]{:S(2)}) copy-start(f32[3,512]{1,0:T(4,128)S(1)} %get-tuple-element.22) | copy-start | bytes 18436
  130.2 35.7 %collective-permute-start.13 = (f32[5,4,4,8]{3,2,1,0:T(4,128)S(1)}, f32[5,4,4,8]{3,2,1,0:T(4,128)S(1)}, u32[]{:S(2)}, u32[]{:S(2)}) collective-permute-start(f32[5,4,4,8]{3,2,1,0:T(4,128)S(1)} %constant_dynamic-update-slice_fusion.36), channel_id=1, source_target_pairs={{1,0},{2,1},{3,2},{0,3},{5,4},{6,5},{7,6},{4,7},{9,8},{10,9},{11,1... | collective-permute-start | bytes 7688 | tf_op jit(solution)/shard_map/ppermute | solution.py:34
  135.1 30.8 %collective-permute-start.12 = (f32[5,4,4,8]{3,2,1,0:T(4,128)S(1)}, f32[5,4,4,8]{3,2,1,0:T(4,128)S(1)}, u32[]{:S(2)}, u32[]{:S(2)}) collective-permute-start(f32[5,4,4,8]{3,2,1,0:T(4,128)S(1)} %constant_dynamic-update-slice_fusion.36), channel_id=1, source_target_pairs={{0,1},{1,2},{2,3},{3,0},{4,5},{5,6},{6,7},{7,4},{8,9},{9,10},{10,1... | collective-permute-start | bytes 7688 | tf_op jit(solution)/shard_map/ppermute | solution.py:32
  166.0 18.8 %collective-permute-start.14 = (f32[5,12,4,4]{3,2,1,0:T(4,128)S(1)}, f32[5,12,4,4]{3,2,1,0:T(4,128)S(1)}, u32[]{:S(2)}, u32[]{:S(2)}) collective-permute-start(f32[5,12,4,4]{3,2,1,0:T(4,128)S(1)} %get-tuple-element.42), channel_id=1, source_target_pairs={{0,64},{64,128},{128,192},{192,256},{256,320},{320,384},{384,448},... | collective-permute-start | bytes 11528 | tf_op jit(solution)/shard_map/ppermute | solution.py:32
  169.7 15.1 %collective-permute-start.15 = (f32[5,12,4,4]{3,2,1,0:T(4,128)S(1)}, f32[5,12,4,4]{3,2,1,0:T(4,128)S(1)}, u32[]{:S(2)}, u32[]{:S(2)}) collective-permute-start(f32[5,12,4,4]{3,2,1,0:T(4,128)S(1)} %get-tuple-element.43), channel_id=1, source_target_pairs={{64,0},{128,64},{192,128},{256,192},{320,256},{384,320},{448,384},... | collective-permute-start | bytes 11528 | tf_op jit(solution)/shard_map/ppermute | solution.py:34
  185.0 7.4 %collective-permute-start.17 = (f32[5,12,4,16]{3,2,1,0:T(4,128)S(1)}, f32[5,12,4,16]{3,2,1,0:T(4,128)S(1)}, u32[]{:S(2)}, u32[]{:S(2)}) collective-permute-start(f32[5,12,4,16]{3,2,1,0:T(4,128)S(1)} %pad_maximum_fusion.7), channel_id=1, source_target_pairs={{4,0},{8,4},{12,8},{16,12},{20,16},{24,20},{28,24},{32,28},{36,32}... | collective-permute-start | bytes 46088 | tf_op jit(solution)/shard_map/ppermute | solution.py:34
  187.9 4.4 %collective-permute-start.16 = (f32[5,12,4,16]{3,2,1,0:T(4,128)S(1)}, f32[5,12,4,16]{3,2,1,0:T(4,128)S(1)}, u32[]{:S(2)}, u32[]{:S(2)}) collective-permute-start(f32[5,12,4,16]{3,2,1,0:T(4,128)S(1)} %pad_maximum_fusion.7), channel_id=1, source_target_pairs={{0,4},{4,8},{8,12},{12,16},{16,20},{20,24},{24,28},{28,32},{32,36}... | collective-permute-start | bytes 46088 | tf_op jit(solution)/shard_map/ppermute | solution.py:32

commit v2 on v0

--- a/solution.py
+++ b/solution.py
@@ -22,16 +22,17 @@
 ROOT_THREE = 1.7320508
 
 
-def padded(cells, sides, width):
+def padded(cells, sides, width, open_axes=()):
     for axis, dim in sides:
         count = lax.axis_size(axis)
+        links = count if axis not in open_axes else count - 1
         head = lax.slice_in_dim(cells, 0, width, axis=dim)
         tail = lax.slice_in_dim(cells, cells.shape[dim] - width, cells.shape[dim], axis=dim)
         cells = jnp.concatenate(
             [
-                lax.ppermute(tail, axis, [(i, (i + 1) % count) for i in range(count)]),
+                lax.ppermute(tail, axis, [(i, (i + 1) % count) for i in range(links)]),
                 cells,
-                lax.ppermute(head, axis, [((i + 1) % count, i) for i in range(count)]),
+                lax.ppermute(head, axis, [((i + 1) % count, i) for i in range(links)]),
             ],
             axis=dim,
         )
@@ -53,7 +54,7 @@
     return jnp.sum(ordered, axis=0)
 
 
-def row_gather(table_rows, flat_index, chunk=1024):
+def row_gather(table_rows, flat_index, chunk=3072):
     rows, width = table_rows.shape
     total = flat_index.shape[0]
 
@@ -68,7 +69,7 @@
             stage_ref[pl.ds(first, 8), :] = jnp.concatenate(picked, axis=0)
             return carry
 
-        lax.fori_loop(0, chunk // 8, copy_rows, 0, unroll=4)
+        lax.fori_loop(0, chunk // 8, copy_rows, 0, unroll=8)
         for part in range(chunk // 128):
             out_ref[:, part * 128 : (part + 1) * 128] = stage_ref[
                 part * 128 : (part + 1) * 128, :
@@ -234,7 +235,7 @@
         [slot_ids // 9 - 1, slot_ids // 3 % 3 - 1, slot_ids % 3 - 1], axis=1
     ).astype(jnp.float32)
     ghost_sent = jnp.take(positions, ghost_list, axis=1).reshape(1, 1, 1, 3, ghosts)
-    framed = padded(ghost_sent, (("gz", 2), (GX, 0), (GY, 1)), 1)
+    framed = padded(ghost_sent, (("gz", 2), (GX, 0), (GY, 1)), 1, ("gz",))
     shifted = framed.reshape(27, 3, ghosts) + offsets[:, :, None]
     pos_table = jnp.concatenate(
         [positions, jnp.transpose(shifted, (1, 0, 2)).reshape(3, 27 * ghosts)], axis=1
@@ -246,7 +247,7 @@
     reduced = jnp.sum(radial_weight.T[:, :, None, None] * adjoint[None], axis=1)
     own_table = reduced.reshape(orders * 16, atom_slots)
     picked = jnp.take(own_table, ghost_list, axis=1).reshape(1, 1, 1, orders * 16, ghosts)
-    framed_adjoint = padded(picked, (("gz", 2), (GX, 0), (GY, 1)), 1)
+    framed_adjoint = padded(picked, (("gz", 2), (GX, 0), (GY, 1)), 1, ("gz",))
     remote = framed_adjoint.reshape(27, orders * 16, ghosts)
     table_rows = jnp.concatenate(
         [own_table.T, jnp.transpose(remote, (0, 2, 1)).reshape(27 * ghosts, orders * 16)], axis=0

time: 196 us -> 194 us (0.990)
  starting transfers between devices: 60.1 us -> 56.9 us
  blocking collectives: 43.7 us -> 46.1 us
    ppermute x18, starting transfers between devices: 60.1 us -> 56.9 us  [the longest x9 36.9 us: padded(): lax.ppermute(tail, axis, [(i, (i + 1) % count) for i in range(links)])]
    psum x5, blocking collectives: 43.7 us -> 46.1 us  [by_axis(): return functools.reduce(lax.psum, axes, shard)]
  transfers between devices with their start and end apart: 18 -> 18, of which waited for: 8 -> 10; matrix products, arithmetic and copies ran while one was open for 9% -> 9% of each run, Pallas kernels for 0% -> 0%
where the time goes in v2:
time: 194 us; the launch traced here: 193 us
  starting transfers between devices  56.9 us (29%)
  blocking collectives  46.1 us (24%)
  other arithmetic  31.2 us (16%)
  local copies, waits for them, and re-layouts  17.7 us (9%)
  Pallas kernels  17.3 us (9%)
  waiting for transfers between devices  16.8 us (9%)
  matrix products  4.84 us (2%)
  between operations  2.05 us (1%)
    psum x5, blocking collectives, by_axis(): return functools.reduce(lax.psum, axes, shard)  46.1 us
    ppermute x9, starting transfers between devices, padded(): lax.ppermute(tail, axis, [(i, (i + 1) % count) for i in range(links)])  36.9 us
    ppermute x9, starting transfers between devices, padded(): lax.ppermute(head, axis, [((i + 1) % count, i) for i in range(links)])  19.9 us
    pallas_call x1, Pallas kernels, row_gather(): pl.pallas_call(kernel, out_shape=jax.ShapeDtypeStruct((width, total), tab...  17.3 us
    unnamed x26, local copies, waits for them, and re-layouts  12.9 us
    ppermute x9, waiting for transfers between devices, padded(): lax.ppermute(head, axis, [((i + 1) % count, i) for i in range(links)])  11.1 us
    unnamed x29, other arithmetic  7.98 us
    ppermute x9, waiting for transfers between devices, padded(): lax.ppermute(tail, axis, [(i, (i + 1) % count) for i in range(links)])  5.73 us
  transfers between devices with their start and end apart: 18, of which 10 were waited for; matrix products, arithmetic and copies ran while one was open for 9% of the time, Pallas kernels for 0%

profile of v2, /device:TPU:1, one launch (start us, length us, event | category | flops | bytes accessed | tf_op | source)
XLA Modules:
  0.0 193.0 jit_solution(10858335166849149580)
XLA Ops:
  2.0 0.8 copy.102
  3.6 6.6 %collective-permute-start = (f32[1,1,1,3,128]{3,4,2,1,0:T(8,128)S(1)}, f32[1,1,1,3,128]{3,4,2,1,0:T(8,128)S(1)}, u32[]{:S(2)}, u32[]{:S(2)}) collective-permute-start(f32[1,1,1,3,128]{3,4,2,1,0:T(8,128)S(1)} %bitcast_select_fusion.1), channel_id=1, source_target_pairs={{0,1},{1,2},{2,3},{4,5},{5,6},{6,7},{8,9},{9,10},{10,11},{12,13},{... | collective-permute-start | bytes 4616 | tf_op jit(solution)/shard_map/ppermute | solution.py:33
  10.2 1.3 collective-permute-start.1
  12.2 0.8 copy.117
  14.0 0.7 fusion.268
  16.1 0.7 broadcast_multiply_fusion.4
  16.8 0.7 constant_dynamic-update-slice_fusion.39
  17.5 0.7 constant_dynamic-update-slice_fusion.38
  18.9 3.1 %collective-permute-start.2 = (f32[1,1,3,3,128]{4,1,3,2,0:T(1,128)S(1)}, f32[1,1,3,3,128]{4,1,3,2,0:T(1,128)S(1)}, u32[]{:S(2)}, u32[]{:S(2)}) collective-permute-start(f32[1,1,3,3,128]{4,1,3,2,0:T(1,128)S(1)} %pad_maximum_fusion.11), channel_id=1, source_target_pairs={{0,64},{64,128},{128,192},{192,256},{256,320},{320,384},{384,448},... | collective-permute-start | bytes 13832 | tf_op jit(solution)/shard_map/ppermute | solution.py:33
  22.1 4.6 %collective-permute-start.3 = (f32[1,1,3,3,128]{4,1,3,2,0:T(1,128)S(1)}, f32[1,1,3,3,128]{4,1,3,2,0:T(1,128)S(1)}, u32[]{:S(2)}, u32[]{:S(2)}) collective-permute-start(f32[1,1,3,3,128]{4,1,3,2,0:T(1,128)S(1)} %pad_maximum_fusion.11), channel_id=1, source_target_pairs={{64,0},{128,64},{192,128},{256,192},{320,256},{384,320},{448,384},... | collective-permute-start | bytes 13832 | tf_op jit(solution)/shard_map/ppermute | solution.py:35
  26.7 0.7 collective-permute-done.3
  27.5 5.0 %collective-permute-start.4 = (f32[3,1,3,3,128]{4,1,3,2,0:T(1,128)S(1)}, f32[3,1,3,3,128]{4,1,3,2,0:T(1,128)S(1)}, u32[]{:S(2)}, u32[]{:S(2)}) collective-permute-start(f32[3,1,3,3,128]{4,1,3,2,0:T(1,128)S(1)} %pad_maximum_fusion.10), channel_id=1, source_target_pairs={{0,4},{4,8},{8,12},{12,16},{16,20},{20,24},{24,28},{28,32},{32,36}... | collective-permute-start | bytes 41480 | tf_op jit(solution)/shard_map/ppermute | solution.py:33
  32.5 0.8 copy.101
  33.5 2.1 %collective-permute-done.5 = f32[3,1,3,3,128]{4,1,3,2,0:T(1,128)S(1)} collective-permute-done((f32[3,1,3,3,128]{4,1,3,2,0:T(1,128)S(1)}, f32[3,1,3,3,128]{4,1,3,2,0:T(1,128)S(1)}, u32[]{:S(2)}, u32[]{:S(2)}) %collective-permute-start.5) | collective-permute-done | bytes 13856 | tf_op jit(solution)/shard_map/ppermute | solution.py:35
  35.7 0.7 pad_maximum_fusion.8
  36.5 3.3 %fusion.5 = f32[3,12288]{1,0:T(4,128)S(1)} fusion(f32[3,31,128]{2,1,0:T(8,128)S(1)} %dot_general.17, s32[12288]{0:T(1024)S(1)} %get-tuple-element.45, pred[31,12288]{1,0:T(8,128)(4,1)S(1)} %iota_compare_fusion.1), kind=kOutput, calls=%fused_computation.19 | convolution fusion | flops 1759137792 | bytes 625152 | tf_op jit(solution)/shard_map/dot_general | solution.py:103
  39.8 0.7 constant_dynamic-update-slice_fusion.34
  41.2 0.8 multiply_reduce_fusion.5
  42.1 2.7 %multiply_reduce_fusion = f32[16,16,512]{2,1,0:T(8,128)S(1)} fusion(f32[16,24,512]{2,1,0:T(8,128)S(1)} %constant_dynamic-update-slice_fusion.8, f32[16,24,512]{2,1,0:T(8,128)S(1)} %broadcast_multiply_fusion), kind=kLoop, calls=%fused_computation.3 | loop fusion | flops 6160384 | bytes 2097152 | tf_op jit(solution)/shard_map/reduce_sum | solution.py:156
  45.1 3.1 %multiply_reduce_fusion.1 = (f32[16,16,512]{2,1,0:T(8,128)S(1)}, f32[16,16,512]{2,1,0:T(8,128)S(1)}) fusion(f32[16,16,16]{2,1,0:T(8,128)S(1)} %copy.111, f32[16,16,512]{2,1,0:T(8,128)S(1)} %copy.110, f32[16,16,16]{2,1,0:T(8,128)S(1)} %get-tuple-element.35), kind=kLoop, calls=%fused_computation.4 | loop fusion | flops 8126464 | bytes 1605632 | tf_op jit(solution)/shard_map/reduce_sum | solution.py:171
  49.7 5.2 %collective-permute-start.6 = (f32[1,1,1,128,128]{3,4,2,1,0:T(8,128)S(1)}, f32[1,1,1,128,128]{3,4,2,1,0:T(8,128)S(1)}, u32[]{:S(2)}, u32[]{:S(2)}) collective-permute-start(f32[1,1,1,128,128]{3,4,2,1,0:T(8,128)S(1)} %bitcast_select_fusion), channel_id=1, source_target_pairs={{0,1},{1,2},{2,3},{4,5},{5,6},{6,7},{8,9},{9,10},{10,11},{12,13},{... | collective-permute-start | bytes 196616 | tf_op jit(solution)/shard_map/ppermute | solution.py:33
  54.9 1.3 collective-permute-start.7
  61.9 0.9 collective-permute-done.7
  62.8 2.7 %collective-permute-start.8 = (f32[1,1,3,128,128]{3,4,2,1,0:T(8,128)S(1)}, f32[1,1,3,128,128]{3,4,2,1,0:T(8,128)S(1)}, u32[]{:S(2)}, u32[]{:S(2)}) collective-permute-start(f32[1,1,3,128,128]{3,4,2,1,0:T(8,128)S(1)} %pad_maximum_fusion.4), channel_id=1, source_target_pairs={{0,64},{64,128},{128,192},{192,256},{256,320},{320,384},{384,448},... | collective-permute-start | bytes 589832 | tf_op jit(solution)/shard_map/ppermute | solution.py:33
  65.6 5.3 %collective-permute-start.9 = (f32[1,1,3,128,128]{3,4,2,1,0:T(8,128)S(1)}, f32[1,1,3,128,128]{3,4,2,1,0:T(8,128)S(1)}, u32[]{:S(2)}, u32[]{:S(2)}) collective-permute-start(f32[1,1,3,128,128]{3,4,2,1,0:T(8,128)S(1)} %pad_maximum_fusion.4), channel_id=1, source_target_pairs={{64,0},{128,64},{192,128},{256,192},{320,256},{384,320},{448,384},... | collective-permute-start | bytes 589832 | tf_op jit(solution)/shard_map/ppermute | solution.py:35
  71.8 1.5 collective-permute-done.9
  73.4 3.4 %collective-permute-start.10 = (f32[3,1,3,128,128]{3,4,2,1,0:T(8,128)S(1)}, f32[3,1,3,128,128]{3,4,2,1,0:T(8,128)S(1)}, u32[]{:S(2)}, u32[]{:S(2)}) collective-permute-start(f32[3,1,3,128,128]{3,4,2,1,0:T(8,128)S(1)} %pad_maximum_fusion.2), channel_id=1, source_target_pairs={{0,4},{4,8},{8,12},{12,16},{16,20},{20,24},{24,28},{28,32},{32,36}... | collective-permute-start | bytes 1769480 | tf_op jit(solution)/shard_map/ppermute | solution.py:33
  78.8 4.8 %collective-permute-done.10 = f32[3,1,3,128,128]{3,4,2,1,0:T(8,128)S(1)} collective-permute-done((f32[3,1,3,128,128]{3,4,2,1,0:T(8,128)S(1)}, f32[3,1,3,128,128]{3,4,2,1,0:T(8,128)S(1)}, u32[]{:S(2)}, u32[]{:S(2)}) %collective-permute-start.10) | collective-permute-done | bytes 589856 | tf_op jit(solution)/shard_map/ppermute | solution.py:33
  83.6 2.8 %collective-permute-done.11 = f32[3,1,3,128,128]{3,4,2,1,0:T(8,128)S(1)} collective-permute-done((f32[3,1,3,128,128]{3,4,2,1,0:T(8,128)S(1)}, f32[3,1,3,128,128]{3,4,2,1,0:T(8,128)S(1)}, u32[]{:S(2)}, u32[]{:S(2)}) %collective-permute-start.11) | collective-permute-done | bytes 589856 | tf_op jit(solution)/shard_map/ppermute | solution.py:35
  86.5 1.5 pad_maximum_fusion.table_ref
  88.0 17.3 %shard_map.156 = f32[128,12288]{1,0:T(8,128)} custom-call(s32[12288]{0:T(1024)} %bitcast.277, f32[3968,128]{1,0:T(8,128)} %pad_maximum_fusion.table_ref), custom_call_target="tpu_custom_call" | custom-call | bytes 14614528 | tf_op jit(solution)/shard_map/pallas_call | solution.py:78
  105.3 7.7 %copy.119 = f32[16,8,24,512]{3,2,1,0:T(8,128)S(1)} copy(f32[16,8,24,512]{3,1,2,0:T(8,128)} %bitcast.270) | data formatting | bytes 12582912
  113.0 2.3 %fusion.1 = (f32[8,24,512]{2,1,0:T(8,128)S(1)}, f32[16,24,512]{2,1,0:T(8,128)S(1)}, f32[16,24,512]{2,1,0:T(8,128)S(1)}, f32[8,24,512]{2,1,0:T(8,128)S(1)}) fusion(f32[16,24,512]{2,1,0:T(8,128)S(1)} %copy-done, f32[8,24,512]{2,1,0:T(8,128)S(1)} %broadcast_multiply_fusion.3, f32[8,16,512]{2,1,0:T(8,128)S(1)} %multiply_reduce_fusion.6, ...), kind=kLoop, calls=%fused_computation.9 | loop fusion | flops 11993088 | bytes 10878976 | tf_op jit(solution)/shard_map/transpose(jvp())/reduce_sum | solution.py:149
  116.5 1.0 convolution_bitcast_fusion
  117.7 0.7 pad_maximum_fusion.12
  118.4 4.9 %psum.35 = f32[11]{0:T(128)S(1)} all-reduce(f32[11]{0:T(128)S(1)} %pad_maximum_fusion.12), channel_id=1, replica_groups=mesh['gx_0'=2,'gx_1'=4,'gy_0'=8,'gy_1'=2,'gz'=4] {'gx_0'}, use_global_device_ids=true, to_apply=%region_17.18 | all-reduce | flops 11 | bytes 88 | tf_op jit(solution)/shard_map/psum | solution.py:43
  125.0 5.8 %collective-permute-start.12 = (f32[5,4,4,8]{3,2,1,0:T(4,128)S(1)}, f32[5,4,4,8]{3,2,1,0:T(4,128)S(1)}, u32[]{:S(2)}, u32[]{:S(2)}) collective-permute-start(f32[5,4,4,8]{3,2,1,0:T(4,128)S(1)} %constant_dynamic-update-slice_fusion.36), channel_id=1, source_target_pairs={{0,1},{1,2},{2,3},{3,0},{4,5},{5,6},{6,7},{7,4},{8,9},{9,10},{10,1... | collective-permute-start | bytes 7688 | tf_op jit(solution)/shard_map/ppermute | solution.py:33
  130.8 1.9 collective-permute-start.13
  132.8 10.2 %psum.36 = f32[11]{0:T(128)S(1)} all-reduce(f32[11]{0:T(128)S(1)} %psum.35), channel_id=1, replica_groups=mesh['gx_0'=2,'gx_1'=4,'gy_0'=8,'gy_1'=2,'gz'=4] {'gx_1'}, use_global_device_ids=true, to_apply=%region_18.19 | all-reduce | flops 11 | bytes 88 | tf_op jit(solution)/shard_map/psum | solution.py:43
  143.0 14.1 %psum.37 = f32[11]{0:T(128)S(1)} all-reduce(f32[11]{0:T(128)S(1)} %psum.36), channel_id=1, replica_groups=mesh['gx_0'=2,'gx_1'=4,'gy_0'=8,'gy_1'=2,'gz'=4] {'gy_0'}, use_global_device_ids=true, to_apply=%region_19.20 | all-reduce | flops 11 | bytes 88 | tf_op jit(solution)/shard_map/psum | solution.py:43
  157.1 8.0 %psum.38 = f32[11]{0:T(128)S(1)} all-reduce(f32[11]{0:T(128)S(1)} %psum.37), channel_id=1, replica_groups=mesh['gx_0'=2,'gx_1'=4,'gy_0'=8,'gy_1'=2,'gz'=4] {'gy_1'}, use_global_device_ids=true, to_apply=%region_20.21 | all-reduce | flops 11 | bytes 88 | tf_op jit(solution)/shard_map/psum | solution.py:43
  165.2 1.9 collective-permute-start.14
  167.2 5.5 %collective-permute-start.15 = (f32[5,12,4,4]{3,2,1,0:T(4,128)S(1)}, f32[5,12,4,4]{3,2,1,0:T(4,128)S(1)}, u32[]{:S(2)}, u32[]{:S(2)}) collective-permute-start(f32[5,12,4,4]{3,2,1,0:T(4,128)S(1)} %get-tuple-element.41), channel_id=1, source_target_pairs={{64,0},{128,64},{192,128},{256,192},{320,256},{384,320},{448,384},... | collective-permute-start | bytes 11528 | tf_op jit(solution)/shard_map/ppermute | solution.py:35
  172.7 8.9 %psum.39 = f32[11]{0:T(128)S(1)} all-reduce(f32[11]{0:T(128)S(1)} %psum.38), channel_id=1, replica_groups=mesh['gx_0'=2,'gx_1'=4,'gy_0'=8,'gy_1'=2,'gz'=4] {'gz'}, use_global_device_ids=true, to_apply=%region_21.22 | all-reduce | flops 11 | bytes 88 | tf_op jit(solution)/shard_map/psum | solution.py:43
  182.4 3.1 %collective-permute-start.16 = (f32[5,12,4,16]{3,2,1,0:T(4,128)S(1)}, f32[5,12,4,16]{3,2,1,0:T(4,128)S(1)}, u32[]{:S(2)}, u32[]{:S(2)}) collective-permute-start(f32[5,12,4,16]{3,2,1,0:T(4,128)S(1)} %pad_maximum_fusion.7), channel_id=1, source_target_pairs={{0,4},{4,8},{8,12},{12,16},{16,20},{20,24},{24,28},{28,32},{32,36}... | collective-permute-start | bytes 46088 | tf_op jit(solution)/shard_map/ppermute | solution.py:33
  185.4 1.2 slice_divide_fusion
  187.3 2.7 %collective-permute-done.17 = f32[5,12,4,16]{3,2,1,0:T(4,128)S(1)} collective-permute-done((f32[5,12,4,16]{3,2,1,0:T(4,128)S(1)}, f32[5,12,4,16]{3,2,1,0:T(4,128)S(1)}, u32[]{:S(2)}, u32[]{:S(2)}) %collective-permute-start.17) | collective-permute-done | bytes 15392 | tf_op jit(solution)/shard_map/ppermute | solution.py:35
  191.3 0.7 add_divide_fusion
  (149 shorter events, 23.4 us)
Async XLA Ops:
  0.6 39.1 %copy-start.2 = (f32[3,512]{1,0:T(4,128)S(1)}, f32[3,512]{1,0:T(4,128)}, u32[]{:S(2)}) copy-start(f32[3,512]{1,0:T(4,128)} %param.13) | copy-start | bytes 18436
  3.6 14.8 %collective-permute-start = (f32[1,1,1,3,128]{3,4,2,1,0:T(8,128)S(1)}, f32[1,1,1,3,128]{3,4,2,1,0:T(8,128)S(1)}, u32[]{:S(2)}, u32[]{:S(2)}) collective-permute-start(f32[1,1,1,3,128]{3,4,2,1,0:T(8,128)S(1)} %bitcast_select_fusion.1), channel_id=1, source_target_pairs={{0,1},{1,2},{2,3},{4,5},{5,6},{6,7},{8,9},{9,10},{10,11},{12,13},{... | collective-permute-start | bytes 4616 | tf_op jit(solution)/shard_map/ppermute | solution.py:33
  10.2 8.7 %collective-permute-start.1 = (f32[1,1,1,3,128]{3,4,2,1,0:T(8,128)S(1)}, f32[1,1,1,3,128]{3,4,2,1,0:T(8,128)S(1)}, u32[]{:S(2)}, u32[]{:S(2)}) collective-permute-start(f32[1,1,1,3,128]{3,4,2,1,0:T(8,128)S(1)} %bitcast_select_fusion.1), channel_id=1, source_target_pairs={{1,0},{2,1},{3,2},{5,4},{6,5},{7,6},{9,8},{10,9},{11,10},{13,12},{... | collective-permute-start | bytes 4616 | tf_op jit(solution)/shard_map/ppermute | solution.py:35
  13.0 27.6 %copy-start.1 = (s32[3,4,8,128]{3,1,2,0:T(4,128)}, s32[3,4,8,128]{3,1,2,0:T(4,128)S(1)}, u32[]{:S(2)}) copy-start(s32[3,4,8,128]{3,1,2,0:T(4,128)S(1)} %copy.117) | copy-start | bytes 147460
  18.9 7.8 %collective-permute-start.2 = (f32[1,1,3,3,128]{4,1,3,2,0:T(1,128)S(1)}, f32[1,1,3,3,128]{4,1,3,2,0:T(1,128)S(1)}, u32[]{:S(2)}, u32[]{:S(2)}) collective-permute-start(f32[1,1,3,3,128]{4,1,3,2,0:T(1,128)S(1)} %pad_maximum_fusion.11), channel_id=1, source_target_pairs={{0,64},{64,128},{128,192},{192,256},{256,320},{320,384},{384,448},... | collective-permute-start | bytes 13832 | tf_op jit(solution)/shard_map/ppermute | solution.py:33
  22.1 5.4 %collective-permute-start.3 = (f32[1,1,3,3,128]{4,1,3,2,0:T(1,128)S(1)}, f32[1,1,3,3,128]{4,1,3,2,0:T(1,128)S(1)}, u32[]{:S(2)}, u32[]{:S(2)}) collective-permute-start(f32[1,1,3,3,128]{4,1,3,2,0:T(1,128)S(1)} %pad_maximum_fusion.11), channel_id=1, source_target_pairs={{64,0},{128,64},{192,128},{256,192},{320,256},{384,320},{448,384},... | collective-permute-start | bytes 13832 | tf_op jit(solution)/shard_map/ppermute | solution.py:35
  27.5 6.0 %collective-permute-start.4 = (f32[3,1,3,3,128]{4,1,3,2,0:T(1,128)S(1)}, f32[3,1,3,3,128]{4,1,3,2,0:T(1,128)S(1)}, u32[]{:S(2)}, u32[]{:S(2)}) collective-permute-start(f32[3,1,3,3,128]{4,1,3,2,0:T(1,128)S(1)} %pad_maximum_fusion.10), channel_id=1, source_target_pairs={{0,4},{4,8},{8,12},{12,16},{16,20},{20,24},{24,28},{28,32},{32,36}... | collective-permute-start | bytes 41480 | tf_op jit(solution)/shard_map/ppermute | solution.py:33
  32.4 3.1 %collective-permute-start.5 = (f32[3,1,3,3,128]{4,1,3,2,0:T(1,128)S(1)}, f32[3,1,3,3,128]{4,1,3,2,0:T(1,128)S(1)}, u32[]{:S(2)}, u32[]{:S(2)}) collective-permute-start(f32[3,1,3,3,128]{4,1,3,2,0:T(1,128)S(1)} %pad_maximum_fusion.10), channel_id=1, source_target_pairs={{4,0},{8,4},{12,8},{16,12},{20,16},{24,20},{28,24},{32,28},{36,32}... | collective-permute-start | bytes 41480 | tf_op jit(solution)/shard_map/ppermute | solution.py:35
  41.2 7.1 %copy-start.5 = (f32[16,8]{0,1:T(8,128)S(1)}, f32[16,8]{0,1:T(8,128)}, u32[]{:S(2)}) copy-start(f32[16,8]{0,1:T(8,128)} %param.20) | copy-start | bytes 1540
  45.1 31.7 %copy-start.6 = (f32[16]{0:T(128)S(1)}, f32[16]{0:T(128)}, u32[]{:S(2)}) copy-start(f32[16]{0:T(128)} %param.21) | copy-start | bytes 196
  49.7 12.2 %collective-permute-start.6 = (f32[1,1,1,128,128]{3,4,2,1,0:T(8,128)S(1)}, f32[1,1,1,128,128]{3,4,2,1,0:T(8,128)S(1)}, u32[]{:S(2)}, u32[]{:S(2)}) collective-permute-start(f32[1,1,1,128,128]{3,4,2,1,0:T(8,128)S(1)} %bitcast_select_fusion), channel_id=1, source_target_pairs={{0,1},{1,2},{2,3},{4,5},{5,6},{6,7},{8,9},{9,10},{10,11},{12,13},{... | collective-permute-start | bytes 196616 | tf_op jit(solution)/shard_map/ppermute | solution.py:33
  54.9 7.9 %collective-permute-start.7 = (f32[1,1,1,128,128]{3,4,2,1,0:T(8,128)S(1)}, f32[1,1,1,128,128]{3,4,2,1,0:T(8,128)S(1)}, u32[]{:S(2)}, u32[]{:S(2)}) collective-permute-start(f32[1,1,1,128,128]{3,4,2,1,0:T(8,128)S(1)} %bitcast_select_fusion), channel_id=1, source_target_pairs={{1,0},{2,1},{3,2},{5,4},{6,5},{7,6},{9,8},{10,9},{11,10},{13,12},{... | collective-permute-start | bytes 196616 | tf_op jit(solution)/shard_map/ppermute | solution.py:35
  62.8 9.0 %collective-permute-start.8 = (f32[1,1,3,128,128]{3,4,2,1,0:T(8,128)S(1)}, f32[1,1,3,128,128]{3,4,2,1,0:T(8,128)S(1)}, u32[]{:S(2)}, u32[]{:S(2)}) collective-permute-start(f32[1,1,3,128,128]{3,4,2,1,0:T(8,128)S(1)} %pad_maximum_fusion.4), channel_id=1, source_target_pairs={{0,64},{64,128},{128,192},{192,256},{256,320},{320,384},{384,448},... | collective-permute-start | bytes 589832 | tf_op jit(solution)/shard_map/ppermute | solution.py:33
  65.6 7.8 %collective-permute-start.9 = (f32[1,1,3,128,128]{3,4,2,1,0:T(8,128)S(1)}, f32[1,1,3,128,128]{3,4,2,1,0:T(8,128)S(1)}, u32[]{:S(2)}, u32[]{:S(2)}) collective-permute-start(f32[1,1,3,128,128]{3,4,2,1,0:T(8,128)S(1)} %pad_maximum_fusion.4), channel_id=1, source_target_pairs={{64,0},{128,64},{192,128},{256,192},{320,256},{384,320},{448,384},... | collective-permute-start | bytes 589832 | tf_op jit(solution)/shard_map/ppermute | solution.py:35
  73.4 10.2 %collective-permute-start.10 = (f32[3,1,3,128,128]{3,4,2,1,0:T(8,128)S(1)}, f32[3,1,3,128,128]{3,4,2,1,0:T(8,128)S(1)}, u32[]{:S(2)}, u32[]{:S(2)}) collective-permute-start(f32[3,1,3,128,128]{3,4,2,1,0:T(8,128)S(1)} %pad_maximum_fusion.2), channel_id=1, source_target_pairs={{0,4},{4,8},{8,12},{12,16},{16,20},{20,24},{24,28},{28,32},{32,36}... | collective-permute-start | bytes 1769480 | tf_op jit(solution)/shard_map/ppermute | solution.py:33
  76.8 9.6 %collective-permute-start.11 = (f32[3,1,3,128,128]{3,4,2,1,0:T(8,128)S(1)}, f32[3,1,3,128,128]{3,4,2,1,0:T(8,128)S(1)}, u32[]{:S(2)}, u32[]{:S(2)}) collective-permute-start(f32[3,1,3,128,128]{3,4,2,1,0:T(8,128)S(1)} %pad_maximum_fusion.2), channel_id=1, source_target_pairs={{4,0},{8,4},{12,8},{16,12},{20,16},{24,20},{28,24},{32,28},{36,32}... | collective-permute-start | bytes 1769480 | tf_op jit(solution)/shard_map/ppermute | solution.py:35
  105.3 7.7 %copy-start = (f32[16,24,512]{2,1,0:T(8,128)S(1)}, f32[16,24,512]{2,1,0:T(8,128)}, u32[]{:S(2)}) copy-start(f32[16,24,512]{2,1,0:T(8,128)} %constant_dynamic-update-slice_fusion.22) | copy-start | bytes 2359300
  115.3 8.0 %copy-start.4 = (f32[3,512]{1,0:T(4,128)S(1)}, f32[3,512]{1,0:T(4,128)}, u32[]{:S(2)}) copy-start(f32[3,512]{1,0:T(4,128)} %param.14) | copy-start | bytes 18436
  115.3 8.0 %copy-start.7 = (s32[512]{0:T(512)S(1)}, s32[512]{0:T(512)}, u32[]{:S(2)}) copy-start(s32[512]{0:T(512)} %param.19) | copy-start | bytes 6148
  116.5 76.4 %copy-start.3 = (f32[3,512]{1,0:T(4,128)}, f32[3,512]{1,0:T(4,128)S(1)}, u32[]{:S(2)}) copy-start(f32[3,512]{1,0:T(4,128)S(1)} %get-tuple-element.22) | copy-start | bytes 18436
  125.0 40.1 %collective-permute-start.12 = (f32[5,4,4,8]{3,2,1,0:T(4,128)S(1)}, f32[5,4,4,8]{3,2,1,0:T(4,128)S(1)}, u32[]{:S(2)}, u32[]{:S(2)}) collective-permute-start(f32[5,4,4,8]{3,2,1,0:T(4,128)S(1)} %constant_dynamic-update-slice_fusion.36), channel_id=1, source_target_pairs={{0,1},{1,2},{2,3},{3,0},{4,5},{5,6},{6,7},{7,4},{8,9},{9,10},{10,1... | collective-permute-start | bytes 7688 | tf_op jit(solution)/shard_map/ppermute | solution.py:33
  130.8 34.2 %collective-permute-start.13 = (f32[5,4,4,8]{3,2,1,0:T(4,128)S(1)}, f32[5,4,4,8]{3,2,1,0:T(4,128)S(1)}, u32[]{:S(2)}, u32[]{:S(2)}) collective-permute-start(f32[5,4,4,8]{3,2,1,0:T(4,128)S(1)} %constant_dynamic-update-slice_fusion.36), channel_id=1, source_target_pairs={{1,0},{2,1},{3,2},{0,3},{5,4},{6,5},{7,6},{4,7},{9,8},{10,9},{11,1... | collective-permute-start | bytes 7688 | tf_op jit(solution)/shard_map/ppermute | solution.py:35
  165.2 16.9 %collective-permute-start.14 = (f32[5,12,4,4]{3,2,1,0:T(4,128)S(1)}, f32[5,12,4,4]{3,2,1,0:T(4,128)S(1)}, u32[]{:S(2)}, u32[]{:S(2)}) collective-permute-start(f32[5,12,4,4]{3,2,1,0:T(4,128)S(1)} %get-tuple-element.40), channel_id=1, source_target_pairs={{0,64},{64,128},{128,192},{192,256},{256,320},{320,384},{384,448},... | collective-permute-start | bytes 11528 | tf_op jit(solution)/shard_map/ppermute | solution.py:33
  167.2 15.0 %collective-permute-start.15 = (f32[5,12,4,4]{3,2,1,0:T(4,128)S(1)}, f32[5,12,4,4]{3,2,1,0:T(4,128)S(1)}, u32[]{:S(2)}, u32[]{:S(2)}) collective-permute-start(f32[5,12,4,4]{3,2,1,0:T(4,128)S(1)} %get-tuple-element.41), channel_id=1, source_target_pairs={{64,0},{128,64},{192,128},{256,192},{320,256},{384,320},{448,384},... | collective-permute-start | bytes 11528 | tf_op jit(solution)/shard_map/ppermute | solution.py:35
  182.4 4.9 %collective-permute-start.16 = (f32[5,12,4,16]{3,2,1,0:T(4,128)S(1)}, f32[5,12,4,16]{3,2,1,0:T(4,128)S(1)}, u32[]{:S(2)}, u32[]{:S(2)}) collective-permute-start(f32[5,12,4,16]{3,2,1,0:T(4,128)S(1)} %pad_maximum_fusion.7), channel_id=1, source_target_pairs={{0,4},{4,8},{8,12},{12,16},{16,20},{20,24},{24,28},{28,32},{32,36}... | collective-permute-start | bytes 46088 | tf_op jit(solution)/shard_map/ppermute | solution.py:33
  185.4 4.6 %collective-permute-start.17 = (f32[5,12,4,16]{3,2,1,0:T(4,128)S(1)}, f32[5,12,4,16]{3,2,1,0:T(4,128)S(1)}, u32[]{:S(2)}, u32[]{:S(2)}) collective-permute-start(f32[5,12,4,16]{3,2,1,0:T(4,128)S(1)} %pad_maximum_fusion.7), channel_id=1, source_target_pairs={{4,0},{8,4},{12,8},{16,12},{20,16},{24,20},{28,24},{32,28},{36,32}... | collective-permute-start | bytes 46088 | tf_op jit(solution)/shard_map/ppermute | solution.py:35

commit v3 on v2

--- a/solution.py
+++ b/solution.py
@@ -145,8 +145,8 @@
 
 
 def pair_energy(vector, weights):
-    basis = radial(vector, weights.shape[0])
-    mixed = jnp.sum(weights * basis[:, None], axis=0)
+    basis = radial(vector, weights.shape[1])
+    mixed = jnp.sum(weights * basis[None], axis=1)
     return jnp.sum(mixed * harmonics(vector), axis=0)
 
 
@@ -245,7 +245,7 @@
     basis_sum = atom_basis(separation, pair_mask, radial_weight)
     energy, adjoint = adjoints(basis_sum, linear_weight, pair_coupling)
     reduced = jnp.sum(radial_weight.T[:, :, None, None] * adjoint[None], axis=1)
-    own_table = reduced.reshape(orders * 16, atom_slots)
+    own_table = jnp.transpose(reduced, (1, 0, 2)).reshape(16 * orders, atom_slots)
     picked = jnp.take(own_table, ghost_list, axis=1).reshape(1, 1, 1, orders * 16, ghosts)
     framed_adjoint = padded(picked, (("gz", 2), (GX, 0), (GY, 1)), 1, ("gz",))
     remote = framed_adjoint.reshape(27, orders * 16, ghosts)
@@ -253,10 +253,10 @@
         [own_table.T, jnp.transpose(remote, (0, 2, 1)).reshape(27 * ghosts, orders * 16)], axis=0
     )
     other_weights = row_gather(table_rows, neighbour_index.reshape(-1)).reshape(
-        orders, 16, neigh_depth, atom_slots
+        16, orders, neigh_depth, atom_slots
     )
     forces, virial = pair_forces(
-        separation, pair_mask, own_table.reshape(orders, 16, 1, atom_slots), other_weights
+        separation, pair_mask, own_table.reshape(16, orders, 1, atom_slots), other_weights
     )
     kicked = velocities + KICK * forces
     grid_shape = electron_temp.shape

time: 194 us -> 191 us (0.985)
  local copies, waits for them, and re-layouts: 17.7 us -> 10.4 us
  other arithmetic: 31.2 us -> 38.1 us
  blocking collectives: 46.1 us -> 43.3 us
    ppermute x9, starting transfers between devices: 19.9 us -> 28.6 us  [padded(): lax.ppermute(head, axis, [((i + 1) % count, i) for i in range(links)])]
    ppermute x9, starting transfers between devices: 36.9 us -> 28.9 us  [padded(): lax.ppermute(tail, axis, [(i, (i + 1) % count) for i in range(links)])]
    unnamed x26 -> x25, local copies, waits for them, and re-layouts: 12.9 us -> 5.19 us
    reduce_sum x1, other arithmetic: 2.3 us -> 7.34 us  [pair_energy(): mixed = jnp.sum(weights * basis[None], axis=1)]
    ppermute x9, waiting for transfers between devices: 11.1 us -> 7.85 us  [padded(): lax.ppermute(head, axis, [((i + 1) % count, i) for i in range(links)])]
    ppermute x9, waiting for transfers between devices: 5.73 us -> 8.75 us  [padded(): lax.ppermute(tail, axis, [(i, (i + 1) % count) for i in range(links)])]
    psum x5, blocking collectives: 46.1 us -> 43.3 us  [by_axis(): return functools.reduce(lax.psum, axes, shard)]
  transfers between devices with their start and end apart: 18 -> 18, of which waited for: 10 -> 6; matrix products, arithmetic and copies ran while one was open for 9% -> 9% of each run, Pallas kernels for 0% -> 0%
where the time goes in v3:
time: 191 us; the launch traced here: 190 us
  starting transfers between devices  57.5 us (30%)
  blocking collectives  43.3 us (23%)
  other arithmetic  38.1 us (20%)
  Pallas kernels  17.4 us (9%)
  waiting for transfers between devices  16.6 us (9%)
  local copies, waits for them, and re-layouts  10.4 us (5%)
  matrix products  4.84 us (3%)
  between operations  2.07 us (1%)
    psum x5, blocking collectives, by_axis(): return functools.reduce(lax.psum, axes, shard)  43.3 us
    ppermute x9, starting transfers between devices, padded(): lax.ppermute(tail, axis, [(i, (i + 1) % count) for i in range(links)])  28.9 us
    ppermute x9, starting transfers between devices, padded(): lax.ppermute(head, axis, [((i + 1) % count, i) for i in range(links)])  28.6 us
    pallas_call x1, Pallas kernels, row_gather(): pl.pallas_call(kernel, out_shape=jax.ShapeDtypeStruct((width, total), tab...  17.4 us
    ppermute x9, waiting for transfers between devices, padded(): lax.ppermute(tail, axis, [(i, (i + 1) % count) for i in range(links)])  8.75 us
    unnamed x29, other arithmetic  7.98 us
    ppermute x9, waiting for transfers between devices, padded(): lax.ppermute(head, axis, [((i + 1) % count, i) for i in range(links)])  7.85 us
    reduce_sum x1, other arithmetic, pair_energy(): mixed = jnp.sum(weights * basis[None], axis=1)  7.34 us
  transfers between devices with their start and end apart: 18, of which 6 were waited for; matrix products, arithmetic and copies ran while one was open for 9% of the time, Pallas kernels for 0%

profile of v3, /device:TPU:1, one launch (start us, length us, event | category | flops | bytes accessed | tf_op | source)
XLA Modules:
  0.0 190.2 jit_solution(9074197581927180658)
XLA Ops:
  2.0 0.8 copy.128
  3.5 1.3 collective-permute-start.1
  4.8 7.3 %collective-permute-start = (f32[1,1,1,3,128]{3,4,2,1,0:T(8,128)S(1)}, f32[1,1,1,3,128]{3,4,2,1,0:T(8,128)S(1)}, u32[]{:S(2)}, u32[]{:S(2)}) collective-permute-start(f32[1,1,1,3,128]{3,4,2,1,0:T(8,128)S(1)} %bitcast_select_fusion.1), channel_id=1, source_target_pairs={{0,1},{1,2},{2,3},{4,5},{5,6},{6,7},{8,9},{9,10},{10,11},{12,13},{... | collective-permute-start | bytes 4616 | tf_op jit(solution)/shard_map/ppermute | solution.py:33
  13.5 0.8 fusion.267
  14.2 0.7 constant_dynamic-update-slice_fusion.40
  14.9 0.7 fusion.167
  15.6 0.8 copy.150
  16.7 0.7 broadcast_multiply_fusion.2
  17.4 0.7 constant_dynamic-update-slice_fusion.39
  18.2 0.7 constant_dynamic-update-slice_fusion.38
  19.2 6.2 %collective-permute-start.3 = (f32[1,1,3,3,128]{4,1,3,2,0:T(1,128)S(1)}, f32[1,1,3,3,128]{4,1,3,2,0:T(1,128)S(1)}, u32[]{:S(2)}, u32[]{:S(2)}) collective-permute-start(f32[1,1,3,3,128]{4,1,3,2,0:T(1,128)S(1)} %pad_maximum_fusion.11), channel_id=1, source_target_pairs={{64,0},{128,64},{192,128},{256,192},{320,256},{384,320},{448,384},... | collective-permute-start | bytes 13832 | tf_op jit(solution)/shard_map/ppermute | solution.py:35
  25.4 1.9 %collective-permute-start.2 = (f32[1,1,3,3,128]{4,1,3,2,0:T(1,128)S(1)}, f32[1,1,3,3,128]{4,1,3,2,0:T(1,128)S(1)}, u32[]{:S(2)}, u32[]{:S(2)}) collective-permute-start(f32[1,1,3,3,128]{4,1,3,2,0:T(1,128)S(1)} %pad_maximum_fusion.11), channel_id=1, source_target_pairs={{0,64},{64,128},{128,192},{192,256},{256,320},{320,384},{384,448},... | collective-permute-start | bytes 13832 | tf_op jit(solution)/shard_map/ppermute | solution.py:33
  27.4 4.5 %collective-permute-done.2 = f32[1,1,3,3,128]{4,1,3,2,0:T(1,128)S(1)} collective-permute-done((f32[1,1,3,3,128]{4,1,3,2,0:T(1,128)S(1)}, f32[1,1,3,3,128]{4,1,3,2,0:T(1,128)S(1)}, u32[]{:S(2)}, u32[]{:S(2)}) %collective-permute-start.2) | collective-permute-done | bytes 4640 | tf_op jit(solution)/shard_map/ppermute | solution.py:33
  31.9 2.4 %collective-permute-start.5 = (f32[3,1,3,3,128]{4,1,3,2,0:T(1,128)S(1)}, f32[3,1,3,3,128]{4,1,3,2,0:T(1,128)S(1)}, u32[]{:S(2)}, u32[]{:S(2)}) collective-permute-start(f32[3,1,3,3,128]{4,1,3,2,0:T(1,128)S(1)} %pad_maximum_fusion.10), channel_id=1, source_target_pairs={{4,0},{8,4},{12,8},{16,12},{20,16},{24,20},{28,24},{32,28},{36,32}... | collective-permute-start | bytes 41480 | tf_op jit(solution)/shard_map/ppermute | solution.py:35
  34.3 1.2 collective-permute-start.4
  35.5 0.8 copy.127
  37.0 0.7 pad_maximum_fusion.8
  37.8 3.3 %fusion.3 = f32[3,12288]{1,0:T(4,128)S(1)} fusion(f32[3,31,128]{2,1,0:T(8,128)S(1)} %dot_general.17, s32[12288]{0:T(1024)S(1)} %get-tuple-element.47, pred[31,12288]{1,0:T(8,128)(4,1)S(1)} %iota_compare_fusion.1), kind=kOutput, calls=%fused_computation.17 | convolution fusion | flops 1759137792 | bytes 625152 | tf_op jit(solution)/shard_map/dot_general | solution.py:103
  41.2 0.7 constant_dynamic-update-slice_fusion.34
  42.7 2.2 %multiply_reduce_fusion.7 = f32[16,24,512]{2,1,0:T(8,128)S(1)} fusion(f32[8,24,512]{2,0,1:T(8,128)S(1)} %copy.136, f32[16,8]{1,0:T(8,128)S(1)} %copy.127), kind=kLoop, calls=%fused_computation.10 | loop fusion | flops 2949120 | bytes 1180160 | tf_op jit(solution)/shard_map/reduce_sum | solution.py:155
  45.1 2.7 %multiply_reduce_fusion = f32[16,16,512]{2,1,0:T(8,128)S(1)} fusion(f32[16,24,512]{2,1,0:T(8,128)S(1)} %constant_dynamic-update-slice_fusion.8, f32[16,24,512]{2,1,0:T(8,128)S(1)} %broadcast_multiply_fusion), kind=kLoop, calls=%fused_computation.3 | loop fusion | flops 6160384 | bytes 2097152 | tf_op jit(solution)/shard_map/reduce_sum | solution.py:156
  48.1 3.1 %multiply_reduce_fusion.1 = (f32[16,16,512]{2,1,0:T(8,128)S(1)}, f32[16,16,512]{2,1,0:T(8,128)S(1)}) fusion(f32[16,16,16]{2,1,0:T(8,128)S(1)} %copy.138, f32[16,16,512]{2,1,0:T(8,128)S(1)} %copy.137, f32[16,16,16]{2,1,0:T(8,128)S(1)} %get-tuple-element.37), kind=kLoop, calls=%fused_computation.4 | loop fusion | flops 8126464 | bytes 1605632 | tf_op jit(solution)/shard_map/reduce_sum | solution.py:171
  52.8 1.3 collective-permute-start.7
  54.1 6.8 %collective-permute-start.6 = (f32[1,1,1,128,128]{3,4,2,1,0:T(8,128)S(1)}, f32[1,1,1,128,128]{3,4,2,1,0:T(8,128)S(1)}, u32[]{:S(2)}, u32[]{:S(2)}) collective-permute-start(f32[1,1,1,128,128]{3,4,2,1,0:T(8,128)S(1)} %bitcast_select_fusion), channel_id=1, source_target_pairs={{0,1},{1,2},{2,3},{4,5},{5,6},{6,7},{8,9},{9,10},{10,11},{12,13},{... | collective-permute-start | bytes 196616 | tf_op jit(solution)/shard_map/ppermute | solution.py:33
  66.6 2.1 %collective-permute-start.9 = (f32[1,1,3,128,128]{3,4,2,1,0:T(8,128)S(1)}, f32[1,1,3,128,128]{3,4,2,1,0:T(8,128)S(1)}, u32[]{:S(2)}, u32[]{:S(2)}) collective-permute-start(f32[1,1,3,128,128]{3,4,2,1,0:T(8,128)S(1)} %pad_maximum_fusion.4), channel_id=1, source_target_pairs={{64,0},{128,64},{192,128},{256,192},{320,256},{384,320},{448,384},... | collective-permute-start | bytes 589832 | tf_op jit(solution)/shard_map/ppermute | solution.py:35
  68.7 3.4 %collective-permute-start.8 = (f32[1,1,3,128,128]{3,4,2,1,0:T(8,128)S(1)}, f32[1,1,3,128,128]{3,4,2,1,0:T(8,128)S(1)}, u32[]{:S(2)}, u32[]{:S(2)}) collective-permute-start(f32[1,1,3,128,128]{3,4,2,1,0:T(8,128)S(1)} %pad_maximum_fusion.4), channel_id=1, source_target_pairs={{0,64},{64,128},{128,192},{192,256},{256,320},{320,384},{384,448},... | collective-permute-start | bytes 589832 | tf_op jit(solution)/shard_map/ppermute | solution.py:33
  73.0 4.2 %collective-permute-done.8 = f32[1,1,3,128,128]{3,4,2,1,0:T(8,128)S(1)} collective-permute-done((f32[1,1,3,128,128]{3,4,2,1,0:T(8,128)S(1)}, f32[1,1,3,128,128]{3,4,2,1,0:T(8,128)S(1)}, u32[]{:S(2)}, u32[]{:S(2)}) %collective-permute-start.8) | collective-permute-done | bytes 196640 | tf_op jit(solution)/shard_map/ppermute | solution.py:33
  77.3 4.4 %collective-permute-start.11 = (f32[3,1,3,128,128]{3,4,2,1,0:T(8,128)S(1)}, f32[3,1,3,128,128]{3,4,2,1,0:T(8,128)S(1)}, u32[]{:S(2)}, u32[]{:S(2)}) collective-permute-start(f32[3,1,3,128,128]{3,4,2,1,0:T(8,128)S(1)} %pad_maximum_fusion.2), channel_id=1, source_target_pairs={{4,0},{8,4},{12,8},{16,12},{20,16},{24,20},{28,24},{32,28},{36,32}... | collective-permute-start | bytes 1769480 | tf_op jit(solution)/shard_map/ppermute | solution.py:35
  83.7 5.6 %collective-permute-done.11 = f32[3,1,3,128,128]{3,4,2,1,0:T(8,128)S(1)} collective-permute-done((f32[3,1,3,128,128]{3,4,2,1,0:T(8,128)S(1)}, f32[3,1,3,128,128]{3,4,2,1,0:T(8,128)S(1)}, u32[]{:S(2)}, u32[]{:S(2)}) %collective-permute-start.11) | collective-permute-done | bytes 589856 | tf_op jit(solution)/shard_map/ppermute | solution.py:35
  89.5 1.5 pad_maximum_fusion.table_ref
  90.9 17.4 %shard_map.156 = f32[128,12288]{1,0:T(8,128)} custom-call(s32[12288]{0:T(1024)} %bitcast.270, f32[3968,128]{1,0:T(8,128)} %pad_maximum_fusion.table_ref), custom_call_target="tpu_custom_call" | custom-call | bytes 14614528 | tf_op jit(solution)/shard_map/pallas_call | solution.py:78
  108.4 7.3 %multiply_reduce_fusion.3 = (f32[8,24,512]{2,0,1:T(8,128)S(1)}, f32[16,24,512]{2,1,0:T(8,128)S(1)}, f32[16,24,512]{2,1,0:T(8,128)S(1)}, f32[8,24,512]{2,0,1:T(8,128)S(1)}) fusion(f32[16,8,24,512]{3,1,2,0:T(8,128)} %bitcast.263, f32[16,24,512]{2,1,0:T(8,128)S(1)} %copy-done, f32[8,24,512]{2,0,1:T(8,128)S(1)} %copy.136, f32[16,8,512]{2,1,0:T(8,128)S(1)} %copy.168, ...), kind=kLoop, calls=%fused_computation.6 | loop fusion | flops 11993088 | bytes 10878976 | tf_op jit(solution)/shard_map/transpose(jvp())/reduce_sum | solution.py:149
  117.3 1.0 convolution_bitcast_fusion
  118.4 0.7 pad_maximum_fusion.12
  119.1 3.8 %psum.35 = f32[11]{0:T(128)S(1)} all-reduce(f32[11]{0:T(128)S(1)} %pad_maximum_fusion.12), channel_id=1, replica_groups=mesh['gx_0'=2,'gx_1'=4,'gy_0'=8,'gy_1'=2,'gz'=4] {'gx_0'}, use_global_device_ids=true, to_apply=%region_17.18 | all-reduce | flops 11 | bytes 88 | tf_op jit(solution)/shard_map/psum | solution.py:43
  124.6 4.2 %collective-permute-start.13 = (f32[5,4,4,8]{3,2,1,0:T(4,128)S(1)}, f32[5,4,4,8]{3,2,1,0:T(4,128)S(1)}, u32[]{:S(2)}, u32[]{:S(2)}) collective-permute-start(f32[5,4,4,8]{3,2,1,0:T(4,128)S(1)} %constant_dynamic-update-slice_fusion.36), channel_id=1, source_target_pairs={{1,0},{2,1},{3,2},{0,3},{5,4},{6,5},{7,6},{4,7},{9,8},{10,9},{11,1... | collective-permute-start | bytes 7688 | tf_op jit(solution)/shard_map/ppermute | solution.py:35
  128.8 3.2 %collective-permute-start.12 = (f32[5,4,4,8]{3,2,1,0:T(4,128)S(1)}, f32[5,4,4,8]{3,2,1,0:T(4,128)S(1)}, u32[]{:S(2)}, u32[]{:S(2)}) collective-permute-start(f32[5,4,4,8]{3,2,1,0:T(4,128)S(1)} %constant_dynamic-update-slice_fusion.36), channel_id=1, source_target_pairs={{0,1},{1,2},{2,3},{3,0},{4,5},{5,6},{6,7},{7,4},{8,9},{9,10},{10,1... | collective-permute-start | bytes 7688 | tf_op jit(solution)/shard_map/ppermute | solution.py:33
  132.0 6.0 %psum.36 = f32[11]{0:T(128)S(1)} all-reduce(f32[11]{0:T(128)S(1)} %psum.35), channel_id=1, replica_groups=mesh['gx_0'=2,'gx_1'=4,'gy_0'=8,'gy_1'=2,'gz'=4] {'gx_1'}, use_global_device_ids=true, to_apply=%region_18.19 | all-reduce | flops 11 | bytes 88 | tf_op jit(solution)/shard_map/psum | solution.py:43
  138.0 13.9 %psum.37 = f32[11]{0:T(128)S(1)} all-reduce(f32[11]{0:T(128)S(1)} %psum.36), channel_id=1, replica_groups=mesh['gx_0'=2,'gx_1'=4,'gy_0'=8,'gy_1'=2,'gz'=4] {'gy_0'}, use_global_device_ids=true, to_apply=%region_19.20 | all-reduce | flops 11 | bytes 88 | tf_op jit(solution)/shard_map/psum | solution.py:43
  151.9 8.9 %psum.38 = f32[11]{0:T(128)S(1)} all-reduce(f32[11]{0:T(128)S(1)} %psum.37), channel_id=1, replica_groups=mesh['gx_0'=2,'gx_1'=4,'gy_0'=8,'gy_1'=2,'gz'=4] {'gy_1'}, use_global_device_ids=true, to_apply=%region_20.21 | all-reduce | flops 11 | bytes 88 | tf_op jit(solution)/shard_map/psum | solution.py:43
  161.0 3.6 %collective-permute-start.14 = (f32[5,12,4,4]{3,2,1,0:T(4,128)S(1)}, f32[5,12,4,4]{3,2,1,0:T(4,128)S(1)}, u32[]{:S(2)}, u32[]{:S(2)}) collective-permute-start(f32[5,12,4,4]{3,2,1,0:T(4,128)S(1)} %get-tuple-element.42), channel_id=1, source_target_pairs={{0,64},{64,128},{128,192},{192,256},{256,320},{320,384},{384,448},... | collective-permute-start | bytes 11528 | tf_op jit(solution)/shard_map/ppermute | solution.py:33
  164.6 3.8 %collective-permute-start.15 = (f32[5,12,4,4]{3,2,1,0:T(4,128)S(1)}, f32[5,12,4,4]{3,2,1,0:T(4,128)S(1)}, u32[]{:S(2)}, u32[]{:S(2)}) collective-permute-start(f32[5,12,4,4]{3,2,1,0:T(4,128)S(1)} %get-tuple-element.43), channel_id=1, source_target_pairs={{64,0},{128,64},{192,128},{256,192},{320,256},{384,320},{448,384},... | collective-permute-start | bytes 11528 | tf_op jit(solution)/shard_map/ppermute | solution.py:35
  168.4 10.8 %psum.39 = f32[11]{0:T(128)S(1)} all-reduce(f32[11]{0:T(128)S(1)} %psum.38), channel_id=1, replica_groups=mesh['gx_0'=2,'gx_1'=4,'gy_0'=8,'gy_1'=2,'gz'=4] {'gz'}, use_global_device_ids=true, to_apply=%region_21.22 | all-reduce | flops 11 | bytes 88 | tf_op jit(solution)/shard_map/psum | solution.py:43
  180.0 2.9 %collective-permute-start.17 = (f32[5,12,4,16]{3,2,1,0:T(4,128)S(1)}, f32[5,12,4,16]{3,2,1,0:T(4,128)S(1)}, u32[]{:S(2)}, u32[]{:S(2)}) collective-permute-start(f32[5,12,4,16]{3,2,1,0:T(4,128)S(1)} %pad_maximum_fusion.7), channel_id=1, source_target_pairs={{4,0},{8,4},{12,8},{16,12},{20,16},{24,20},{28,24},{32,28},{36,32}... | collective-permute-start | bytes 46088 | tf_op jit(solution)/shard_map/ppermute | solution.py:35
  182.9 1.6 collective-permute-start.16
  184.5 1.2 slice_divide_fusion
  185.7 1.6 collective-permute-done.17
  188.6 0.7 add_divide_fusion
  (150 shorter events, 22.1 us)
Async XLA Ops:
  3.5 15.5 %collective-permute-start.1 = (f32[1,1,1,3,128]{3,4,2,1,0:T(8,128)S(1)}, f32[1,1,1,3,128]{3,4,2,1,0:T(8,128)S(1)}, u32[]{:S(2)}, u32[]{:S(2)}) collective-permute-start(f32[1,1,1,3,128]{3,4,2,1,0:T(8,128)S(1)} %bitcast_select_fusion.1), channel_id=1, source_target_pairs={{1,0},{2,1},{3,2},{5,4},{6,5},{7,6},{9,8},{10,9},{11,10},{13,12},{... | collective-permute-start | bytes 4616 | tf_op jit(solution)/shard_map/ppermute | solution.py:35
  4.8 14.3 %collective-permute-start = (f32[1,1,1,3,128]{3,4,2,1,0:T(8,128)S(1)}, f32[1,1,1,3,128]{3,4,2,1,0:T(8,128)S(1)}, u32[]{:S(2)}, u32[]{:S(2)}) collective-permute-start(f32[1,1,1,3,128]{3,4,2,1,0:T(8,128)S(1)} %bitcast_select_fusion.1), channel_id=1, source_target_pairs={{0,1},{1,2},{2,3},{4,5},{5,6},{6,7},{8,9},{9,10},{10,11},{12,13},{... | collective-permute-start | bytes 4616 | tf_op jit(solution)/shard_map/ppermute | solution.py:33
  12.1 29.0 %copy-start.2 = (f32[3,512]{1,0:T(4,128)S(1)}, f32[3,512]{1,0:T(4,128)}, u32[]{:S(2)}) copy-start(f32[3,512]{1,0:T(4,128)} %param.13) | copy-start | bytes 18436
  16.4 24.8 %copy-start.1 = (s32[3,4,8,128]{3,1,2,0:T(4,128)}, s32[3,4,8,128]{3,1,2,0:T(4,128)S(1)}, u32[]{:S(2)}) copy-start(s32[3,4,8,128]{3,1,2,0:T(4,128)S(1)} %copy.150) | copy-start | bytes 147460
  19.2 8.1 %collective-permute-start.3 = (f32[1,1,3,3,128]{4,1,3,2,0:T(1,128)S(1)}, f32[1,1,3,3,128]{4,1,3,2,0:T(1,128)S(1)}, u32[]{:S(2)}, u32[]{:S(2)}) collective-permute-start(f32[1,1,3,3,128]{4,1,3,2,0:T(1,128)S(1)} %pad_maximum_fusion.11), channel_id=1, source_target_pairs={{64,0},{128,64},{192,128},{256,192},{320,256},{384,320},{448,384},... | collective-permute-start | bytes 13832 | tf_op jit(solution)/shard_map/ppermute | solution.py:35
  25.4 6.5 %collective-permute-start.2 = (f32[1,1,3,3,128]{4,1,3,2,0:T(1,128)S(1)}, f32[1,1,3,3,128]{4,1,3,2,0:T(1,128)S(1)}, u32[]{:S(2)}, u32[]{:S(2)}) collective-permute-start(f32[1,1,3,3,128]{4,1,3,2,0:T(1,128)S(1)} %pad_maximum_fusion.11), channel_id=1, source_target_pairs={{0,64},{64,128},{128,192},{192,256},{256,320},{320,384},{384,448},... | collective-permute-start | bytes 13832 | tf_op jit(solution)/shard_map/ppermute | solution.py:33
  31.9 5.0 %collective-permute-start.5 = (f32[3,1,3,3,128]{4,1,3,2,0:T(1,128)S(1)}, f32[3,1,3,3,128]{4,1,3,2,0:T(1,128)S(1)}, u32[]{:S(2)}, u32[]{:S(2)}) collective-permute-start(f32[3,1,3,3,128]{4,1,3,2,0:T(1,128)S(1)} %pad_maximum_fusion.10), channel_id=1, source_target_pairs={{4,0},{8,4},{12,8},{16,12},{20,16},{24,20},{28,24},{32,28},{36,32}... | collective-permute-start | bytes 41480 | tf_op jit(solution)/shard_map/ppermute | solution.py:35
  34.3 2.6 %collective-permute-start.4 = (f32[3,1,3,3,128]{4,1,3,2,0:T(1,128)S(1)}, f32[3,1,3,3,128]{4,1,3,2,0:T(1,128)S(1)}, u32[]{:S(2)}, u32[]{:S(2)}) collective-permute-start(f32[3,1,3,3,128]{4,1,3,2,0:T(1,128)S(1)} %pad_maximum_fusion.10), channel_id=1, source_target_pairs={{0,4},{4,8},{8,12},{12,16},{16,20},{20,24},{24,28},{28,32},{32,36}... | collective-permute-start | bytes 41480 | tf_op jit(solution)/shard_map/ppermute | solution.py:33
  45.0 6.3 %copy-start.5 = (f32[16,8]{0,1:T(8,128)S(1)}, f32[16,8]{0,1:T(8,128)}, u32[]{:S(2)}) copy-start(f32[16,8]{0,1:T(8,128)} %param.20) | copy-start | bytes 1540
  51.1 30.6 %copy-start.6 = (f32[16]{0:T(128)S(1)}, f32[16]{0:T(128)}, u32[]{:S(2)}) copy-start(f32[16]{0:T(128)} %param.21) | copy-start | bytes 196
  52.8 13.8 %collective-permute-start.7 = (f32[1,1,1,128,128]{3,4,2,1,0:T(8,128)S(1)}, f32[1,1,1,128,128]{3,4,2,1,0:T(8,128)S(1)}, u32[]{:S(2)}, u32[]{:S(2)}) collective-permute-start(f32[1,1,1,128,128]{3,4,2,1,0:T(8,128)S(1)} %bitcast_select_fusion), channel_id=1, source_target_pairs={{1,0},{2,1},{3,2},{5,4},{6,5},{7,6},{9,8},{10,9},{11,10},{13,12},{... | collective-permute-start | bytes 196616 | tf_op jit(solution)/shard_map/ppermute | solution.py:35
  54.1 12.5 %collective-permute-start.6 = (f32[1,1,1,128,128]{3,4,2,1,0:T(8,128)S(1)}, f32[1,1,1,128,128]{3,4,2,1,0:T(8,128)S(1)}, u32[]{:S(2)}, u32[]{:S(2)}) collective-permute-start(f32[1,1,1,128,128]{3,4,2,1,0:T(8,128)S(1)} %bitcast_select_fusion), channel_id=1, source_target_pairs={{0,1},{1,2},{2,3},{4,5},{5,6},{6,7},{8,9},{9,10},{10,11},{12,13},{... | collective-permute-start | bytes 196616 | tf_op jit(solution)/shard_map/ppermute | solution.py:33
  66.6 6.4 %collective-permute-start.9 = (f32[1,1,3,128,128]{3,4,2,1,0:T(8,128)S(1)}, f32[1,1,3,128,128]{3,4,2,1,0:T(8,128)S(1)}, u32[]{:S(2)}, u32[]{:S(2)}) collective-permute-start(f32[1,1,3,128,128]{3,4,2,1,0:T(8,128)S(1)} %pad_maximum_fusion.4), channel_id=1, source_target_pairs={{64,0},{128,64},{192,128},{256,192},{320,256},{384,320},{448,384},... | collective-permute-start | bytes 589832 | tf_op jit(solution)/shard_map/ppermute | solution.py:35
  68.7 8.5 %collective-permute-start.8 = (f32[1,1,3,128,128]{3,4,2,1,0:T(8,128)S(1)}, f32[1,1,3,128,128]{3,4,2,1,0:T(8,128)S(1)}, u32[]{:S(2)}, u32[]{:S(2)}) collective-permute-start(f32[1,1,3,128,128]{3,4,2,1,0:T(8,128)S(1)} %pad_maximum_fusion.4), channel_id=1, source_target_pairs={{0,64},{64,128},{128,192},{192,256},{256,320},{320,384},{384,448},... | collective-permute-start | bytes 589832 | tf_op jit(solution)/shard_map/ppermute | solution.py:33
  77.3 12.0 %collective-permute-start.11 = (f32[3,1,3,128,128]{3,4,2,1,0:T(8,128)S(1)}, f32[3,1,3,128,128]{3,4,2,1,0:T(8,128)S(1)}, u32[]{:S(2)}, u32[]{:S(2)}) collective-permute-start(f32[3,1,3,128,128]{3,4,2,1,0:T(8,128)S(1)} %pad_maximum_fusion.2), channel_id=1, source_target_pairs={{4,0},{8,4},{12,8},{16,12},{20,16},{24,20},{28,24},{32,28},{36,32}... | collective-permute-start | bytes 1769480 | tf_op jit(solution)/shard_map/ppermute | solution.py:35
  81.7 7.6 %collective-permute-start.10 = (f32[3,1,3,128,128]{3,4,2,1,0:T(8,128)S(1)}, f32[3,1,3,128,128]{3,4,2,1,0:T(8,128)S(1)}, u32[]{:S(2)}, u32[]{:S(2)}) collective-permute-start(f32[3,1,3,128,128]{3,4,2,1,0:T(8,128)S(1)} %pad_maximum_fusion.2), channel_id=1, source_target_pairs={{0,4},{4,8},{8,12},{12,16},{16,20},{20,24},{24,28},{28,32},{32,36}... | collective-permute-start | bytes 1769480 | tf_op jit(solution)/shard_map/ppermute | solution.py:33
  90.9 17.4 %copy-start = (f32[16,24,512]{2,1,0:T(8,128)S(1)}, f32[16,24,512]{2,1,0:T(8,128)}, u32[]{:S(2)}) copy-start(f32[16,24,512]{2,1,0:T(8,128)} %constant_dynamic-update-slice_fusion.22) | copy-start | bytes 2359300
  115.7 7.2 %copy-start.4 = (f32[3,512]{1,0:T(4,128)S(1)}, f32[3,512]{1,0:T(4,128)}, u32[]{:S(2)}) copy-start(f32[3,512]{1,0:T(4,128)} %param.14) | copy-start | bytes 18436
  115.7 7.2 %copy-start.7 = (s32[512]{0:T(512)S(1)}, s32[512]{0:T(512)}, u32[]{:S(2)}) copy-start(s32[512]{0:T(512)} %param.19) | copy-start | bytes 6148
  117.3 73.0 %copy-start.3 = (f32[3,512]{1,0:T(4,128)}, f32[3,512]{1,0:T(4,128)S(1)}, u32[]{:S(2)}) copy-start(f32[3,512]{1,0:T(4,128)S(1)} %get-tuple-element.22) | copy-start | bytes 18436
  124.6 36.3 %collective-permute-start.13 = (f32[5,4,4,8]{3,2,1,0:T(4,128)S(1)}, f32[5,4,4,8]{3,2,1,0:T(4,128)S(1)}, u32[]{:S(2)}, u32[]{:S(2)}) collective-permute-start(f32[5,4,4,8]{3,2,1,0:T(4,128)S(1)} %constant_dynamic-update-slice_fusion.36), channel_id=1, source_target_pairs={{1,0},{2,1},{3,2},{0,3},{5,4},{6,5},{7,6},{4,7},{9,8},{10,9},{11,1... | collective-permute-start | bytes 7688 | tf_op jit(solution)/shard_map/ppermute | solution.py:35
  128.8 32.0 %collective-permute-start.12 = (f32[5,4,4,8]{3,2,1,0:T(4,128)S(1)}, f32[5,4,4,8]{3,2,1,0:T(4,128)S(1)}, u32[]{:S(2)}, u32[]{:S(2)}) collective-permute-start(f32[5,4,4,8]{3,2,1,0:T(4,128)S(1)} %constant_dynamic-update-slice_fusion.36), channel_id=1, source_target_pairs={{0,1},{1,2},{2,3},{3,0},{4,5},{5,6},{6,7},{7,4},{8,9},{9,10},{10,1... | collective-permute-start | bytes 7688 | tf_op jit(solution)/shard_map/ppermute | solution.py:33
  161.0 18.8 %collective-permute-start.14 = (f32[5,12,4,4]{3,2,1,0:T(4,128)S(1)}, f32[5,12,4,4]{3,2,1,0:T(4,128)S(1)}, u32[]{:S(2)}, u32[]{:S(2)}) collective-permute-start(f32[5,12,4,4]{3,2,1,0:T(4,128)S(1)} %get-tuple-element.42), channel_id=1, source_target_pairs={{0,64},{64,128},{128,192},{192,256},{256,320},{320,384},{384,448},... | collective-permute-start | bytes 11528 | tf_op jit(solution)/shard_map/ppermute | solution.py:33
  164.6 15.1 %collective-permute-start.15 = (f32[5,12,4,4]{3,2,1,0:T(4,128)S(1)}, f32[5,12,4,4]{3,2,1,0:T(4,128)S(1)}, u32[]{:S(2)}, u32[]{:S(2)}) collective-permute-start(f32[5,12,4,4]{3,2,1,0:T(4,128)S(1)} %get-tuple-element.43), channel_id=1, source_target_pairs={{64,0},{128,64},{192,128},{256,192},{320,256},{384,320},{448,384},... | collective-permute-start | bytes 11528 | tf_op jit(solution)/shard_map/ppermute | solution.py:35
  180.0 7.4 %collective-permute-start.17 = (f32[5,12,4,16]{3,2,1,0:T(4,128)S(1)}, f32[5,12,4,16]{3,2,1,0:T(4,128)S(1)}, u32[]{:S(2)}, u32[]{:S(2)}) collective-permute-start(f32[5,12,4,16]{3,2,1,0:T(4,128)S(1)} %pad_maximum_fusion.7), channel_id=1, source_target_pairs={{4,0},{8,4},{12,8},{16,12},{20,16},{24,20},{28,24},{32,28},{36,32}... | collective-permute-start | bytes 46088 | tf_op jit(solution)/shard_map/ppermute | solution.py:35
  182.9 4.4 %collective-permute-start.16 = (f32[5,12,4,16]{3,2,1,0:T(4,128)S(1)}, f32[5,12,4,16]{3,2,1,0:T(4,128)S(1)}, u32[]{:S(2)}, u32[]{:S(2)}) collective-permute-start(f32[5,12,4,16]{3,2,1,0:T(4,128)S(1)} %pad_maximum_fusion.7), channel_id=1, source_target_pairs={{0,4},{4,8},{8,12},{12,16},{16,20},{20,24},{24,28},{28,32},{32,36}... | collective-permute-start | bytes 46088 | tf_op jit(solution)/shard_map/ppermute | solution.py:33

commit v4 on v3

--- a/solution.py
+++ b/solution.py
@@ -54,7 +54,7 @@
     return jnp.sum(ordered, axis=0)
 
 
-def row_gather(table_rows, flat_index, chunk=3072):
+def row_gather(table_rows, flat_index, chunk=4096):
     rows, width = table_rows.shape
     total = flat_index.shape[0]
 
@@ -69,7 +69,7 @@
             stage_ref[pl.ds(first, 8), :] = jnp.concatenate(picked, axis=0)
             return carry
 
-        lax.fori_loop(0, chunk // 8, copy_rows, 0, unroll=8)
+        lax.fori_loop(0, chunk // 8, copy_rows, 0, unroll=16)
         for part in range(chunk // 128):
             out_ref[:, part * 128 : (part + 1) * 128] = stage_ref[
                 part * 128 : (part + 1) * 128, :

time: 191 us -> 191 us (level)
  no operation moved by 1% of the time
where the time goes in v4:
time: 191 us; the launch traced here: 190 us
  starting transfers between devices  57.5 us (30%)
  blocking collectives  43.3 us (23%)
  other arithmetic  38.1 us (20%)
  Pallas kernels  17 us (9%)
  waiting for transfers between devices  16.6 us (9%)
  local copies, waits for them, and re-layouts  10.4 us (5%)
  matrix products  4.83 us (3%)
  between operations  2.07 us (1%)
    psum x5, blocking collectives, by_axis(): return functools.reduce(lax.psum, axes, shard)  43.3 us
    ppermute x9, starting transfers between devices, padded(): lax.ppermute(tail, axis, [(i, (i + 1) % count) for i in range(links)])  28.9 us
    ppermute x9, starting transfers between devices, padded(): lax.ppermute(head, axis, [((i + 1) % count, i) for i in range(links)])  28.7 us
    pallas_call x1, Pallas kernels, row_gather(): pl.pallas_call(kernel, out_shape=jax.ShapeDtypeStruct((width, total), tab...  17 us
    ppermute x9, waiting for transfers between devices, padded(): lax.ppermute(tail, axis, [(i, (i + 1) % count) for i in range(links)])  8.75 us
    unnamed x29, other arithmetic  7.98 us
    ppermute x9, waiting for transfers between devices, padded(): lax.ppermute(head, axis, [((i + 1) % count, i) for i in range(links)])  7.85 us
    reduce_sum x1, other arithmetic, pair_energy(): mixed = jnp.sum(weights * basis[None], axis=1)  7.34 us
  transfers between devices with their start and end apart: 18, of which 6 were waited for; matrix products, arithmetic and copies ran while one was open for 9% of the time, Pallas kernels for 0%

profile of v4, /device:TPU:1, one launch (start us, length us, event | category | flops | bytes accessed | tf_op | source)
XLA Modules:
  0.0 189.8 jit_solution(2125174681654643655)
XLA Ops:
  2.0 0.8 copy.128
  3.5 1.3 collective-permute-start.1
  4.8 7.3 %collective-permute-start = (f32[1,1,1,3,128]{3,4,2,1,0:T(8,128)S(1)}, f32[1,1,1,3,128]{3,4,2,1,0:T(8,128)S(1)}, u32[]{:S(2)}, u32[]{:S(2)}) collective-permute-start(f32[1,1,1,3,128]{3,4,2,1,0:T(8,128)S(1)} %bitcast_select_fusion.1), channel_id=1, source_target_pairs={{0,1},{1,2},{2,3},{4,5},{5,6},{6,7},{8,9},{9,10},{10,11},{12,13},{... | collective-permute-start | bytes 4616 | tf_op jit(solution)/shard_map/ppermute | solution.py:33
  13.5 0.8 fusion.267
  14.2 0.7 constant_dynamic-update-slice_fusion.40
  14.9 0.7 fusion.167
  15.6 0.8 copy.150
  16.7 0.7 broadcast_multiply_fusion.2
  17.4 0.7 constant_dynamic-update-slice_fusion.39
  18.2 0.7 constant_dynamic-update-slice_fusion.38
  19.2 6.2 %collective-permute-start.3 = (f32[1,1,3,3,128]{4,1,3,2,0:T(1,128)S(1)}, f32[1,1,3,3,128]{4,1,3,2,0:T(1,128)S(1)}, u32[]{:S(2)}, u32[]{:S(2)}) collective-permute-start(f32[1,1,3,3,128]{4,1,3,2,0:T(1,128)S(1)} %pad_maximum_fusion.11), channel_id=1, source_target_pairs={{64,0},{128,64},{192,128},{256,192},{320,256},{384,320},{448,384},... | collective-permute-start | bytes 13832 | tf_op jit(solution)/shard_map/ppermute | solution.py:35
  25.4 1.9 %collective-permute-start.2 = (f32[1,1,3,3,128]{4,1,3,2,0:T(1,128)S(1)}, f32[1,1,3,3,128]{4,1,3,2,0:T(1,128)S(1)}, u32[]{:S(2)}, u32[]{:S(2)}) collective-permute-start(f32[1,1,3,3,128]{4,1,3,2,0:T(1,128)S(1)} %pad_maximum_fusion.11), channel_id=1, source_target_pairs={{0,64},{64,128},{128,192},{192,256},{256,320},{320,384},{384,448},... | collective-permute-start | bytes 13832 | tf_op jit(solution)/shard_map/ppermute | solution.py:33
  27.4 4.5 %collective-permute-done.2 = f32[1,1,3,3,128]{4,1,3,2,0:T(1,128)S(1)} collective-permute-done((f32[1,1,3,3,128]{4,1,3,2,0:T(1,128)S(1)}, f32[1,1,3,3,128]{4,1,3,2,0:T(1,128)S(1)}, u32[]{:S(2)}, u32[]{:S(2)}) %collective-permute-start.2) | collective-permute-done | bytes 4640 | tf_op jit(solution)/shard_map/ppermute | solution.py:33
  31.9 2.4 %collective-permute-start.5 = (f32[3,1,3,3,128]{4,1,3,2,0:T(1,128)S(1)}, f32[3,1,3,3,128]{4,1,3,2,0:T(1,128)S(1)}, u32[]{:S(2)}, u32[]{:S(2)}) collective-permute-start(f32[3,1,3,3,128]{4,1,3,2,0:T(1,128)S(1)} %pad_maximum_fusion.10), channel_id=1, source_target_pairs={{4,0},{8,4},{12,8},{16,12},{20,16},{24,20},{28,24},{32,28},{36,32}... | collective-permute-start | bytes 41480 | tf_op jit(solution)/shard_map/ppermute | solution.py:35
  34.3 1.2 collective-permute-start.4
  35.5 0.8 copy.127
  37.0 0.7 pad_maximum_fusion.8
  37.8 3.3 %fusion.3 = f32[3,12288]{1,0:T(4,128)S(1)} fusion(f32[3,31,128]{2,1,0:T(8,128)S(1)} %dot_general.17, s32[12288]{0:T(1024)S(1)} %get-tuple-element.47, pred[31,12288]{1,0:T(8,128)(4,1)S(1)} %iota_compare_fusion.1), kind=kOutput, calls=%fused_computation.17 | convolution fusion | flops 1759137792 | bytes 625152 | tf_op jit(solution)/shard_map/dot_general | solution.py:103
  41.2 0.7 constant_dynamic-update-slice_fusion.34
  42.7 2.2 %multiply_reduce_fusion.7 = f32[16,24,512]{2,1,0:T(8,128)S(1)} fusion(f32[8,24,512]{2,0,1:T(8,128)S(1)} %copy.136, f32[16,8]{1,0:T(8,128)S(1)} %copy.127), kind=kLoop, calls=%fused_computation.10 | loop fusion | flops 2949120 | bytes 1180160 | tf_op jit(solution)/shard_map/reduce_sum | solution.py:155
  45.1 2.7 %multiply_reduce_fusion = f32[16,16,512]{2,1,0:T(8,128)S(1)} fusion(f32[16,24,512]{2,1,0:T(8,128)S(1)} %constant_dynamic-update-slice_fusion.8, f32[16,24,512]{2,1,0:T(8,128)S(1)} %broadcast_multiply_fusion), kind=kLoop, calls=%fused_computation.3 | loop fusion | flops 6160384 | bytes 2097152 | tf_op jit(solution)/shard_map/reduce_sum | solution.py:156
  48.1 3.1 %multiply_reduce_fusion.1 = (f32[16,16,512]{2,1,0:T(8,128)S(1)}, f32[16,16,512]{2,1,0:T(8,128)S(1)}) fusion(f32[16,16,16]{2,1,0:T(8,128)S(1)} %copy.138, f32[16,16,512]{2,1,0:T(8,128)S(1)} %copy.137, f32[16,16,16]{2,1,0:T(8,128)S(1)} %get-tuple-element.37), kind=kLoop, calls=%fused_computation.4 | loop fusion | flops 8126464 | bytes 1605632 | tf_op jit(solution)/shard_map/reduce_sum | solution.py:171
  52.8 1.3 collective-permute-start.7
  54.1 6.8 %collective-permute-start.6 = (f32[1,1,1,128,128]{3,4,2,1,0:T(8,128)S(1)}, f32[1,1,1,128,128]{3,4,2,1,0:T(8,128)S(1)}, u32[]{:S(2)}, u32[]{:S(2)}) collective-permute-start(f32[1,1,1,128,128]{3,4,2,1,0:T(8,128)S(1)} %bitcast_select_fusion), channel_id=1, source_target_pairs={{0,1},{1,2},{2,3},{4,5},{5,6},{6,7},{8,9},{9,10},{10,11},{12,13},{... | collective-permute-start | bytes 196616 | tf_op jit(solution)/shard_map/ppermute | solution.py:33
  66.6 2.1 %collective-permute-start.9 = (f32[1,1,3,128,128]{3,4,2,1,0:T(8,128)S(1)}, f32[1,1,3,128,128]{3,4,2,1,0:T(8,128)S(1)}, u32[]{:S(2)}, u32[]{:S(2)}) collective-permute-start(f32[1,1,3,128,128]{3,4,2,1,0:T(8,128)S(1)} %pad_maximum_fusion.4), channel_id=1, source_target_pairs={{64,0},{128,64},{192,128},{256,192},{320,256},{384,320},{448,384},... | collective-permute-start | bytes 589832 | tf_op jit(solution)/shard_map/ppermute | solution.py:35
  68.7 3.4 %collective-permute-start.8 = (f32[1,1,3,128,128]{3,4,2,1,0:T(8,128)S(1)}, f32[1,1,3,128,128]{3,4,2,1,0:T(8,128)S(1)}, u32[]{:S(2)}, u32[]{:S(2)}) collective-permute-start(f32[1,1,3,128,128]{3,4,2,1,0:T(8,128)S(1)} %pad_maximum_fusion.4), channel_id=1, source_target_pairs={{0,64},{64,128},{128,192},{192,256},{256,320},{320,384},{384,448},... | collective-permute-start | bytes 589832 | tf_op jit(solution)/shard_map/ppermute | solution.py:33
  73.0 4.2 %collective-permute-done.8 = f32[1,1,3,128,128]{3,4,2,1,0:T(8,128)S(1)} collective-permute-done((f32[1,1,3,128,128]{3,4,2,1,0:T(8,128)S(1)}, f32[1,1,3,128,128]{3,4,2,1,0:T(8,128)S(1)}, u32[]{:S(2)}, u32[]{:S(2)}) %collective-permute-start.8) | collective-permute-done | bytes 196640 | tf_op jit(solution)/shard_map/ppermute | solution.py:33
  77.3 4.4 %collective-permute-start.11 = (f32[3,1,3,128,128]{3,4,2,1,0:T(8,128)S(1)}, f32[3,1,3,128,128]{3,4,2,1,0:T(8,128)S(1)}, u32[]{:S(2)}, u32[]{:S(2)}) collective-permute-start(f32[3,1,3,128,128]{3,4,2,1,0:T(8,128)S(1)} %pad_maximum_fusion.2), channel_id=1, source_target_pairs={{4,0},{8,4},{12,8},{16,12},{20,16},{24,20},{28,24},{32,28},{36,32}... | collective-permute-start | bytes 1769480 | tf_op jit(solution)/shard_map/ppermute | solution.py:35
  83.7 5.6 %collective-permute-done.11 = f32[3,1,3,128,128]{3,4,2,1,0:T(8,128)S(1)} collective-permute-done((f32[3,1,3,128,128]{3,4,2,1,0:T(8,128)S(1)}, f32[3,1,3,128,128]{3,4,2,1,0:T(8,128)S(1)}, u32[]{:S(2)}, u32[]{:S(2)}) %collective-permute-start.11) | collective-permute-done | bytes 589856 | tf_op jit(solution)/shard_map/ppermute | solution.py:35
  89.5 1.5 pad_maximum_fusion.table_ref
  90.9 17.0 %shard_map.156 = f32[128,12288]{1,0:T(8,128)} custom-call(s32[12288]{0:T(1024)} %bitcast.270, f32[3968,128]{1,0:T(8,128)} %pad_maximum_fusion.table_ref), custom_call_target="tpu_custom_call" | custom-call | bytes 14614528 | tf_op jit(solution)/shard_map/pallas_call | solution.py:78
  107.9 7.3 %multiply_reduce_fusion.3 = (f32[8,24,512]{2,0,1:T(8,128)S(1)}, f32[16,24,512]{2,1,0:T(8,128)S(1)}, f32[16,24,512]{2,1,0:T(8,128)S(1)}, f32[8,24,512]{2,0,1:T(8,128)S(1)}) fusion(f32[16,8,24,512]{3,1,2,0:T(8,128)} %bitcast.263, f32[16,24,512]{2,1,0:T(8,128)S(1)} %copy-done, f32[8,24,512]{2,0,1:T(8,128)S(1)} %copy.136, f32[16,8,512]{2,1,0:T(8,128)S(1)} %copy.168, ...), kind=kLoop, calls=%fused_computation.6 | loop fusion | flops 11993088 | bytes 10878976 | tf_op jit(solution)/shard_map/transpose(jvp())/reduce_sum | solution.py:149
  116.8 1.0 convolution_bitcast_fusion
  118.0 0.7 pad_maximum_fusion.12
  118.7 3.8 %psum.35 = f32[11]{0:T(128)S(1)} all-reduce(f32[11]{0:T(128)S(1)} %pad_maximum_fusion.12), channel_id=1, replica_groups=mesh['gx_0'=2,'gx_1'=4,'gy_0'=8,'gy_1'=2,'gz'=4] {'gx_0'}, use_global_device_ids=true, to_apply=%region_17.18 | all-reduce | flops 11 | bytes 88 | tf_op jit(solution)/shard_map/psum | solution.py:43
  124.1 4.3 %collective-permute-start.13 = (f32[5,4,4,8]{3,2,1,0:T(4,128)S(1)}, f32[5,4,4,8]{3,2,1,0:T(4,128)S(1)}, u32[]{:S(2)}, u32[]{:S(2)}) collective-permute-start(f32[5,4,4,8]{3,2,1,0:T(4,128)S(1)} %constant_dynamic-update-slice_fusion.36), channel_id=1, source_target_pairs={{1,0},{2,1},{3,2},{0,3},{5,4},{6,5},{7,6},{4,7},{9,8},{10,9},{11,1... | collective-permute-start | bytes 7688 | tf_op jit(solution)/shard_map/ppermute | solution.py:35
  128.4 3.1 %collective-permute-start.12 = (f32[5,4,4,8]{3,2,1,0:T(4,128)S(1)}, f32[5,4,4,8]{3,2,1,0:T(4,128)S(1)}, u32[]{:S(2)}, u32[]{:S(2)}) collective-permute-start(f32[5,4,4,8]{3,2,1,0:T(4,128)S(1)} %constant_dynamic-update-slice_fusion.36), channel_id=1, source_target_pairs={{0,1},{1,2},{2,3},{3,0},{4,5},{5,6},{6,7},{7,4},{8,9},{9,10},{10,1... | collective-permute-start | bytes 7688 | tf_op jit(solution)/shard_map/ppermute | solution.py:33
  131.5 6.0 %psum.36 = f32[11]{0:T(128)S(1)} all-reduce(f32[11]{0:T(128)S(1)} %psum.35), channel_id=1, replica_groups=mesh['gx_0'=2,'gx_1'=4,'gy_0'=8,'gy_1'=2,'gz'=4] {'gx_1'}, use_global_device_ids=true, to_apply=%region_18.19 | all-reduce | flops 11 | bytes 88 | tf_op jit(solution)/shard_map/psum | solution.py:43
  137.6 13.9 %psum.37 = f32[11]{0:T(128)S(1)} all-reduce(f32[11]{0:T(128)S(1)} %psum.36), channel_id=1, replica_groups=mesh['gx_0'=2,'gx_1'=4,'gy_0'=8,'gy_1'=2,'gz'=4] {'gy_0'}, use_global_device_ids=true, to_apply=%region_19.20 | all-reduce | flops 11 | bytes 88 | tf_op jit(solution)/shard_map/psum | solution.py:43
  151.5 8.9 %psum.38 = f32[11]{0:T(128)S(1)} all-reduce(f32[11]{0:T(128)S(1)} %psum.37), channel_id=1, replica_groups=mesh['gx_0'=2,'gx_1'=4,'gy_0'=8,'gy_1'=2,'gz'=4] {'gy_1'}, use_global_device_ids=true, to_apply=%region_20.21 | all-reduce | flops 11 | bytes 88 | tf_op jit(solution)/shard_map/psum | solution.py:43
  160.6 3.6 %collective-permute-start.14 = (f32[5,12,4,4]{3,2,1,0:T(4,128)S(1)}, f32[5,12,4,4]{3,2,1,0:T(4,128)S(1)}, u32[]{:S(2)}, u32[]{:S(2)}) collective-permute-start(f32[5,12,4,4]{3,2,1,0:T(4,128)S(1)} %get-tuple-element.42), channel_id=1, source_target_pairs={{0,64},{64,128},{128,192},{192,256},{256,320},{320,384},{384,448},... | collective-permute-start | bytes 11528 | tf_op jit(solution)/shard_map/ppermute | solution.py:33
  164.2 3.8 %collective-permute-start.15 = (f32[5,12,4,4]{3,2,1,0:T(4,128)S(1)}, f32[5,12,4,4]{3,2,1,0:T(4,128)S(1)}, u32[]{:S(2)}, u32[]{:S(2)}) collective-permute-start(f32[5,12,4,4]{3,2,1,0:T(4,128)S(1)} %get-tuple-element.43), channel_id=1, source_target_pairs={{64,0},{128,64},{192,128},{256,192},{320,256},{384,320},{448,384},... | collective-permute-start | bytes 11528 | tf_op jit(solution)/shard_map/ppermute | solution.py:35
  168.0 10.8 %psum.39 = f32[11]{0:T(128)S(1)} all-reduce(f32[11]{0:T(128)S(1)} %psum.38), channel_id=1, replica_groups=mesh['gx_0'=2,'gx_1'=4,'gy_0'=8,'gy_1'=2,'gz'=4] {'gz'}, use_global_device_ids=true, to_apply=%region_21.22 | all-reduce | flops 11 | bytes 88 | tf_op jit(solution)/shard_map/psum | solution.py:43
  179.5 2.9 %collective-permute-start.17 = (f32[5,12,4,16]{3,2,1,0:T(4,128)S(1)}, f32[5,12,4,16]{3,2,1,0:T(4,128)S(1)}, u32[]{:S(2)}, u32[]{:S(2)}) collective-permute-start(f32[5,12,4,16]{3,2,1,0:T(4,128)S(1)} %pad_maximum_fusion.7), channel_id=1, source_target_pairs={{4,0},{8,4},{12,8},{16,12},{20,16},{24,20},{28,24},{32,28},{36,32}... | collective-permute-start | bytes 46088 | tf_op jit(solution)/shard_map/ppermute | solution.py:35
  182.5 1.6 collective-permute-start.16
  184.1 1.2 slice_divide_fusion
  185.3 1.6 collective-permute-done.17
  188.2 0.7 add_divide_fusion
  (150 shorter events, 22.1 us)
Async XLA Ops:
  3.5 15.5 %collective-permute-start.1 = (f32[1,1,1,3,128]{3,4,2,1,0:T(8,128)S(1)}, f32[1,1,1,3,128]{3,4,2,1,0:T(8,128)S(1)}, u32[]{:S(2)}, u32[]{:S(2)}) collective-permute-start(f32[1,1,1,3,128]{3,4,2,1,0:T(8,128)S(1)} %bitcast_select_fusion.1), channel_id=1, source_target_pairs={{1,0},{2,1},{3,2},{5,4},{6,5},{7,6},{9,8},{10,9},{11,10},{13,12},{... | collective-permute-start | bytes 4616 | tf_op jit(solution)/shard_map/ppermute | solution.py:35
  4.8 14.3 %collective-permute-start = (f32[1,1,1,3,128]{3,4,2,1,0:T(8,128)S(1)}, f32[1,1,1,3,128]{3,4,2,1,0:T(8,128)S(1)}, u32[]{:S(2)}, u32[]{:S(2)}) collective-permute-start(f32[1,1,1,3,128]{3,4,2,1,0:T(8,128)S(1)} %bitcast_select_fusion.1), channel_id=1, source_target_pairs={{0,1},{1,2},{2,3},{4,5},{5,6},{6,7},{8,9},{9,10},{10,11},{12,13},{... | collective-permute-start | bytes 4616 | tf_op jit(solution)/shard_map/ppermute | solution.py:33
  12.1 29.0 %copy-start.2 = (f32[3,512]{1,0:T(4,128)S(1)}, f32[3,512]{1,0:T(4,128)}, u32[]{:S(2)}) copy-start(f32[3,512]{1,0:T(4,128)} %param.13) | copy-start | bytes 18436
  16.4 24.7 %copy-start.1 = (s32[3,4,8,128]{3,1,2,0:T(4,128)}, s32[3,4,8,128]{3,1,2,0:T(4,128)S(1)}, u32[]{:S(2)}) copy-start(s32[3,4,8,128]{3,1,2,0:T(4,128)S(1)} %copy.150) | copy-start | bytes 147460
  19.2 8.1 %collective-permute-start.3 = (f32[1,1,3,3,128]{4,1,3,2,0:T(1,128)S(1)}, f32[1,1,3,3,128]{4,1,3,2,0:T(1,128)S(1)}, u32[]{:S(2)}, u32[]{:S(2)}) collective-permute-start(f32[1,1,3,3,128]{4,1,3,2,0:T(1,128)S(1)} %pad_maximum_fusion.11), channel_id=1, source_target_pairs={{64,0},{128,64},{192,128},{256,192},{320,256},{384,320},{448,384},... | collective-permute-start | bytes 13832 | tf_op jit(solution)/shard_map/ppermute | solution.py:35
  25.4 6.5 %collective-permute-start.2 = (f32[1,1,3,3,128]{4,1,3,2,0:T(1,128)S(1)}, f32[1,1,3,3,128]{4,1,3,2,0:T(1,128)S(1)}, u32[]{:S(2)}, u32[]{:S(2)}) collective-permute-start(f32[1,1,3,3,128]{4,1,3,2,0:T(1,128)S(1)} %pad_maximum_fusion.11), channel_id=1, source_target_pairs={{0,64},{64,128},{128,192},{192,256},{256,320},{320,384},{384,448},... | collective-permute-start | bytes 13832 | tf_op jit(solution)/shard_map/ppermute | solution.py:33
  31.9 5.0 %collective-permute-start.5 = (f32[3,1,3,3,128]{4,1,3,2,0:T(1,128)S(1)}, f32[3,1,3,3,128]{4,1,3,2,0:T(1,128)S(1)}, u32[]{:S(2)}, u32[]{:S(2)}) collective-permute-start(f32[3,1,3,3,128]{4,1,3,2,0:T(1,128)S(1)} %pad_maximum_fusion.10), channel_id=1, source_target_pairs={{4,0},{8,4},{12,8},{16,12},{20,16},{24,20},{28,24},{32,28},{36,32}... | collective-permute-start | bytes 41480 | tf_op jit(solution)/shard_map/ppermute | solution.py:35
  34.3 2.6 %collective-permute-start.4 = (f32[3,1,3,3,128]{4,1,3,2,0:T(1,128)S(1)}, f32[3,1,3,3,128]{4,1,3,2,0:T(1,128)S(1)}, u32[]{:S(2)}, u32[]{:S(2)}) collective-permute-start(f32[3,1,3,3,128]{4,1,3,2,0:T(1,128)S(1)} %pad_maximum_fusion.10), channel_id=1, source_target_pairs={{0,4},{4,8},{8,12},{12,16},{16,20},{20,24},{24,28},{28,32},{32,36}... | collective-permute-start | bytes 41480 | tf_op jit(solution)/shard_map/ppermute | solution.py:33
  45.0 6.3 %copy-start.5 = (f32[16,8]{0,1:T(8,128)S(1)}, f32[16,8]{0,1:T(8,128)}, u32[]{:S(2)}) copy-start(f32[16,8]{0,1:T(8,128)} %param.20) | copy-start | bytes 1540
  51.1 30.6 %copy-start.6 = (f32[16]{0:T(128)S(1)}, f32[16]{0:T(128)}, u32[]{:S(2)}) copy-start(f32[16]{0:T(128)} %param.21) | copy-start | bytes 196
  52.8 13.7 %collective-permute-start.7 = (f32[1,1,1,128,128]{3,4,2,1,0:T(8,128)S(1)}, f32[1,1,1,128,128]{3,4,2,1,0:T(8,128)S(1)}, u32[]{:S(2)}, u32[]{:S(2)}) collective-permute-start(f32[1,1,1,128,128]{3,4,2,1,0:T(8,128)S(1)} %bitcast_select_fusion), channel_id=1, source_target_pairs={{1,0},{2,1},{3,2},{5,4},{6,5},{7,6},{9,8},{10,9},{11,10},{13,12},{... | collective-permute-start | bytes 196616 | tf_op jit(solution)/shard_map/ppermute | solution.py:35
  54.1 12.5 %collective-permute-start.6 = (f32[1,1,1,128,128]{3,4,2,1,0:T(8,128)S(1)}, f32[1,1,1,128,128]{3,4,2,1,0:T(8,128)S(1)}, u32[]{:S(2)}, u32[]{:S(2)}) collective-permute-start(f32[1,1,1,128,128]{3,4,2,1,0:T(8,128)S(1)} %bitcast_select_fusion), channel_id=1, source_target_pairs={{0,1},{1,2},{2,3},{4,5},{5,6},{6,7},{8,9},{9,10},{10,11},{12,13},{... | collective-permute-start | bytes 196616 | tf_op jit(solution)/shard_map/ppermute | solution.py:33
  66.6 6.4 %collective-permute-start.9 = (f32[1,1,3,128,128]{3,4,2,1,0:T(8,128)S(1)}, f32[1,1,3,128,128]{3,4,2,1,0:T(8,128)S(1)}, u32[]{:S(2)}, u32[]{:S(2)}) collective-permute-start(f32[1,1,3,128,128]{3,4,2,1,0:T(8,128)S(1)} %pad_maximum_fusion.4), channel_id=1, source_target_pairs={{64,0},{128,64},{192,128},{256,192},{320,256},{384,320},{448,384},... | collective-permute-start | bytes 589832 | tf_op jit(solution)/shard_map/ppermute | solution.py:35
  68.7 8.5 %collective-permute-start.8 = (f32[1,1,3,128,128]{3,4,2,1,0:T(8,128)S(1)}, f32[1,1,3,128,128]{3,4,2,1,0:T(8,128)S(1)}, u32[]{:S(2)}, u32[]{:S(2)}) collective-permute-start(f32[1,1,3,128,128]{3,4,2,1,0:T(8,128)S(1)} %pad_maximum_fusion.4), channel_id=1, source_target_pairs={{0,64},{64,128},{128,192},{192,256},{256,320},{320,384},{384,448},... | collective-permute-start | bytes 589832 | tf_op jit(solution)/shard_map/ppermute | solution.py:33
  77.3 12.0 %collective-permute-start.11 = (f32[3,1,3,128,128]{3,4,2,1,0:T(8,128)S(1)}, f32[3,1,3,128,128]{3,4,2,1,0:T(8,128)S(1)}, u32[]{:S(2)}, u32[]{:S(2)}) collective-permute-start(f32[3,1,3,128,128]{3,4,2,1,0:T(8,128)S(1)} %pad_maximum_fusion.2), channel_id=1, source_target_pairs={{4,0},{8,4},{12,8},{16,12},{20,16},{24,20},{28,24},{32,28},{36,32}... | collective-permute-start | bytes 1769480 | tf_op jit(solution)/shard_map/ppermute | solution.py:35
  81.7 7.6 %collective-permute-start.10 = (f32[3,1,3,128,128]{3,4,2,1,0:T(8,128)S(1)}, f32[3,1,3,128,128]{3,4,2,1,0:T(8,128)S(1)}, u32[]{:S(2)}, u32[]{:S(2)}) collective-permute-start(f32[3,1,3,128,128]{3,4,2,1,0:T(8,128)S(1)} %pad_maximum_fusion.2), channel_id=1, source_target_pairs={{0,4},{4,8},{8,12},{12,16},{16,20},{20,24},{24,28},{28,32},{32,36}... | collective-permute-start | bytes 1769480 | tf_op jit(solution)/shard_map/ppermute | solution.py:33
  90.9 17.0 %copy-start = (f32[16,24,512]{2,1,0:T(8,128)S(1)}, f32[16,24,512]{2,1,0:T(8,128)}, u32[]{:S(2)}) copy-start(f32[16,24,512]{2,1,0:T(8,128)} %constant_dynamic-update-slice_fusion.22) | copy-start | bytes 2359300
  115.3 7.2 %copy-start.4 = (f32[3,512]{1,0:T(4,128)S(1)}, f32[3,512]{1,0:T(4,128)}, u32[]{:S(2)}) copy-start(f32[3,512]{1,0:T(4,128)} %param.14) | copy-start | bytes 18436
  115.3 7.2 %copy-start.7 = (s32[512]{0:T(512)S(1)}, s32[512]{0:T(512)}, u32[]{:S(2)}) copy-start(s32[512]{0:T(512)} %param.19) | copy-start | bytes 6148
  116.8 73.0 %copy-start.3 = (f32[3,512]{1,0:T(4,128)}, f32[3,512]{1,0:T(4,128)S(1)}, u32[]{:S(2)}) copy-start(f32[3,512]{1,0:T(4,128)S(1)} %get-tuple-element.22) | copy-start | bytes 18436
  124.1 36.2 %collective-permute-start.13 = (f32[5,4,4,8]{3,2,1,0:T(4,128)S(1)}, f32[5,4,4,8]{3,2,1,0:T(4,128)S(1)}, u32[]{:S(2)}, u32[]{:S(2)}) collective-permute-start(f32[5,4,4,8]{3,2,1,0:T(4,128)S(1)} %constant_dynamic-update-slice_fusion.36), channel_id=1, source_target_pairs={{1,0},{2,1},{3,2},{0,3},{5,4},{6,5},{7,6},{4,7},{9,8},{10,9},{11,1... | collective-permute-start | bytes 7688 | tf_op jit(solution)/shard_map/ppermute | solution.py:35
  128.4 32.0 %collective-permute-start.12 = (f32[5,4,4,8]{3,2,1,0:T(4,128)S(1)}, f32[5,4,4,8]{3,2,1,0:T(4,128)S(1)}, u32[]{:S(2)}, u32[]{:S(2)}) collective-permute-start(f32[5,4,4,8]{3,2,1,0:T(4,128)S(1)} %constant_dynamic-update-slice_fusion.36), channel_id=1, source_target_pairs={{0,1},{1,2},{2,3},{3,0},{4,5},{5,6},{6,7},{7,4},{8,9},{9,10},{10,1... | collective-permute-start | bytes 7688 | tf_op jit(solution)/shard_map/ppermute | solution.py:33
  160.6 18.8 %collective-permute-start.14 = (f32[5,12,4,4]{3,2,1,0:T(4,128)S(1)}, f32[5,12,4,4]{3,2,1,0:T(4,128)S(1)}, u32[]{:S(2)}, u32[]{:S(2)}) collective-permute-start(f32[5,12,4,4]{3,2,1,0:T(4,128)S(1)} %get-tuple-element.42), channel_id=1, source_target_pairs={{0,64},{64,128},{128,192},{192,256},{256,320},{320,384},{384,448},... | collective-permute-start | bytes 11528 | tf_op jit(solution)/shard_map/ppermute | solution.py:33
  164.2 15.1 %collective-permute-start.15 = (f32[5,12,4,4]{3,2,1,0:T(4,128)S(1)}, f32[5,12,4,4]{3,2,1,0:T(4,128)S(1)}, u32[]{:S(2)}, u32[]{:S(2)}) collective-permute-start(f32[5,12,4,4]{3,2,1,0:T(4,128)S(1)} %get-tuple-element.43), channel_id=1, source_target_pairs={{64,0},{128,64},{192,128},{256,192},{320,256},{384,320},{448,384},... | collective-permute-start | bytes 11528 | tf_op jit(solution)/shard_map/ppermute | solution.py:35
  179.5 7.4 %collective-permute-start.17 = (f32[5,12,4,16]{3,2,1,0:T(4,128)S(1)}, f32[5,12,4,16]{3,2,1,0:T(4,128)S(1)}, u32[]{:S(2)}, u32[]{:S(2)}) collective-permute-start(f32[5,12,4,16]{3,2,1,0:T(4,128)S(1)} %pad_maximum_fusion.7), channel_id=1, source_target_pairs={{4,0},{8,4},{12,8},{16,12},{20,16},{24,20},{28,24},{32,28},{36,32}... | collective-permute-start | bytes 46088 | tf_op jit(solution)/shard_map/ppermute | solution.py:35
  182.5 4.4 %collective-permute-start.16 = (f32[5,12,4,16]{3,2,1,0:T(4,128)S(1)}, f32[5,12,4,16]{3,2,1,0:T(4,128)S(1)}, u32[]{:S(2)}, u32[]{:S(2)}) collective-permute-start(f32[5,12,4,16]{3,2,1,0:T(4,128)S(1)} %pad_maximum_fusion.7), channel_id=1, source_target_pairs={{0,4},{4,8},{8,12},{12,16},{16,20},{20,24},{24,28},{28,32},{32,36}... | collective-permute-start | bytes 46088 | tf_op jit(solution)/shard_map/ppermute | solution.py:33

commit v5 on v3

--- a/solution.py
+++ b/solution.py
@@ -181,11 +181,17 @@
 
 def pair_forces(separation, pair_mask, own_weights, other_weights):
     own_grad = jax.grad(lambda vector: jnp.sum(pair_energy(vector, own_weights)))(separation)
+    own_pieces = own_grad * pair_mask
+    own_force = jnp.sum(own_pieces, axis=1)
+    own_virial = jnp.einsum(
+        "aki,bki->ab", separation, own_pieces, precision=lax.Precision.HIGHEST
+    )
     other_grad = jax.grad(lambda vector: jnp.sum(pair_energy(vector, other_weights)))(-separation)
-    pieces = (own_grad - other_grad) * pair_mask
+    other_pieces = other_grad * pair_mask
     return (
-        jnp.sum(pieces, axis=1),
-        jnp.einsum("aki,bki->ab", separation, pieces, precision=lax.Precision.HIGHEST),
+        own_force - jnp.sum(other_pieces, axis=1),
+        own_virial
+        - jnp.einsum("aki,bki->ab", separation, other_pieces, precision=lax.Precision.HIGHEST),
     )
 
 

time: 191 us -> 192 us (level)
  no operation moved by 1% of the time
where the time goes in v5:
time: 192 us; the launch traced here: 191 us
  starting transfers between devices  57.5 us (30%)
  blocking collectives  43.4 us (23%)
  other arithmetic  38.1 us (20%)
  Pallas kernels  17.4 us (9%)
  waiting for transfers between devices  16.6 us (9%)
  local copies, waits for them, and re-layouts  10.4 us (5%)
  matrix products  5.88 us (3%)
  between operations  2.08 us (1%)
    psum x5, blocking collectives, by_axis(): return functools.reduce(lax.psum, axes, shard)  43.4 us
    ppermute x9, starting transfers between devices, padded(): lax.ppermute(tail, axis, [(i, (i + 1) % count) for i in range(links)])  28.9 us
    ppermute x9, starting transfers between devices, padded(): lax.ppermute(head, axis, [((i + 1) % count, i) for i in range(links)])  28.7 us
    pallas_call x1, Pallas kernels, row_gather(): pl.pallas_call(kernel, out_shape=jax.ShapeDtypeStruct((width, total), tab...  17.4 us
    ppermute x9, waiting for transfers between devices, padded(): lax.ppermute(tail, axis, [(i, (i + 1) % count) for i in range(links)])  8.75 us
    unnamed x29, other arithmetic  7.98 us
    ppermute x9, waiting for transfers between devices, padded(): lax.ppermute(head, axis, [((i + 1) % count, i) for i in range(links)])  7.86 us
    reduce_sum x1, other arithmetic, pair_energy(): mixed = jnp.sum(weights * basis[None], axis=1)  7.34 us
  transfers between devices with their start and end apart: 18, of which 6 were waited for; matrix products, arithmetic and copies ran while one was open for 9% of the time, Pallas kernels for 0%

profile of v5, /device:TPU:1, one launch (start us, length us, event | category | flops | bytes accessed | tf_op | source)
XLA Modules:
  0.0 191.3 jit_solution(19310764273850750)
XLA Ops:
  2.0 0.8 copy.132
  3.5 1.3 collective-permute-start.1
  4.8 7.3 %collective-permute-start = (f32[1,1,1,3,128]{3,4,2,1,0:T(8,128)S(1)}, f32[1,1,1,3,128]{3,4,2,1,0:T(8,128)S(1)}, u32[]{:S(2)}, u32[]{:S(2)}) collective-permute-start(f32[1,1,1,3,128]{3,4,2,1,0:T(8,128)S(1)} %bitcast_select_fusion.1), channel_id=1, source_target_pairs={{0,1},{1,2},{2,3},{4,5},{5,6},{6,7},{8,9},{9,10},{10,11},{12,13},{... | collective-permute-start | bytes 4616 | tf_op jit(solution)/shard_map/ppermute | solution.py:33
  13.5 0.8 fusion.272
  14.2 0.7 constant_dynamic-update-slice_fusion.40
  15.6 0.8 copy.156
  16.7 0.7 broadcast_multiply_fusion.2
  17.4 0.7 constant_dynamic-update-slice_fusion.39
  18.2 0.7 constant_dynamic-update-slice_fusion.38
  19.2 6.2 %collective-permute-start.3 = (f32[1,1,3,3,128]{4,1,3,2,0:T(1,128)S(1)}, f32[1,1,3,3,128]{4,1,3,2,0:T(1,128)S(1)}, u32[]{:S(2)}, u32[]{:S(2)}) collective-permute-start(f32[1,1,3,3,128]{4,1,3,2,0:T(1,128)S(1)} %pad_maximum_fusion.11), channel_id=1, source_target_pairs={{64,0},{128,64},{192,128},{256,192},{320,256},{384,320},{448,384},... | collective-permute-start | bytes 13832 | tf_op jit(solution)/shard_map/ppermute | solution.py:35
  25.4 1.9 %collective-permute-start.2 = (f32[1,1,3,3,128]{4,1,3,2,0:T(1,128)S(1)}, f32[1,1,3,3,128]{4,1,3,2,0:T(1,128)S(1)}, u32[]{:S(2)}, u32[]{:S(2)}) collective-permute-start(f32[1,1,3,3,128]{4,1,3,2,0:T(1,128)S(1)} %pad_maximum_fusion.11), channel_id=1, source_target_pairs={{0,64},{64,128},{128,192},{192,256},{256,320},{320,384},{384,448},... | collective-permute-start | bytes 13832 | tf_op jit(solution)/shard_map/ppermute | solution.py:33
  27.4 4.5 %collective-permute-done.2 = f32[1,1,3,3,128]{4,1,3,2,0:T(1,128)S(1)} collective-permute-done((f32[1,1,3,3,128]{4,1,3,2,0:T(1,128)S(1)}, f32[1,1,3,3,128]{4,1,3,2,0:T(1,128)S(1)}, u32[]{:S(2)}, u32[]{:S(2)}) %collective-permute-start.2) | collective-permute-done | bytes 4640 | tf_op jit(solution)/shard_map/ppermute | solution.py:33
  31.9 2.4 %collective-permute-start.5 = (f32[3,1,3,3,128]{4,1,3,2,0:T(1,128)S(1)}, f32[3,1,3,3,128]{4,1,3,2,0:T(1,128)S(1)}, u32[]{:S(2)}, u32[]{:S(2)}) collective-permute-start(f32[3,1,3,3,128]{4,1,3,2,0:T(1,128)S(1)} %pad_maximum_fusion.10), channel_id=1, source_target_pairs={{4,0},{8,4},{12,8},{16,12},{20,16},{24,20},{28,24},{32,28},{36,32}... | collective-permute-start | bytes 41480 | tf_op jit(solution)/shard_map/ppermute | solution.py:35
  34.3 1.2 collective-permute-start.4
  35.5 0.8 copy.131
  37.0 0.7 pad_maximum_fusion.8
  37.8 3.3 %fusion.3 = f32[3,12288]{1,0:T(4,128)S(1)} fusion(f32[3,31,128]{2,1,0:T(8,128)S(1)} %dot_general.20, s32[12288]{0:T(1024)S(1)} %get-tuple-element.53, pred[31,12288]{1,0:T(8,128)(4,1)S(1)} %iota_compare_fusion.1), kind=kOutput, calls=%fused_computation.17 | convolution fusion | flops 1759137792 | bytes 625152 | tf_op jit(solution)/shard_map/dot_general | solution.py:103
  41.2 0.7 constant_dynamic-update-slice_fusion.34
  42.7 2.2 %multiply_reduce_fusion.7 = f32[16,24,512]{2,1,0:T(8,128)S(1)} fusion(f32[8,24,512]{2,0,1:T(8,128)S(1)} %copy.140, f32[16,8]{1,0:T(8,128)S(1)} %copy.131), kind=kLoop, calls=%fused_computation.10 | loop fusion | flops 2949120 | bytes 1180160 | tf_op jit(solution)/shard_map/reduce_sum | solution.py:155
  45.1 2.7 %multiply_reduce_fusion = f32[16,16,512]{2,1,0:T(8,128)S(1)} fusion(f32[16,24,512]{2,1,0:T(8,128)S(1)} %constant_dynamic-update-slice_fusion.8, f32[16,24,512]{2,1,0:T(8,128)S(1)} %broadcast_multiply_fusion), kind=kLoop, calls=%fused_computation.3 | loop fusion | flops 6160384 | bytes 2097152 | tf_op jit(solution)/shard_map/reduce_sum | solution.py:156
  48.1 3.1 %multiply_reduce_fusion.1 = (f32[16,16,512]{2,1,0:T(8,128)S(1)}, f32[16,16,512]{2,1,0:T(8,128)S(1)}) fusion(f32[16,16,16]{2,1,0:T(8,128)S(1)} %copy.142, f32[16,16,512]{2,1,0:T(8,128)S(1)} %copy.141, f32[16,16,16]{2,1,0:T(8,128)S(1)} %get-tuple-element.43), kind=kLoop, calls=%fused_computation.4 | loop fusion | flops 8126464 | bytes 1605632 | tf_op jit(solution)/shard_map/reduce_sum | solution.py:171
  52.8 1.3 collective-permute-start.7
  54.1 6.7 %collective-permute-start.6 = (f32[1,1,1,128,128]{3,4,2,1,0:T(8,128)S(1)}, f32[1,1,1,128,128]{3,4,2,1,0:T(8,128)S(1)}, u32[]{:S(2)}, u32[]{:S(2)}) collective-permute-start(f32[1,1,1,128,128]{3,4,2,1,0:T(8,128)S(1)} %bitcast_select_fusion), channel_id=1, source_target_pairs={{0,1},{1,2},{2,3},{4,5},{5,6},{6,7},{8,9},{9,10},{10,11},{12,13},{... | collective-permute-start | bytes 196616 | tf_op jit(solution)/shard_map/ppermute | solution.py:33
  66.6 2.1 %collective-permute-start.9 = (f32[1,1,3,128,128]{3,4,2,1,0:T(8,128)S(1)}, f32[1,1,3,128,128]{3,4,2,1,0:T(8,128)S(1)}, u32[]{:S(2)}, u32[]{:S(2)}) collective-permute-start(f32[1,1,3,128,128]{3,4,2,1,0:T(8,128)S(1)} %pad_maximum_fusion.4), channel_id=1, source_target_pairs={{64,0},{128,64},{192,128},{256,192},{320,256},{384,320},{448,384},... | collective-permute-start | bytes 589832 | tf_op jit(solution)/shard_map/ppermute | solution.py:35
  68.7 3.4 %collective-permute-start.8 = (f32[1,1,3,128,128]{3,4,2,1,0:T(8,128)S(1)}, f32[1,1,3,128,128]{3,4,2,1,0:T(8,128)S(1)}, u32[]{:S(2)}, u32[]{:S(2)}) collective-permute-start(f32[1,1,3,128,128]{3,4,2,1,0:T(8,128)S(1)} %pad_maximum_fusion.4), channel_id=1, source_target_pairs={{0,64},{64,128},{128,192},{192,256},{256,320},{320,384},{384,448},... | collective-permute-start | bytes 589832 | tf_op jit(solution)/shard_map/ppermute | solution.py:33
  73.0 4.2 %collective-permute-done.8 = f32[1,1,3,128,128]{3,4,2,1,0:T(8,128)S(1)} collective-permute-done((f32[1,1,3,128,128]{3,4,2,1,0:T(8,128)S(1)}, f32[1,1,3,128,128]{3,4,2,1,0:T(8,128)S(1)}, u32[]{:S(2)}, u32[]{:S(2)}) %collective-permute-start.8) | collective-permute-done | bytes 196640 | tf_op jit(solution)/shard_map/ppermute | solution.py:33
  77.3 4.4 %collective-permute-start.11 = (f32[3,1,3,128,128]{3,4,2,1,0:T(8,128)S(1)}, f32[3,1,3,128,128]{3,4,2,1,0:T(8,128)S(1)}, u32[]{:S(2)}, u32[]{:S(2)}) collective-permute-start(f32[3,1,3,128,128]{3,4,2,1,0:T(8,128)S(1)} %pad_maximum_fusion.2), channel_id=1, source_target_pairs={{4,0},{8,4},{12,8},{16,12},{20,16},{24,20},{28,24},{32,28},{36,32}... | collective-permute-start | bytes 1769480 | tf_op jit(solution)/shard_map/ppermute | solution.py:35
  83.7 5.6 %collective-permute-done.11 = f32[3,1,3,128,128]{3,4,2,1,0:T(8,128)S(1)} collective-permute-done((f32[3,1,3,128,128]{3,4,2,1,0:T(8,128)S(1)}, f32[3,1,3,128,128]{3,4,2,1,0:T(8,128)S(1)}, u32[]{:S(2)}, u32[]{:S(2)}) %collective-permute-start.11) | collective-permute-done | bytes 589856 | tf_op jit(solution)/shard_map/ppermute | solution.py:35
  89.5 1.5 pad_maximum_fusion.table_ref
  90.9 17.4 %shard_map.156 = f32[128,12288]{1,0:T(8,128)} custom-call(s32[12288]{0:T(1024)} %bitcast.274, f32[3968,128]{1,0:T(8,128)} %pad_maximum_fusion.table_ref), custom_call_target="tpu_custom_call" | custom-call | bytes 14614528 | tf_op jit(solution)/shard_map/pallas_call | solution.py:78
  108.4 7.3 %multiply_reduce_fusion.3 = (f32[8,24,512]{2,0,1:T(8,128)S(1)}, f32[16,24,512]{2,1,0:T(8,128)S(1)}, f32[16,24,512]{2,1,0:T(8,128)S(1)}, f32[8,24,512]{2,0,1:T(8,128)S(1)}) fusion(f32[16,8,24,512]{3,1,2,0:T(8,128)} %bitcast.267, f32[16,24,512]{2,1,0:T(8,128)S(1)} %copy-done, f32[8,24,512]{2,0,1:T(8,128)S(1)} %copy.140, f32[16,8,512]{2,1,0:T(8,128)S(1)} %copy.178, ...), kind=kLoop, calls=%fused_computation.6 | loop fusion | flops 11993088 | bytes 10878976 | tf_op jit(solution)/shard_map/transpose(jvp())/reduce_sum | solution.py:149
  117.3 1.0 convolution_bitcast_fusion
  118.3 1.0 fusion.6
  119.4 0.7 pad_maximum_fusion.12
  120.2 3.8 %psum.35 = f32[11]{0:T(128)S(1)} all-reduce(f32[11]{0:T(128)S(1)} %pad_maximum_fusion.12), channel_id=1, replica_groups=mesh['gx_0'=2,'gx_1'=4,'gy_0'=8,'gy_1'=2,'gz'=4] {'gx_0'}, use_global_device_ids=true, to_apply=%region_18.19 | all-reduce | flops 11 | bytes 88 | tf_op jit(solution)/shard_map/psum | solution.py:43
  125.6 4.2 %collective-permute-start.13 = (f32[5,4,4,8]{3,2,1,0:T(4,128)S(1)}, f32[5,4,4,8]{3,2,1,0:T(4,128)S(1)}, u32[]{:S(2)}, u32[]{:S(2)}) collective-permute-start(f32[5,4,4,8]{3,2,1,0:T(4,128)S(1)} %constant_dynamic-update-slice_fusion.36), channel_id=1, source_target_pairs={{1,0},{2,1},{3,2},{0,3},{5,4},{6,5},{7,6},{4,7},{9,8},{10,9},{11,1... | collective-permute-start | bytes 7688 | tf_op jit(solution)/shard_map/ppermute | solution.py:35
  129.9 3.2 %collective-permute-start.12 = (f32[5,4,4,8]{3,2,1,0:T(4,128)S(1)}, f32[5,4,4,8]{3,2,1,0:T(4,128)S(1)}, u32[]{:S(2)}, u32[]{:S(2)}) collective-permute-start(f32[5,4,4,8]{3,2,1,0:T(4,128)S(1)} %constant_dynamic-update-slice_fusion.36), channel_id=1, source_target_pairs={{0,1},{1,2},{2,3},{3,0},{4,5},{5,6},{6,7},{7,4},{8,9},{9,10},{10,1... | collective-permute-start | bytes 7688 | tf_op jit(solution)/shard_map/ppermute | solution.py:33
  133.0 6.0 %psum.36 = f32[11]{0:T(128)S(1)} all-reduce(f32[11]{0:T(128)S(1)} %psum.35), channel_id=1, replica_groups=mesh['gx_0'=2,'gx_1'=4,'gy_0'=8,'gy_1'=2,'gz'=4] {'gx_1'}, use_global_device_ids=true, to_apply=%region_19.20 | all-reduce | flops 11 | bytes 88 | tf_op jit(solution)/shard_map/psum | solution.py:43
  139.0 13.9 %psum.37 = f32[11]{0:T(128)S(1)} all-reduce(f32[11]{0:T(128)S(1)} %psum.36), channel_id=1, replica_groups=mesh['gx_0'=2,'gx_1'=4,'gy_0'=8,'gy_1'=2,'gz'=4] {'gy_0'}, use_global_device_ids=true, to_apply=%region_20.21 | all-reduce | flops 11 | bytes 88 | tf_op jit(solution)/shard_map/psum | solution.py:43
  153.0 8.9 %psum.38 = f32[11]{0:T(128)S(1)} all-reduce(f32[11]{0:T(128)S(1)} %psum.37), channel_id=1, replica_groups=mesh['gx_0'=2,'gx_1'=4,'gy_0'=8,'gy_1'=2,'gz'=4] {'gy_1'}, use_global_device_ids=true, to_apply=%region_21.22 | all-reduce | flops 11 | bytes 88 | tf_op jit(solution)/shard_map/psum | solution.py:43
  162.1 3.6 %collective-permute-start.14 = (f32[5,12,4,4]{3,2,1,0:T(4,128)S(1)}, f32[5,12,4,4]{3,2,1,0:T(4,128)S(1)}, u32[]{:S(2)}, u32[]{:S(2)}) collective-permute-start(f32[5,12,4,4]{3,2,1,0:T(4,128)S(1)} %get-tuple-element.48), channel_id=1, source_target_pairs={{0,64},{64,128},{128,192},{192,256},{256,320},{320,384},{384,448},... | collective-permute-start | bytes 11528 | tf_op jit(solution)/shard_map/ppermute | solution.py:33
  165.7 3.8 %collective-permute-start.15 = (f32[5,12,4,4]{3,2,1,0:T(4,128)S(1)}, f32[5,12,4,4]{3,2,1,0:T(4,128)S(1)}, u32[]{:S(2)}, u32[]{:S(2)}) collective-permute-start(f32[5,12,4,4]{3,2,1,0:T(4,128)S(1)} %get-tuple-element.49), channel_id=1, source_target_pairs={{64,0},{128,64},{192,128},{256,192},{320,256},{384,320},{448,384},... | collective-permute-start | bytes 11528 | tf_op jit(solution)/shard_map/ppermute | solution.py:35
  169.5 10.8 %psum.39 = f32[11]{0:T(128)S(1)} all-reduce(f32[11]{0:T(128)S(1)} %psum.38), channel_id=1, replica_groups=mesh['gx_0'=2,'gx_1'=4,'gy_0'=8,'gy_1'=2,'gz'=4] {'gz'}, use_global_device_ids=true, to_apply=%region_22.23 | all-reduce | flops 11 | bytes 88 | tf_op jit(solution)/shard_map/psum | solution.py:43
  181.0 3.0 %collective-permute-start.17 = (f32[5,12,4,16]{3,2,1,0:T(4,128)S(1)}, f32[5,12,4,16]{3,2,1,0:T(4,128)S(1)}, u32[]{:S(2)}, u32[]{:S(2)}) collective-permute-start(f32[5,12,4,16]{3,2,1,0:T(4,128)S(1)} %pad_maximum_fusion.7), channel_id=1, source_target_pairs={{4,0},{8,4},{12,8},{16,12},{20,16},{24,20},{28,24},{32,28},{36,32}... | collective-permute-start | bytes 46088 | tf_op jit(solution)/shard_map/ppermute | solution.py:35
  184.0 1.6 collective-permute-start.16
  185.6 1.2 slice_divide_fusion
  186.8 1.6 collective-permute-done.17
  189.7 0.7 add_divide_fusion
  (151 shorter events, 22.8 us)
Async XLA Ops:
  3.5 15.5 %collective-permute-start.1 = (f32[1,1,1,3,128]{3,4,2,1,0:T(8,128)S(1)}, f32[1,1,1,3,128]{3,4,2,1,0:T(8,128)S(1)}, u32[]{:S(2)}, u32[]{:S(2)}) collective-permute-start(f32[1,1,1,3,128]{3,4,2,1,0:T(8,128)S(1)} %bitcast_select_fusion.1), channel_id=1, source_target_pairs={{1,0},{2,1},{3,2},{5,4},{6,5},{7,6},{9,8},{10,9},{11,10},{13,12},{... | collective-permute-start | bytes 4616 | tf_op jit(solution)/shard_map/ppermute | solution.py:35
  4.8 14.3 %collective-permute-start = (f32[1,1,1,3,128]{3,4,2,1,0:T(8,128)S(1)}, f32[1,1,1,3,128]{3,4,2,1,0:T(8,128)S(1)}, u32[]{:S(2)}, u32[]{:S(2)}) collective-permute-start(f32[1,1,1,3,128]{3,4,2,1,0:T(8,128)S(1)} %bitcast_select_fusion.1), channel_id=1, source_target_pairs={{0,1},{1,2},{2,3},{4,5},{5,6},{6,7},{8,9},{9,10},{10,11},{12,13},{... | collective-permute-start | bytes 4616 | tf_op jit(solution)/shard_map/ppermute | solution.py:33
  12.1 29.0 %copy-start.2 = (f32[3,512]{1,0:T(4,128)S(1)}, f32[3,512]{1,0:T(4,128)}, u32[]{:S(2)}) copy-start(f32[3,512]{1,0:T(4,128)} %param.13) | copy-start | bytes 18436
  16.4 24.8 %copy-start.1 = (s32[3,4,8,128]{3,1,2,0:T(4,128)}, s32[3,4,8,128]{3,1,2,0:T(4,128)S(1)}, u32[]{:S(2)}) copy-start(s32[3,4,8,128]{3,1,2,0:T(4,128)S(1)} %copy.156) | copy-start | bytes 147460
  19.2 8.1 %collective-permute-start.3 = (f32[1,1,3,3,128]{4,1,3,2,0:T(1,128)S(1)}, f32[1,1,3,3,128]{4,1,3,2,0:T(1,128)S(1)}, u32[]{:S(2)}, u32[]{:S(2)}) collective-permute-start(f32[1,1,3,3,128]{4,1,3,2,0:T(1,128)S(1)} %pad_maximum_fusion.11), channel_id=1, source_target_pairs={{64,0},{128,64},{192,128},{256,192},{320,256},{384,320},{448,384},... | collective-permute-start | bytes 13832 | tf_op jit(solution)/shard_map/ppermute | solution.py:35
  25.4 6.5 %collective-permute-start.2 = (f32[1,1,3,3,128]{4,1,3,2,0:T(1,128)S(1)}, f32[1,1,3,3,128]{4,1,3,2,0:T(1,128)S(1)}, u32[]{:S(2)}, u32[]{:S(2)}) collective-permute-start(f32[1,1,3,3,128]{4,1,3,2,0:T(1,128)S(1)} %pad_maximum_fusion.11), channel_id=1, source_target_pairs={{0,64},{64,128},{128,192},{192,256},{256,320},{320,384},{384,448},... | collective-permute-start | bytes 13832 | tf_op jit(solution)/shard_map/ppermute | solution.py:33
  31.9 5.0 %collective-permute-start.5 = (f32[3,1,3,3,128]{4,1,3,2,0:T(1,128)S(1)}, f32[3,1,3,3,128]{4,1,3,2,0:T(1,128)S(1)}, u32[]{:S(2)}, u32[]{:S(2)}) collective-permute-start(f32[3,1,3,3,128]{4,1,3,2,0:T(1,128)S(1)} %pad_maximum_fusion.10), channel_id=1, source_target_pairs={{4,0},{8,4},{12,8},{16,12},{20,16},{24,20},{28,24},{32,28},{36,32}... | collective-permute-start | bytes 41480 | tf_op jit(solution)/shard_map/ppermute | solution.py:35
  34.3 2.6 %collective-permute-start.4 = (f32[3,1,3,3,128]{4,1,3,2,0:T(1,128)S(1)}, f32[3,1,3,3,128]{4,1,3,2,0:T(1,128)S(1)}, u32[]{:S(2)}, u32[]{:S(2)}) collective-permute-start(f32[3,1,3,3,128]{4,1,3,2,0:T(1,128)S(1)} %pad_maximum_fusion.10), channel_id=1, source_target_pairs={{0,4},{4,8},{8,12},{12,16},{16,20},{20,24},{24,28},{28,32},{32,36}... | collective-permute-start | bytes 41480 | tf_op jit(solution)/shard_map/ppermute | solution.py:33
  45.0 6.3 %copy-start.5 = (f32[16,8]{0,1:T(8,128)S(1)}, f32[16,8]{0,1:T(8,128)}, u32[]{:S(2)}) copy-start(f32[16,8]{0,1:T(8,128)} %param.20) | copy-start | bytes 1540
  51.1 30.6 %copy-start.6 = (f32[16]{0:T(128)S(1)}, f32[16]{0:T(128)}, u32[]{:S(2)}) copy-start(f32[16]{0:T(128)} %param.21) | copy-start | bytes 196
  52.8 13.7 %collective-permute-start.7 = (f32[1,1,1,128,128]{3,4,2,1,0:T(8,128)S(1)}, f32[1,1,1,128,128]{3,4,2,1,0:T(8,128)S(1)}, u32[]{:S(2)}, u32[]{:S(2)}) collective-permute-start(f32[1,1,1,128,128]{3,4,2,1,0:T(8,128)S(1)} %bitcast_select_fusion), channel_id=1, source_target_pairs={{1,0},{2,1},{3,2},{5,4},{6,5},{7,6},{9,8},{10,9},{11,10},{13,12},{... | collective-permute-start | bytes 196616 | tf_op jit(solution)/shard_map/ppermute | solution.py:35
  54.1 12.4 %collective-permute-start.6 = (f32[1,1,1,128,128]{3,4,2,1,0:T(8,128)S(1)}, f32[1,1,1,128,128]{3,4,2,1,0:T(8,128)S(1)}, u32[]{:S(2)}, u32[]{:S(2)}) collective-permute-start(f32[1,1,1,128,128]{3,4,2,1,0:T(8,128)S(1)} %bitcast_select_fusion), channel_id=1, source_target_pairs={{0,1},{1,2},{2,3},{4,5},{5,6},{6,7},{8,9},{9,10},{10,11},{12,13},{... | collective-permute-start | bytes 196616 | tf_op jit(solution)/shard_map/ppermute | solution.py:33
  66.6 6.4 %collective-permute-start.9 = (f32[1,1,3,128,128]{3,4,2,1,0:T(8,128)S(1)}, f32[1,1,3,128,128]{3,4,2,1,0:T(8,128)S(1)}, u32[]{:S(2)}, u32[]{:S(2)}) collective-permute-start(f32[1,1,3,128,128]{3,4,2,1,0:T(8,128)S(1)} %pad_maximum_fusion.4), channel_id=1, source_target_pairs={{64,0},{128,64},{192,128},{256,192},{320,256},{384,320},{448,384},... | collective-permute-start | bytes 589832 | tf_op jit(solution)/shard_map/ppermute | solution.py:35
  68.7 8.5 %collective-permute-start.8 = (f32[1,1,3,128,128]{3,4,2,1,0:T(8,128)S(1)}, f32[1,1,3,128,128]{3,4,2,1,0:T(8,128)S(1)}, u32[]{:S(2)}, u32[]{:S(2)}) collective-permute-start(f32[1,1,3,128,128]{3,4,2,1,0:T(8,128)S(1)} %pad_maximum_fusion.4), channel_id=1, source_target_pairs={{0,64},{64,128},{128,192},{192,256},{256,320},{320,384},{384,448},... | collective-permute-start | bytes 589832 | tf_op jit(solution)/shard_map/ppermute | solution.py:33
  77.3 12.0 %collective-permute-start.11 = (f32[3,1,3,128,128]{3,4,2,1,0:T(8,128)S(1)}, f32[3,1,3,128,128]{3,4,2,1,0:T(8,128)S(1)}, u32[]{:S(2)}, u32[]{:S(2)}) collective-permute-start(f32[3,1,3,128,128]{3,4,2,1,0:T(8,128)S(1)} %pad_maximum_fusion.2), channel_id=1, source_target_pairs={{4,0},{8,4},{12,8},{16,12},{20,16},{24,20},{28,24},{32,28},{36,32}... | collective-permute-start | bytes 1769480 | tf_op jit(solution)/shard_map/ppermute | solution.py:35
  81.7 7.6 %collective-permute-start.10 = (f32[3,1,3,128,128]{3,4,2,1,0:T(8,128)S(1)}, f32[3,1,3,128,128]{3,4,2,1,0:T(8,128)S(1)}, u32[]{:S(2)}, u32[]{:S(2)}) collective-permute-start(f32[3,1,3,128,128]{3,4,2,1,0:T(8,128)S(1)} %pad_maximum_fusion.2), channel_id=1, source_target_pairs={{0,4},{4,8},{8,12},{12,16},{16,20},{20,24},{24,28},{28,32},{32,36}... | collective-permute-start | bytes 1769480 | tf_op jit(solution)/shard_map/ppermute | solution.py:33
  90.9 17.4 %copy-start = (f32[16,24,512]{2,1,0:T(8,128)S(1)}, f32[16,24,512]{2,1,0:T(8,128)}, u32[]{:S(2)}) copy-start(f32[16,24,512]{2,1,0:T(8,128)} %constant_dynamic-update-slice_fusion.22) | copy-start | bytes 2359300
  115.8 8.1 %copy-start.3 = (f32[3,512]{1,0:T(4,128)S(1)}, f32[3,512]{1,0:T(4,128)}, u32[]{:S(2)}) copy-start(f32[3,512]{1,0:T(4,128)} %param.14) | copy-start | bytes 18436
  115.8 8.1 %copy-start.7 = (s32[512]{0:T(512)S(1)}, s32[512]{0:T(512)}, u32[]{:S(2)}) copy-start(s32[512]{0:T(512)} %param.19) | copy-start | bytes 6148
  124.0 67.4 %copy-start.4 = (f32[3,512]{1,0:T(4,128)}, f32[3,512]{1,0:T(4,128)S(1)}, u32[]{:S(2)}) copy-start(f32[3,512]{1,0:T(4,128)S(1)} %get-tuple-element.23) | copy-start | bytes 18436
  125.6 36.3 %collective-permute-start.13 = (f32[5,4,4,8]{3,2,1,0:T(4,128)S(1)}, f32[5,4,4,8]{3,2,1,0:T(4,128)S(1)}, u32[]{:S(2)}, u32[]{:S(2)}) collective-permute-start(f32[5,4,4,8]{3,2,1,0:T(4,128)S(1)} %constant_dynamic-update-slice_fusion.36), channel_id=1, source_target_pairs={{1,0},{2,1},{3,2},{0,3},{5,4},{6,5},{7,6},{4,7},{9,8},{10,9},{11,1... | collective-permute-start | bytes 7688 | tf_op jit(solution)/shard_map/ppermute | solution.py:35
  129.9 32.0 %collective-permute-start.12 = (f32[5,4,4,8]{3,2,1,0:T(4,128)S(1)}, f32[5,4,4,8]{3,2,1,0:T(4,128)S(1)}, u32[]{:S(2)}, u32[]{:S(2)}) collective-permute-start(f32[5,4,4,8]{3,2,1,0:T(4,128)S(1)} %constant_dynamic-update-slice_fusion.36), channel_id=1, source_target_pairs={{0,1},{1,2},{2,3},{3,0},{4,5},{5,6},{6,7},{7,4},{8,9},{9,10},{10,1... | collective-permute-start | bytes 7688 | tf_op jit(solution)/shard_map/ppermute | solution.py:33
  162.1 18.8 %collective-permute-start.14 = (f32[5,12,4,4]{3,2,1,0:T(4,128)S(1)}, f32[5,12,4,4]{3,2,1,0:T(4,128)S(1)}, u32[]{:S(2)}, u32[]{:S(2)}) collective-permute-start(f32[5,12,4,4]{3,2,1,0:T(4,128)S(1)} %get-tuple-element.48), channel_id=1, source_target_pairs={{0,64},{64,128},{128,192},{192,256},{256,320},{320,384},{384,448},... | collective-permute-start | bytes 11528 | tf_op jit(solution)/shard_map/ppermute | solution.py:33
  165.7 15.1 %collective-permute-start.15 = (f32[5,12,4,4]{3,2,1,0:T(4,128)S(1)}, f32[5,12,4,4]{3,2,1,0:T(4,128)S(1)}, u32[]{:S(2)}, u32[]{:S(2)}) collective-permute-start(f32[5,12,4,4]{3,2,1,0:T(4,128)S(1)} %get-tuple-element.49), channel_id=1, source_target_pairs={{64,0},{128,64},{192,128},{256,192},{320,256},{384,320},{448,384},... | collective-permute-start | bytes 11528 | tf_op jit(solution)/shard_map/ppermute | solution.py:35
  181.0 7.4 %collective-permute-start.17 = (f32[5,12,4,16]{3,2,1,0:T(4,128)S(1)}, f32[5,12,4,16]{3,2,1,0:T(4,128)S(1)}, u32[]{:S(2)}, u32[]{:S(2)}) collective-permute-start(f32[5,12,4,16]{3,2,1,0:T(4,128)S(1)} %pad_maximum_fusion.7), channel_id=1, source_target_pairs={{4,0},{8,4},{12,8},{16,12},{20,16},{24,20},{28,24},{32,28},{36,32}... | collective-permute-start | bytes 46088 | tf_op jit(solution)/shard_map/ppermute | solution.py:35
  184.0 4.4 %collective-permute-start.16 = (f32[5,12,4,16]{3,2,1,0:T(4,128)S(1)}, f32[5,12,4,16]{3,2,1,0:T(4,128)S(1)}, u32[]{:S(2)}, u32[]{:S(2)}) collective-permute-start(f32[5,12,4,16]{3,2,1,0:T(4,128)S(1)} %pad_maximum_fusion.7), channel_id=1, source_target_pairs={{0,4},{4,8},{8,12},{12,16},{16,20},{20,24},{24,28},{28,32},{32,36}... | collective-permute-start | bytes 46088 | tf_op jit(solution)/shard_map/ppermute | solution.py:33
